TPU v7x, 512 devices: a whole 4x4x16 slice. The times are simulated.
512 devices in a mesh: gx: 32 (over y, x, core), gy: 16 (over z).
Axes of the slice: x: 4, y: 4, z: 16, core: 2. Of those that a mesh axis runs over, the one named last changes fastest.
Arguments:
- diffusivity: float32 [1024, 2048], P('gx', 'gy'), may hold values from 0.25 to 1
- base_humidity: float32 [1024, 2048], P('gx', 'gy'), may hold values from -4 to 4
- coupling: float32 [1024, 2048], P('gx', 'gy'), may hold values from 0.1 to 0.4
- basis_rows: float32 [1024, 64], P('gx'), may hold values from -0.45 to 0.45
- basis_cols: float32 [2048, 32], P('gy'), may hold values from -0.45 to 0.45
- directions: float32 [16, 64, 32], replicated, may hold values from -5 to 5
- send_cell: int32 [32, 16, 32, 8], P('gx', 'gy'), may hold values from 0 to 4095
- send_weight: float32 [32, 16, 32, 8], P('gx', 'gy'), may hold values from 0.1 to 1
- send_count: int32 [32, 16, 32], P('gx', 'gy'), may hold values from 1 to 8, as said below
- owner_gauge: int32 [32, 16, 32, 8], P('gx', 'gy'), may hold values from 0 to 39
- noise_precision: float32 [32, 16, 40], P('gx', 'gy'), may hold values from 1 to 16
Outputs:
- readings: float32 [32, 16, 16, 40], P('gx', 'gy')
- hess_action: float32 [16, 64, 32], replicated
Inputs may be any that keep to these rules, and one draw needn't show every extreme that they name: `send_count`: entries from one device to one owner; in every draw, in each row of the gy axis one owner receives exactly 8 from every device. `send_cell`: A local cell index of the sending device. `owner_gauge`: A gauge of the owner.
All inputs are finite; a program needn't handle non-finite values.
Results may differ from a plain program's by a relative error of at most 0.00011.
Values sent between devices are 32-bit elements; how exact they have to be, the bound alone decides.
No kernel may reach another device: no remote copies, remote signals or barrier semaphores. Data moves between devices by JAX's collectives and lax.ppermute only.
A program may use at most 64 MiB of HBM per device.

v0:
```python
import jax
import jax.numpy as jnp
from jax import lax
from jax.sharding import PartitionSpec as P

STEPS = 6


step_ratio = 0.2
exact = lax.Precision.HIGHEST


def extended(cells, sides, width):
    for axis, dim in sides:
        count = lax.axis_size(axis)
        ends = count - 1
        head = lax.slice_in_dim(cells, 0, width, axis=dim)
        tail = lax.slice_in_dim(cells, cells.shape[dim] - width, cells.shape[dim], axis=dim)
        cells = jnp.concatenate(
            [
                lax.ppermute(tail, axis, [(i, (i + 1) % count) for i in range(ends)]),
                cells,
                lax.ppermute(head, axis, [((i + 1) % count, i) for i in range(ends)]),
            ],
            axis=dim,
        )
    return cells


def spread(field):
    middle = field[..., 1:-1, 1:-1]
    return (
        middle,
        (field[..., :-2, 1:-1], field[..., 2:, 1:-1], field[..., 1:-1, :-2], field[..., 1:-1, 2:]),
    )


def window(field, have, want):
    offset = have - want
    return field[..., offset : field.shape[-2] - offset, offset : field.shape[-1] - offset]


def advance(state_now, static_pad, orient):
    temp_mid, temp_near = spread(state_now[0])
    hum_mid, hum_near = spread(state_now[1])
    diff_mid, diff_near = spread(static_pad[0])
    couple_mid = static_pad[2, 1:-1, 1:-1]
    inside = static_pad[3, 1:-1, 1:-1]
    lap_temp = sum((n - temp_mid for n in temp_near))
    lap_hum = sum((0.5 * (diff_mid + k) * (n - hum_mid) for k, n in zip(diff_near, hum_near)))
    new_temp = temp_mid + step_ratio * lap_temp + orient * couple_mid * hum_mid
    new_hum = hum_mid + step_ratio * lap_hum - orient * couple_mid * temp_mid
    return jnp.stack([new_temp * inside, new_hum * inside])


def make_source(param_pad, static_pad):
    param_mid, param_near = spread(param_pad)
    hum_mid, hum_near = spread(static_pad[1])
    inside = static_pad[3, 1:-1, 1:-1]
    return (
        sum((0.5 * (param_mid + p) * (h - hum_mid) for p, h in zip(param_near, hum_near))) * inside
    )


def state_rim(state_now):
    return extended(state_now, (("gx", 2), ("gy", 3)), 1)


def local(
    diffusivity,
    base_humidity,
    coupling,
    basis_rows,
    basis_cols,
    directions,
    send_cell,
    send_weight,
    send_count,
    owner_gauge,
    noise_precision,
):
    rim_depth = STEPS
    height, breadth = diffusivity.shape
    n_dirs = directions.shape[0]
    static = jnp.stack([diffusivity, base_humidity, coupling, jnp.ones_like(diffusivity)])
    static_wide = extended(static, (("gx", 1), ("gy", 2)), rim_depth)
    static_near = window(static_wide, rim_depth, 1)
    perturb = jnp.einsum("xa,rab->rxb", basis_rows, directions, precision=exact)
    perturb = jnp.einsum("rxb,yb->rxy", perturb, basis_cols, precision=exact)
    param_field = diffusivity * perturb
    param_wide = extended(param_field, (("gx", 1), ("gy", 2)), 1)
    source = make_source(param_wide, static_near)
    state_now = jnp.stack([jnp.zeros_like(source), step_ratio * source])
    for i in range(rim_depth - 1):
        state_now = advance(state_rim(state_now), static_near, 1.0)
        state_now = jnp.stack([state_now[0], state_now[1] + step_ratio * source])
    humid = state_now[1]
    peers = send_cell.shape[2]
    slots = send_cell.shape[3]
    gauges = noise_precision.shape[2]
    cell_ids = send_cell.reshape(-1)
    live_mask = (
        lax.broadcasted_iota(jnp.int32, (peers, slots), 1) < send_count.reshape(peers, 1)
    ).astype(jnp.float32)
    factor = send_weight.reshape(peers, slots) * live_mask
    picked = (
        jnp.take(humid.reshape(n_dirs, height * breadth), cell_ids, axis=1).reshape(
            n_dirs, peers, slots
        )
        * factor
    )
    gauge_ids = owner_gauge.reshape(-1)
    lookup = (gauge_ids[:, None] == lax.broadcasted_iota(jnp.int32, (1, gauges), 1)).astype(
        jnp.float32
    )
    gauge_weights = noise_precision.reshape(1, gauges)
    arrived = lax.all_to_all(picked, "gx", split_axis=1, concat_axis=1, tiled=True)
    n_items = arrived.shape[0]
    gauge_read = jnp.dot(arrived.reshape(n_items, peers * slots), lookup, precision=exact)
    backward = jnp.dot(gauge_read * gauge_weights, lookup.T, precision=exact).reshape(
        n_items, peers, slots
    )
    returned = lax.all_to_all(backward, "gx", split_axis=1, concat_axis=1, tiled=True)
    gauge_read, returned = (gauge_read, returned)
    load_values = (returned * factor).reshape(n_dirs, peers * slots)
    adjoint_load = (
        jnp.zeros((n_dirs, height * breadth), jnp.float32).at[:, cell_ids].add(load_values)
    )
    adjoint_load = adjoint_load.reshape(n_dirs, height, breadth)
    state_now = jnp.stack([jnp.zeros_like(adjoint_load), adjoint_load])
    summed = adjoint_load
    for i in range(rim_depth - 1):
        state_now = advance(state_rim(state_now), static_near, -1.0)
        summed = summed + state_now[1]
    lam_wide = extended(step_ratio * summed, (("gx", 1), ("gy", 2)), 1)
    lam_mid, lam_near = spread(lam_wide)
    hum_mid, hum_near = spread(static_near[1])
    gradient = diffusivity * sum(
        (0.5 * (h - hum_mid) * (lam_mid - l) for h, l in zip(hum_near, lam_near))
    )
    projected = jnp.einsum("rxy,yb->rxb", gradient, basis_cols, precision=exact)
    projected = jnp.einsum("xa,rxb->rab", basis_rows, projected, precision=exact).reshape(
        n_dirs, -1
    )
    summed_modes = lax.psum(projected, ("gx", "gy"))
    hess_action = directions + summed_modes.reshape(directions.shape)
    return (gauge_read.reshape(1, 1, n_dirs, gauges), hess_action)


def solution(mesh):
    placed = (
        P("gx", "gy"),
        P("gx", "gy"),
        P("gx", "gy"),
        P("gx", None),
        P("gy", None),
        P(),
        P("gx", "gy", None, None),
        P("gx", "gy", None, None),
        P("gx", "gy", None),
        P("gx", "gy", None, None),
        P("gx", "gy", None),
    )
    return jax.shard_map(
        local,
        mesh=mesh,
        in_specs=placed,
        out_specs=(P("gx", "gy", None, None), P()),
        check_vma=False,
    )
```

profile of v0, /device:TPU:1, one launch (start us, length us, event | category | flops | bytes accessed | tf_op | source)
XLA Modules:
  0.0 823.3 jit_solution(16059278599221910814)
XLA Ops:
  9.9 4.5 collective-permute-start
  14.4 5.5 collective-permute-start.5
  31.0 4.2 collective-permute-start.6
  36.9 4.6 collective-permute-done.6
  41.5 4.1 collective-permute-done.7
  46.0 4.5 collective-permute-start.8
  57.8 5.0 collective-permute-start.10
  70.7 3.1 collective-permute-done.13
  74.5 5.1 collective-permute-start.14
  81.6 4.1 collective-permute-done.15
  92.8 3.1 collective-permute-done.17
  96.6 4.8 collective-permute-start.18
  103.4 4.7 collective-permute-done.19
  120.6 5.7 collective-permute-start.22
  134.3 3.8 collective-permute-done.25
  140.3 4.3 collective-permute-start.26
  149.9 17.4 %all-to-all-start = ((f32[32,1,128]{2,1,0:T(1,128)}), f32[32,1,128]{2,1,0:T(1,128)S(1)}, u32[]{:S(2)}, u32[]{:S(2)}) async-start(f32[32,1,128]{2,1,0:T(1,128)} %reshape.148), calls=%async_computation | async-start | bytes 32768 | tf_op jit(solution)/shard_map/all_to_all | solution.py:117
  167.6 6.7 all-to-all-done
  176.9 10.7 %all_to_all.10 = f32[32,1,128]{2,1,0:T(1,128)S(1)} all-to-all(f32[32,1,128]{2,1,0:T(1,128)S(1)} %reshape.150), channel_id=1, replica_groups=mesh['gx'=32,'gy'=16] {'gx'}, dimensions={0} | all-to-all | bytes 32768 | tf_op jit(solution)/shard_map/all_to_all | solution.py:123
  203.0 4.3 collective-permute-start.30
  222.7 4.1 collective-permute-start.34
  228.8 4.5 collective-permute-done.35
  248.9 5.4 collective-permute-start.38
  257.6 3.6 collective-permute-done.39
  277.3 4.8 collective-permute-start.42
  297.3 3.1 collective-permute-done.45
  303.1 4.2 collective-permute-start.46
  317.4 4.5 collective-permute-start.48
  327.2 4.7 collective-permute-start.50
  333.4 3.7 collective-permute-done.50
  337.1 4.3 collective-permute-done.51
  343.9 470.9 %all-reduce.4.cloned.1.call-done = f32[16,64,32]{1,2,0:T(8,128)} async-done(((f32[16,64,32]{1,2,0:T(8,128)}), f32[16,64,32]{1,2,0:T(8,128)}) %all-reduce.4.cloned.1.call-update) | async-done | bytes 131088 | tf_op jit(solution)/shard_map/psum | solution.py:145
  (294 shorter events, 179.5 us)
Async XLA Ops:
  9.9 15.2 %collective-permute-start = (f32[16,1,128]{2,1,0:T(1,128)S(1)}, f32[16,1,128]{2,1,0:T(1,128)S(1)}, u32[]{:S(2)}, u32[]{:S(2)}) collective-permute-start(f32[16,1,128]{2,1,0:T(1,128)S(1)} %get-tuple-element.84), channel_id=1, source_target_pairs={{0,16},{16,32},{32,48},{48,64},{64,80},{80,96},{96,112},{112,128},... | collective-permute-start | bytes 24584 | tf_op jit(solution)/shard_map/ppermute | solution.py:21
  14.4 10.7 %collective-permute-start.5 = (f32[16,1,128]{2,1,0:T(1,128)S(1)}, f32[16,1,128]{2,1,0:T(1,128)S(1)}, u32[]{:S(2)}, u32[]{:S(2)}) collective-permute-start(f32[16,1,128]{2,1,0:T(1,128)S(1)} %get-tuple-element.85), channel_id=1, source_target_pairs={{16,0},{32,16},{48,32},{64,48},{80,64},{96,80},{112,96},{128,112},... | collective-permute-start | bytes 24584 | tf_op jit(solution)/shard_map/ppermute | solution.py:23
  22.7 5.1 collective-permute-start.2
  27.8 8.6 %collective-permute-start.3 = (f32[4,44,6]{2,1,0:T(8,128)S(1)}, f32[4,44,6]{2,1,0:T(8,128)S(1)}, u32[]{:S(2)}, u32[]{:S(2)}) collective-permute-start(f32[4,44,6]{2,1,0:T(8,128)S(1)} %get-tuple-element.88), channel_id=1, source_target_pairs={{0,1},{1,2},{2,3},{3,4},{4,5},{5,6},{6,7},{7,8},{8,9},{9,10},{10,1... | collective-permute-start | bytes 12680 | tf_op jit(solution)/shard_map/ppermute | solution.py:21
  29.5 7.0 collective-permute-start.4
  31.0 10.6 %collective-permute-start.6 = (f32[16,34,1]{2,1,0:T(8,128)S(1)}, f32[16,34,1]{2,1,0:T(8,128)S(1)}, u32[]{:S(2)}, u32[]{:S(2)}) collective-permute-start(f32[16,34,1]{2,1,0:T(8,128)S(1)} %get-tuple-element.76), channel_id=1, source_target_pairs={{0,1},{1,2},{2,3},{3,4},{4,5},{5,6},{6,7},{7,8},{8,9},{9,10},{10,1... | collective-permute-start | bytes 6536 | tf_op jit(solution)/shard_map/ppermute | solution.py:21
  35.1 10.5 %collective-permute-start.7 = (f32[16,34,1]{2,1,0:T(8,128)S(1)}, f32[16,34,1]{2,1,0:T(8,128)S(1)}, u32[]{:S(2)}, u32[]{:S(2)}) collective-permute-start(f32[16,34,1]{2,1,0:T(8,128)S(1)} %get-tuple-element.77), channel_id=1, source_target_pairs={{1,0},{2,1},{3,2},{4,3},{5,4},{6,5},{7,6},{8,7},{9,8},{10,9},{11,1... | collective-permute-start | bytes 6536 | tf_op jit(solution)/shard_map/ppermute | solution.py:23
  46.0 6.4 collective-permute-start.8
  56.5 7.5 collective-permute-start.11
  57.8 5.8 collective-permute-start.10
  74.5 6.7 collective-permute-start.14
  79.9 5.8 collective-permute-start.15
  96.6 6.5 collective-permute-start.18
  101.7 6.4 collective-permute-start.19
  119.3 8.2 collective-permute-start.23
  120.6 6.5 collective-permute-start.22
  132.3 5.7 collective-permute-start.25
  139.0 6.8 collective-permute-start.27
  140.3 5.1 collective-permute-start.26
  149.9 24.3 %all-to-all-start = ((f32[32,1,128]{2,1,0:T(1,128)}), f32[32,1,128]{2,1,0:T(1,128)S(1)}, u32[]{:S(2)}, u32[]{:S(2)}) async-start(f32[32,1,128]{2,1,0:T(1,128)} %reshape.148), calls=%async_computation | async-start | bytes 32768 | tf_op jit(solution)/shard_map/all_to_all | solution.py:117
  167.4 647.4 %all-reduce.4.cloned.1.call-start = ((), (), s32[]{:S(2)}) async-start(), calls=%async_computation.2 | async-start | bytes 524288 | tf_op jit(solution)/shard_map/psum | solution.py:145
  201.7 6.8 collective-permute-start.31
  203.0 5.1 collective-permute-start.30
  222.7 5.8 collective-permute-start.34
  227.1 6.1 collective-permute-start.35
  248.9 7.6 collective-permute-start.38
  255.3 6.0 collective-permute-start.39
  277.3 7.5 collective-permute-start.42
  303.1 8.8 %collective-permute-start.46 = (f32[2,16,34,1]{2,1,3,0:T(8,128)S(1)}, f32[2,16,34,1]{2,1,3,0:T(8,128)}, u32[]{:S(2)}, u32[]{:S(2)}) collective-permute-start(f32[2,16,34,1]{2,1,3,0:T(8,128)S(1)} %copy.73), channel_id=1, source_target_pairs={{0,1},{1,2},{2,3},{3,4},{4,5},{5,6},{6,7},{7,8},{8,9},{9,10},{10,1... | collective-permute-start | bytes 13064 | tf_op jit(solution)/shard_map/ppermute | solution.py:21
  317.4 6.5 collective-permute-start.48
  327.2 9.9 %collective-permute-start.50 = (f32[16,34,1]{2,1,0:T(8,128)S(1)}, f32[16,34,1]{2,1,0:T(8,128)S(1)}, u32[]{:S(2)}, u32[]{:S(2)}) collective-permute-start(f32[16,34,1]{2,1,0:T(8,128)S(1)} %get-tuple-element.74), channel_id=1, source_target_pairs={{0,1},{1,2},{2,3},{3,4},{4,5},{5,6},{6,7},{7,8},{8,9},{9,10},{10,1... | collective-permute-start | bytes 6536 | tf_op jit(solution)/shard_map/ppermute | solution.py:21
  331.9 9.4 %collective-permute-start.51 = (f32[16,34,1]{2,1,0:T(8,128)S(1)}, f32[16,34,1]{2,1,0:T(8,128)S(1)}, u32[]{:S(2)}, u32[]{:S(2)}) collective-permute-start(f32[16,34,1]{2,1,0:T(8,128)S(1)} %get-tuple-element.75), channel_id=1, source_target_pairs={{1,0},{2,1},{3,2},{4,3},{5,4},{6,5},{7,6},{8,7},{9,8},{10,9},{11,1... | collective-permute-start | bytes 6536 | tf_op jit(solution)/shard_map/ppermute | solution.py:23
  (56 other events, 2030.4 us)
Sparse Core Ops, SparseCore 0:
  344.0 470.7 all-reduce.3
where the time goes:
time: 826 us; the launch traced here: 823 us
  waiting for transfers between devices  555 us (67%)
  starting transfers between devices  164 us (20%)
  local copies, waits for them, and re-layouts  46.3 us (6%)
  other arithmetic  26.5 us (3%)
  between operations  15.6 us (2%)
  blocking collectives  10.7 us (1%)
    psum x1, waiting for transfers between devices, local(): summed_modes = lax.psum(projected, ('gx', 'gy'))  471 us
    ppermute x26, starting transfers between devices, extended(): lax.ppermute(tail, axis, [(i, (i + 1) % count) for i in range(ends)])  100 us
    ppermute x26, waiting for transfers between devices, extended(): lax.ppermute(head, axis, [((i + 1) % count, i) for i in range(ends)])  66 us
    ppermute x26, starting transfers between devices, extended(): lax.ppermute(head, axis, [((i + 1) % count, i) for i in range(ends)])  45.9 us
    all_to_all x1, starting transfers between devices, local(): lax.all_to_all(picked, 'gx', split_axis=1, concat_axis=1, tiled=True)  17.4 us
    slice x27, local copies, waits for them, and re-layouts, extended(): lax.slice_in_dim(cells, cells.shape[dim] - width, cells.shape[dim], axis=...  16.5 us
  transfers between devices with their start and end apart: 54, of which 28 were waited for; matrix products, arithmetic and copies ran while one was open for 2% of the time, Pallas kernels for 0%

commit v1 on v0

--- a/solution.py
+++ b/solution.py
@@ -66,6 +66,15 @@
     return extended(state_now, (("gx", 2), ("gy", 3)), 1)
 
 
+def butterfly(values, axis):
+    count = lax.axis_size(axis)
+    stride = 1
+    while stride < count:
+        values = values + lax.ppermute(values, axis, [(i, i ^ stride) for i in range(count)])
+        stride *= 2
+    return values
+
+
 def local(
     diffusivity,
     base_humidity,
@@ -85,15 +94,20 @@
     static = jnp.stack([diffusivity, base_humidity, coupling, jnp.ones_like(diffusivity)])
     static_wide = extended(static, (("gx", 1), ("gy", 2)), rim_depth)
     static_near = window(static_wide, rim_depth, 1)
-    perturb = jnp.einsum("xa,rab->rxb", basis_rows, directions, precision=exact)
-    perturb = jnp.einsum("rxb,yb->rxy", perturb, basis_cols, precision=exact)
-    param_field = diffusivity * perturb
-    param_wide = extended(param_field, (("gx", 1), ("gy", 2)), 1)
-    source = make_source(param_wide, static_near)
+    rows_wide = extended(basis_rows, (("gx", 0),), rim_depth)
+    cols_wide = extended(basis_cols, (("gy", 0),), rim_depth)
+    perturb = jnp.einsum("xa,rab->rxb", rows_wide, directions, precision=exact)
+    perturb = jnp.einsum("rxb,yb->rxy", perturb, cols_wide, precision=exact)
+    param_wide = static_wide[0] * perturb
+    source = make_source(param_wide, static_wide)
+    src_depth = rim_depth - 1
     state_now = jnp.stack([jnp.zeros_like(source), step_ratio * source])
     for i in range(rim_depth - 1):
-        state_now = advance(state_rim(state_now), static_near, 1.0)
-        state_now = jnp.stack([state_now[0], state_now[1] + step_ratio * source])
+        depth = src_depth - i
+        state_now = advance(state_now, window(static_wide, rim_depth, depth), 1.0)
+        state_now = jnp.stack(
+            [state_now[0], state_now[1] + step_ratio * window(source, src_depth, depth - 1)]
+        )
     humid = state_now[1]
     peers = send_cell.shape[2]
     slots = send_cell.shape[3]
@@ -121,18 +135,19 @@
         n_items, peers, slots
     )
     returned = lax.all_to_all(backward, "gx", split_axis=1, concat_axis=1, tiled=True)
-    gauge_read, returned = (gauge_read, returned)
     load_values = (returned * factor).reshape(n_dirs, peers * slots)
     adjoint_load = (
         jnp.zeros((n_dirs, height * breadth), jnp.float32).at[:, cell_ids].add(load_values)
     )
     adjoint_load = adjoint_load.reshape(n_dirs, height, breadth)
-    state_now = jnp.stack([jnp.zeros_like(adjoint_load), adjoint_load])
-    summed = adjoint_load
+    load_wide = extended(adjoint_load, (("gx", 1), ("gy", 2)), rim_depth)
+    state_now = jnp.stack([jnp.zeros_like(load_wide), load_wide])
+    summed = window(load_wide, rim_depth, 1)
     for i in range(rim_depth - 1):
-        state_now = advance(state_rim(state_now), static_near, -1.0)
-        summed = summed + state_now[1]
-    lam_wide = extended(step_ratio * summed, (("gx", 1), ("gy", 2)), 1)
+        depth = rim_depth - i
+        state_now = advance(state_now, window(static_wide, rim_depth, depth), -1.0)
+        summed = summed + window(state_now[1], depth - 1, 1)
+    lam_wide = step_ratio * summed
     lam_mid, lam_near = spread(lam_wide)
     hum_mid, hum_near = spread(static_near[1])
     gradient = diffusivity * sum(
@@ -142,7 +157,7 @@
     projected = jnp.einsum("xa,rxb->rab", basis_rows, projected, precision=exact).reshape(
         n_dirs, -1
     )
-    summed_modes = lax.psum(projected, ("gx", "gy"))
+    summed_modes = butterfly(butterfly(projected, "gx"), "gy")
     hess_action = directions + summed_modes.reshape(directions.shape)
     return (gauge_read.reshape(1, 1, n_dirs, gauges), hess_action)
 

time: 826 us -> 214 us (0.26)
  the two profiles are of different devices: /device:TPU:1 before, /device:TPU:2 now
where the time goes in v1:
time: 214 us; the launch traced here: 212 us
  starting transfers between devices  84.2 us (39%)
  waiting for transfers between devices  69.9 us (33%)
  other arithmetic  28.5 us (13%)
  local copies, waits for them, and re-layouts  12 us (6%)
  blocking collectives  10.7 us (5%)
  matrix products  5.25 us (2%)
    ppermute x9, waiting for transfers between devices, butterfly(): lax.ppermute(values, axis, [(i, i ^ stride) for i in range(count)])  45.7 us
    ppermute x9, starting transfers between devices, butterfly(): lax.ppermute(values, axis, [(i, i ^ stride) for i in range(count)])  41.1 us
    ppermute x6, starting transfers between devices, extended(): lax.ppermute(tail, axis, [(i, (i + 1) % count) for i in range(ends)])  17.1 us
    ppermute x6, starting transfers between devices, extended(): lax.ppermute(head, axis, [((i + 1) % count, i) for i in range(ends)])  16.7 us
    ppermute x6, waiting for transfers between devices, extended(): lax.ppermute(head, axis, [((i + 1) % count, i) for i in range(ends)])  11.2 us
    all_to_all x1, blocking collectives, local(): lax.all_to_all(backward, 'gx', split_axis=1, concat_axis=1, tiled=True)  10.7 us
    mul x7, other arithmetic, advance(): return jnp.stack([new_temp * inside, new_hum * inside])  9.48 us
    all_to_all x1, starting transfers between devices, local(): lax.all_to_all(picked, 'gx', split_axis=1, concat_axis=1, tiled=True)  9.38 us
  transfers between devices with their start and end apart: 22, of which 14 were waited for; matrix products, arithmetic and copies ran while one was open for 7% of the time, Pallas kernels for 0%

profile of v1, /device:TPU:2, one launch (start us, length us, event | category | flops | bytes accessed | tf_op | source)
XLA Modules:
  0.0 211.9 jit_solution(5020722360895179963)
XLA Ops:
  3.3 3.6 %collective-permute-start.1 = (f32[4,6,128]{2,1,0:T(8,128)S(1)}, f32[4,6,128]{2,1,0:T(8,128)S(1)}, u32[]{:S(2)}, u32[]{:S(2)}) collective-permute-start(f32[4,6,128]{2,1,0:T(8,128)S(1)} %get-tuple-element.56), channel_id=1, source_target_pairs={{16,0},{32,16},{48,32},{64,48},{80,64},{96,80},{112,96},{128,112},... | collective-permute-start | bytes 36872 | tf_op jit(solution)/shard_map/ppermute | solution.py:23
  9.6 5.5 %collective-permute-start.5 = (f32[6,64]{1,0:T(8,128)S(1)}, f32[6,64]{1,0:T(8,128)S(1)}, u32[]{:S(2)}, u32[]{:S(2)}) collective-permute-start(f32[6,64]{1,0:T(8,128)S(1)} %get-tuple-element.92), channel_id=1, source_target_pairs={{16,0},{32,16},{48,32},{64,48},{80,64},{96,80},{112,96},{128,112},... | collective-permute-start | bytes 4616 | tf_op jit(solution)/shard_map/ppermute | solution.py:23
  16.0 1.9 collective-permute-start.6
  24.3 4.6 %collective-permute-start.2 = (f32[4,44,6]{2,1,0:T(8,128)S(1)}, f32[4,44,6]{2,1,0:T(8,128)S(1)}, u32[]{:S(2)}, u32[]{:S(2)}) collective-permute-start(f32[4,44,6]{2,1,0:T(8,128)S(1)} %get-tuple-element.53), channel_id=1, source_target_pairs={{0,1},{1,2},{2,3},{3,4},{4,5},{5,6},{6,7},{7,8},{8,9},{9,10},{10,1... | collective-permute-start | bytes 12680 | tf_op jit(solution)/shard_map/ppermute | solution.py:21
  31.6 3.8 %collective-permute-done.3 = f32[4,44,6]{2,1,0:T(8,128)S(1)} collective-permute-done((f32[4,44,6]{2,1,0:T(8,128)S(1)}, f32[4,44,6]{2,1,0:T(8,128)S(1)}, u32[]{:S(2)}, u32[]{:S(2)}) %collective-permute-start.3) | collective-permute-done | bytes 4256 | tf_op jit(solution)/shard_map/ppermute | solution.py:23
  52.2 9.4 %all-to-all-start = ((f32[32,1,128]{2,1,0:T(1,128)}), f32[32,1,128]{2,1,0:T(1,128)S(1)}, u32[]{:S(2)}, u32[]{:S(2)}) async-start(f32[32,1,128]{2,1,0:T(1,128)} %reshape.168), calls=%async_computation | async-start | bytes 32768 | tf_op jit(solution)/shard_map/all_to_all | solution.py:131
  62.4 5.3 %all-to-all-done = f32[32,1,128]{2,1,0:T(1,128)S(1)} async-done(((f32[32,1,128]{2,1,0:T(1,128)}), f32[32,1,128]{2,1,0:T(1,128)S(1)}, u32[]{:S(2)}, u32[]{:S(2)}) %all-to-all-start) | async-done | bytes 16416 | tf_op jit(solution)/shard_map/all_to_all | solution.py:131
  71.0 10.7 %all_to_all.10 = f32[32,1,128]{2,1,0:T(1,128)S(1)} all-to-all(f32[32,1,128]{2,1,0:T(1,128)S(1)} %reshape.170), channel_id=1, replica_groups=mesh['gx'=32,'gy'=16] {'gx'}, dimensions={0} | all-to-all | bytes 32768 | tf_op jit(solution)/shard_map/all_to_all | solution.py:137
  82.4 2.2 %scatter_custom_fusion = f32[16,4096]{0,1:T(8,128)S(1)} fusion(s32[256]{0:T(256)} %bitcast.138, f32[]{:T(128)} %constant.15.clone.1, f32[32,8]{1,0:T(8,128)} %copy.22, f32[32,8,16]{2,1,0:T(8,128)S(1)} %reshape.171), kind=kCustom, calls=%fused_computation.4 | custom fusion | flops 8192 | bytes 295424 | tf_op jit(solution)/shard_map/scatter-add | solution.py:140
  85.3 1.9 collective-permute-start.8
  87.2 3.6 %collective-permute-start.9 = (f32[16,6,128]{2,1,0:T(8,128)S(1)}, f32[16,6,128]{2,1,0:T(8,128)S(1)}, u32[]{:S(2)}, u32[]{:S(2)}) collective-permute-start(f32[16,6,128]{2,1,0:T(8,128)S(1)} %get-tuple-element.30), channel_id=1, source_target_pairs={{16,0},{32,16},{48,32},{64,48},{80,64},{96,80},{112,96},{128,112},... | collective-permute-start | bytes 147464 | tf_op jit(solution)/shard_map/ppermute | solution.py:23
  93.0 4.9 %collective-permute-start.10 = (f32[16,44,6]{2,1,0:T(8,128)S(1)}, f32[16,44,6]{2,1,0:T(8,128)S(1)}, u32[]{:S(2)}, u32[]{:S(2)}) collective-permute-start(f32[16,44,6]{2,1,0:T(8,128)S(1)} %get-tuple-element.27), channel_id=1, source_target_pairs={{0,1},{1,2},{2,3},{3,4},{4,5},{5,6},{6,7},{7,8},{8,9},{9,10},{10,1... | collective-permute-start | bytes 50696 | tf_op jit(solution)/shard_map/ppermute | solution.py:21
  99.4 7.6 %collective-permute-done.10 = f32[16,44,6]{2,1,0:T(8,128)S(1)} collective-permute-done((f32[16,44,6]{2,1,0:T(8,128)S(1)}, f32[16,44,6]{2,1,0:T(8,128)S(1)}, u32[]{:S(2)}, u32[]{:S(2)}) %collective-permute-start.10) | collective-permute-done | bytes 16928 | tf_op jit(solution)/shard_map/ppermute | solution.py:21
  107.1 5.6 %collective-permute-done.11 = f32[16,44,6]{2,1,0:T(8,128)S(1)} collective-permute-done((f32[16,44,6]{2,1,0:T(8,128)S(1)}, f32[16,44,6]{2,1,0:T(8,128)S(1)}, u32[]{:S(2)}, u32[]{:S(2)}) %collective-permute-start.11) | collective-permute-done | bytes 16928 | tf_op jit(solution)/shard_map/ppermute | solution.py:23
  118.8 2.4 %fusion.27 = f32[16,34,130]{2,1,0:T(8,128)S(1)} fusion(f32[16,36,132]{2,1,0:T(8,128)S(1)} %slice.904, f32[16,36,132]{2,1,0:T(8,128)S(1)} %get-tuple-element.21, f32[16,36,132]{2,1,0:T(8,128)S(1)} %get-tuple-element.22, f32[16,36,132]{2,1,0:T(8,128)S(1)} %get-tuple-element.19, f32[16,36,132]{2,1,0:T(8,128)S(1)} %get-tuple-element.20, ...), kind=kLoop, calls=%fused_computation.42 | loop fusion | flops 2121600 | bytes 4384640 | tf_op jit(solution)/shard_map/mul | solution.py:150
  123.5 1.9 collective-permute-start.12
  126.8 1.9 collective-permute-start.13
  128.7 5.5 %collective-permute-done.13 = f32[16,2048]{1,0:T(8,128)S(1)} collective-permute-done((f32[16,2048]{1,0:T(8,128)S(1)}, f32[16,2048]{1,0:T(8,128)S(1)}, u32[]{:S(2)}, u32[]{:S(2)}) %collective-permute-start.13) | collective-permute-done | bytes 131104 | tf_op jit(solution)/shard_map/ppermute | solution.py:73
  134.2 3.3 %collective-permute-start.14 = (f32[16,2048]{1,0:T(8,128)S(1)}, f32[16,2048]{1,0:T(8,128)S(1)}, u32[]{:S(2)}, u32[]{:S(2)}) collective-permute-start(f32[16,2048]{1,0:T(8,128)S(1)} %add.533), channel_id=1, source_target_pairs={{0,64},{16,80},{32,96},{48,112},{64,0},{80,16},{96,32},{112,48},{1... | collective-permute-start | bytes 393224 | tf_op jit(solution)/shard_map/ppermute | solution.py:73
  137.5 5.1 %collective-permute-done.14 = f32[16,2048]{1,0:T(8,128)S(1)} collective-permute-done((f32[16,2048]{1,0:T(8,128)S(1)}, f32[16,2048]{1,0:T(8,128)S(1)}, u32[]{:S(2)}, u32[]{:S(2)}) %collective-permute-start.14) | collective-permute-done | bytes 131104 | tf_op jit(solution)/shard_map/ppermute | solution.py:73
  142.6 2.5 %collective-permute-start.15 = (f32[16,2048]{1,0:T(8,128)S(1)}, f32[16,2048]{1,0:T(8,128)S(1)}, u32[]{:S(2)}, u32[]{:S(2)}) collective-permute-start(f32[16,2048]{1,0:T(8,128)S(1)} %add.534), channel_id=1, source_target_pairs={{0,128},{16,144},{32,160},{48,176},{64,192},{80,208},{96,224},{112... | collective-permute-start | bytes 393224 | tf_op jit(solution)/shard_map/ppermute | solution.py:73
  145.1 4.3 %collective-permute-done.15 = f32[16,2048]{1,0:T(8,128)S(1)} collective-permute-done((f32[16,2048]{1,0:T(8,128)S(1)}, f32[16,2048]{1,0:T(8,128)S(1)}, u32[]{:S(2)}, u32[]{:S(2)}) %collective-permute-start.15) | collective-permute-done | bytes 131104 | tf_op jit(solution)/shard_map/ppermute | solution.py:73
  149.5 3.1 %collective-permute-start.16 = (f32[16,2048]{1,0:T(8,128)S(1)}, f32[16,2048]{1,0:T(8,128)S(1)}, u32[]{:S(2)}, u32[]{:S(2)}) collective-permute-start(f32[16,2048]{1,0:T(8,128)S(1)} %add.535), channel_id=1, source_target_pairs={{0,256},{16,272},{32,288},{48,304},{64,320},{80,336},{96,352},{112... | collective-permute-start | bytes 393224 | tf_op jit(solution)/shard_map/ppermute | solution.py:73
  152.6 5.2 %collective-permute-done.16 = f32[16,2048]{1,0:T(8,128)S(1)} collective-permute-done((f32[16,2048]{1,0:T(8,128)S(1)}, f32[16,2048]{1,0:T(8,128)S(1)}, u32[]{:S(2)}, u32[]{:S(2)}) %collective-permute-start.16) | collective-permute-done | bytes 131104 | tf_op jit(solution)/shard_map/ppermute | solution.py:73
  157.9 5.1 %collective-permute-start.17 = (f32[16,2048]{1,0:T(8,128)S(1)}, f32[16,2048]{1,0:T(8,128)S(1)}, u32[]{:S(2)}, u32[]{:S(2)}) collective-permute-start(f32[16,2048]{1,0:T(8,128)S(1)} %add.536), channel_id=1, source_target_pairs={{0,1},{1,0},{2,3},{3,2},{4,5},{5,4},{6,7},{7,6},{8,9},{9,8},{10,11... | collective-permute-start | bytes 393224 | tf_op jit(solution)/shard_map/ppermute | solution.py:73
  163.0 2.9 %collective-permute-done.17 = f32[16,2048]{1,0:T(8,128)S(1)} collective-permute-done((f32[16,2048]{1,0:T(8,128)S(1)}, f32[16,2048]{1,0:T(8,128)S(1)}, u32[]{:S(2)}, u32[]{:S(2)}) %collective-permute-start.17) | collective-permute-done | bytes 131104 | tf_op jit(solution)/shard_map/ppermute | solution.py:73
  166.0 6.1 %collective-permute-start.18 = (f32[16,2048]{1,0:T(8,128)S(1)}, f32[16,2048]{1,0:T(8,128)S(1)}, u32[]{:S(2)}, u32[]{:S(2)}) collective-permute-start(f32[16,2048]{1,0:T(8,128)S(1)} %add.537), channel_id=1, source_target_pairs={{0,2},{1,3},{2,0},{3,1},{4,6},{5,7},{6,4},{7,5},{8,10},{9,11},{10,... | collective-permute-start | bytes 393224 | tf_op jit(solution)/shard_map/ppermute | solution.py:73
  172.1 4.3 %collective-permute-done.18 = f32[16,2048]{1,0:T(8,128)S(1)} collective-permute-done((f32[16,2048]{1,0:T(8,128)S(1)}, f32[16,2048]{1,0:T(8,128)S(1)}, u32[]{:S(2)}, u32[]{:S(2)}) %collective-permute-start.18) | collective-permute-done | bytes 131104 | tf_op jit(solution)/shard_map/ppermute | solution.py:73
  176.4 11.6 %collective-permute-start.19 = (f32[16,2048]{1,0:T(8,128)S(1)}, f32[16,2048]{1,0:T(8,128)S(1)}, u32[]{:S(2)}, u32[]{:S(2)}) collective-permute-start(f32[16,2048]{1,0:T(8,128)S(1)} %add.538), channel_id=1, source_target_pairs={{0,4},{1,5},{2,6},{3,7},{4,0},{5,1},{6,2},{7,3},{8,12},{9,13},{10,... | collective-permute-start | bytes 393224 | tf_op jit(solution)/shard_map/ppermute | solution.py:73
  188.1 4.7 %collective-permute-done.19 = f32[16,2048]{1,0:T(8,128)S(1)} collective-permute-done((f32[16,2048]{1,0:T(8,128)S(1)}, f32[16,2048]{1,0:T(8,128)S(1)}, u32[]{:S(2)}, u32[]{:S(2)}) %collective-permute-start.19) | collective-permute-done | bytes 131104 | tf_op jit(solution)/shard_map/ppermute | solution.py:73
  192.8 5.4 %collective-permute-start.20 = (f32[16,2048]{1,0:T(8,128)S(1)}, f32[16,2048]{1,0:T(8,128)S(1)}, u32[]{:S(2)}, u32[]{:S(2)}) collective-permute-start(f32[16,2048]{1,0:T(8,128)S(1)} %add.539), channel_id=1, source_target_pairs={{0,8},{1,9},{2,10},{3,11},{4,12},{5,13},{6,14},{7,15},{8,0},{9,1},... | collective-permute-start | bytes 393224 | tf_op jit(solution)/shard_map/ppermute | solution.py:73
  198.5 12.3 %collective-permute-done.20 = f32[16,2048]{1,0:T(8,128)S(1)} collective-permute-done((f32[16,2048]{1,0:T(8,128)S(1)}, f32[16,2048]{1,0:T(8,128)S(1)}, u32[]{:S(2)}, u32[]{:S(2)}) %collective-permute-start.20) | collective-permute-done | bytes 131104 | tf_op jit(solution)/shard_map/ppermute | solution.py:73
  (124 shorter events, 51.9 us)
Async XLA Ops:
  1.4 20.7 %collective-permute-start = (f32[4,6,128]{2,1,0:T(8,128)S(1)}, f32[4,6,128]{2,1,0:T(8,128)S(1)}, u32[]{:S(2)}, u32[]{:S(2)}) collective-permute-start(f32[4,6,128]{2,1,0:T(8,128)S(1)} %get-tuple-element.55), channel_id=1, source_target_pairs={{0,16},{16,32},{32,48},{48,64},{64,80},{80,96},{96,112},{112,128},... | collective-permute-start | bytes 36872 | tf_op jit(solution)/shard_map/ppermute | solution.py:21
  3.3 20.1 %collective-permute-start.1 = (f32[4,6,128]{2,1,0:T(8,128)S(1)}, f32[4,6,128]{2,1,0:T(8,128)S(1)}, u32[]{:S(2)}, u32[]{:S(2)}) collective-permute-start(f32[4,6,128]{2,1,0:T(8,128)S(1)} %get-tuple-element.56), channel_id=1, source_target_pairs={{16,0},{32,16},{48,32},{64,48},{80,64},{96,80},{112,96},{128,112},... | collective-permute-start | bytes 36872 | tf_op jit(solution)/shard_map/ppermute | solution.py:23
  7.7 21.2 %collective-permute-start.4 = (f32[6,64]{1,0:T(8,128)S(1)}, f32[6,64]{1,0:T(8,128)S(1)}, u32[]{:S(2)}, u32[]{:S(2)}) collective-permute-start(f32[6,64]{1,0:T(8,128)S(1)} %get-tuple-element.91), channel_id=1, source_target_pairs={{0,16},{16,32},{32,48},{48,64},{64,80},{80,96},{96,112},{112,128},... | collective-permute-start | bytes 4616 | tf_op jit(solution)/shard_map/ppermute | solution.py:21
  9.6 20.6 %collective-permute-start.5 = (f32[6,64]{1,0:T(8,128)S(1)}, f32[6,64]{1,0:T(8,128)S(1)}, u32[]{:S(2)}, u32[]{:S(2)}) collective-permute-start(f32[6,64]{1,0:T(8,128)S(1)} %get-tuple-element.92), channel_id=1, source_target_pairs={{16,0},{32,16},{48,32},{64,48},{80,64},{96,80},{112,96},{128,112},... | collective-permute-start | bytes 4616 | tf_op jit(solution)/shard_map/ppermute | solution.py:23
  16.0 23.9 %collective-permute-start.6 = (f32[6,32]{0,1:T(8,128)S(1)}, f32[6,32]{0,1:T(8,128)S(1)}, u32[]{:S(2)}, u32[]{:S(2)}) collective-permute-start(f32[6,32]{0,1:T(8,128)S(1)} %get-tuple-element.89), channel_id=1, source_target_pairs={{0,1},{1,2},{2,3},{3,4},{4,5},{5,6},{6,7},{7,8},{8,9},{9,10},{10,1... | collective-permute-start | bytes 2312 | tf_op jit(solution)/shard_map/ppermute | solution.py:21
  19.5 3.9 %copy-start.11 = (s32[256,1]{0,1:T(1,128)}, s32[256,1]{0,1:T(1,128)S(1)}, u32[]{:S(2)}) copy-start(s32[256,1]{0,1:T(1,128)S(1)} %compare_select_fusion.1) | copy-start | bytes 3076
  22.1 17.8 %collective-permute-start.7 = (f32[6,32]{0,1:T(8,128)S(1)}, f32[6,32]{0,1:T(8,128)S(1)}, u32[]{:S(2)}, u32[]{:S(2)}) collective-permute-start(f32[6,32]{0,1:T(8,128)S(1)} %get-tuple-element.90), channel_id=1, source_target_pairs={{1,0},{2,1},{3,2},{4,3},{5,4},{6,5},{7,6},{8,7},{9,8},{10,9},{11,1... | collective-permute-start | bytes 2312 | tf_op jit(solution)/shard_map/ppermute | solution.py:23
  24.3 7.2 %collective-permute-start.2 = (f32[4,44,6]{2,1,0:T(8,128)S(1)}, f32[4,44,6]{2,1,0:T(8,128)S(1)}, u32[]{:S(2)}, u32[]{:S(2)}) collective-permute-start(f32[4,44,6]{2,1,0:T(8,128)S(1)} %get-tuple-element.53), channel_id=1, source_target_pairs={{0,1},{1,2},{2,3},{3,4},{4,5},{5,6},{6,7},{7,8},{8,9},{9,10},{10,1... | collective-permute-start | bytes 12680 | tf_op jit(solution)/shard_map/ppermute | solution.py:21
  28.9 6.5 %collective-permute-start.3 = (f32[4,44,6]{2,1,0:T(8,128)S(1)}, f32[4,44,6]{2,1,0:T(8,128)S(1)}, u32[]{:S(2)}, u32[]{:S(2)}) collective-permute-start(f32[4,44,6]{2,1,0:T(8,128)S(1)} %get-tuple-element.54), channel_id=1, source_target_pairs={{1,0},{2,1},{3,2},{4,3},{5,4},{6,5},{7,6},{8,7},{9,8},{10,9},{11,1... | collective-permute-start | bytes 12680 | tf_op jit(solution)/shard_map/ppermute | solution.py:23
  31.5 8.4 %copy-start.6 = (f32[128,32]{0,1:T(8,128)S(1)}, f32[128,32]{0,1:T(8,128)}, u32[]{:S(2)}) copy-start(f32[128,32]{0,1:T(8,128)} %param.15) | copy-start | bytes 49156
  46.7 1.6 copy-start.1
  52.2 15.6 %all-to-all-start = ((f32[32,1,128]{2,1,0:T(1,128)}), f32[32,1,128]{2,1,0:T(1,128)S(1)}, u32[]{:S(2)}, u32[]{:S(2)}) async-start(f32[32,1,128]{2,1,0:T(1,128)} %reshape.168), calls=%async_computation | async-start | bytes 32768 | tf_op jit(solution)/shard_map/all_to_all | solution.py:131
  85.3 5.7 %collective-permute-start.8 = (f32[16,6,128]{2,1,0:T(8,128)S(1)}, f32[16,6,128]{2,1,0:T(8,128)S(1)}, u32[]{:S(2)}, u32[]{:S(2)}) collective-permute-start(f32[16,6,128]{2,1,0:T(8,128)S(1)} %get-tuple-element.29), channel_id=1, source_target_pairs={{0,16},{16,32},{32,48},{48,64},{64,80},{80,96},{96,112},{112,128},... | collective-permute-start | bytes 147464 | tf_op jit(solution)/shard_map/ppermute | solution.py:21
  87.2 5.5 %collective-permute-start.9 = (f32[16,6,128]{2,1,0:T(8,128)S(1)}, f32[16,6,128]{2,1,0:T(8,128)S(1)}, u32[]{:S(2)}, u32[]{:S(2)}) collective-permute-start(f32[16,6,128]{2,1,0:T(8,128)S(1)} %get-tuple-element.30), channel_id=1, source_target_pairs={{16,0},{32,16},{48,32},{64,48},{80,64},{96,80},{112,96},{128,112},... | collective-permute-start | bytes 147464 | tf_op jit(solution)/shard_map/ppermute | solution.py:23
  92.8 20.3 %copy-start.2 = (f32[42,138]{1,0:T(8,128)S(1)}, f32[42,138]{1,0:T(8,128)}, u32[]{:S(2)}) copy-start(f32[42,138]{1,0:T(8,128)} %get-tuple-element.48) | copy-start | bytes 69556
  93.0 14.1 %collective-permute-start.10 = (f32[16,44,6]{2,1,0:T(8,128)S(1)}, f32[16,44,6]{2,1,0:T(8,128)S(1)}, u32[]{:S(2)}, u32[]{:S(2)}) collective-permute-start(f32[16,44,6]{2,1,0:T(8,128)S(1)} %get-tuple-element.27), channel_id=1, source_target_pairs={{0,1},{1,2},{2,3},{3,4},{4,5},{5,6},{6,7},{7,8},{8,9},{9,10},{10,1... | collective-permute-start | bytes 50696 | tf_op jit(solution)/shard_map/ppermute | solution.py:21
  97.9 14.8 %collective-permute-start.11 = (f32[16,44,6]{2,1,0:T(8,128)S(1)}, f32[16,44,6]{2,1,0:T(8,128)S(1)}, u32[]{:S(2)}, u32[]{:S(2)}) collective-permute-start(f32[16,44,6]{2,1,0:T(8,128)S(1)} %get-tuple-element.28), channel_id=1, source_target_pairs={{1,0},{2,1},{3,2},{4,3},{5,4},{6,5},{7,6},{8,7},{9,8},{10,9},{11,1... | collective-permute-start | bytes 50696 | tf_op jit(solution)/shard_map/ppermute | solution.py:23
  114.1 1.5 copy-start.4
  117.3 1.4 copy-start.3
  118.7 2.4 %copy-start.7 = (f32[128,32]{0,1:T(8,128)S(1)}, f32[128,32]{0,1:T(8,128)}, u32[]{:S(2)}) copy-start(f32[128,32]{0,1:T(8,128)} %param.15) | copy-start | bytes 49156
  118.7 2.4 %copy-start.8 = (f32[32,128]{1,0:T(8,128)S(1)}, f32[32,128]{1,0:T(8,128)}, u32[]{:S(2)}) copy-start(f32[32,128]{1,0:T(8,128)} %param.11) | copy-start | bytes 49156
  118.8 3.9 %copy-start.9 = (f32[32,64]{1,0:T(8,128)S(1)}, f32[32,64]{1,0:T(8,128)}, u32[]{:S(2)}) copy-start(f32[32,64]{1,0:T(8,128)} %param.14) | copy-start | bytes 24580
  123.0 75.2 %copy-start = (f32[16,64,32]{1,2,0:T(8,128)S(1)}, f32[16,64,32]{1,2,0:T(8,128)}, u32[]{:S(2)}) copy-start(f32[16,64,32]{1,2,0:T(8,128)} %param.16) | copy-start | bytes 393220
  123.5 3.2 %collective-permute-start.12 = (f32[16,2048]{1,0:T(8,128)S(1)}, f32[16,2048]{1,0:T(8,128)S(1)}, u32[]{:S(2)}, u32[]{:S(2)}) collective-permute-start(f32[16,2048]{1,0:T(8,128)S(1)} %reshape.143), channel_id=1, source_target_pairs={{0,16},{16,0},{32,48},{48,32},{64,80},{80,64},{96,112},{112,96},{1... | collective-permute-start | bytes 393224 | tf_op jit(solution)/shard_map/ppermute | solution.py:73
  126.8 7.4 %collective-permute-start.13 = (f32[16,2048]{1,0:T(8,128)S(1)}, f32[16,2048]{1,0:T(8,128)S(1)}, u32[]{:S(2)}, u32[]{:S(2)}) collective-permute-start(f32[16,2048]{1,0:T(8,128)S(1)} %add.532), channel_id=1, source_target_pairs={{0,32},{16,48},{32,0},{48,16},{64,96},{80,112},{96,64},{112,80},{1... | collective-permute-start | bytes 393224 | tf_op jit(solution)/shard_map/ppermute | solution.py:73
  134.2 8.4 %collective-permute-start.14 = (f32[16,2048]{1,0:T(8,128)S(1)}, f32[16,2048]{1,0:T(8,128)S(1)}, u32[]{:S(2)}, u32[]{:S(2)}) collective-permute-start(f32[16,2048]{1,0:T(8,128)S(1)} %add.533), channel_id=1, source_target_pairs={{0,64},{16,80},{32,96},{48,112},{64,0},{80,16},{96,32},{112,48},{1... | collective-permute-start | bytes 393224 | tf_op jit(solution)/shard_map/ppermute | solution.py:73
  142.6 6.9 %collective-permute-start.15 = (f32[16,2048]{1,0:T(8,128)S(1)}, f32[16,2048]{1,0:T(8,128)S(1)}, u32[]{:S(2)}, u32[]{:S(2)}) collective-permute-start(f32[16,2048]{1,0:T(8,128)S(1)} %add.534), channel_id=1, source_target_pairs={{0,128},{16,144},{32,160},{48,176},{64,192},{80,208},{96,224},{112... | collective-permute-start | bytes 393224 | tf_op jit(solution)/shard_map/ppermute | solution.py:73
  149.5 8.4 %collective-permute-start.16 = (f32[16,2048]{1,0:T(8,128)S(1)}, f32[16,2048]{1,0:T(8,128)S(1)}, u32[]{:S(2)}, u32[]{:S(2)}) collective-permute-start(f32[16,2048]{1,0:T(8,128)S(1)} %add.535), channel_id=1, source_target_pairs={{0,256},{16,272},{32,288},{48,304},{64,320},{80,336},{96,352},{112... | collective-permute-start | bytes 393224 | tf_op jit(solution)/shard_map/ppermute | solution.py:73
  157.9 8.1 %collective-permute-start.17 = (f32[16,2048]{1,0:T(8,128)S(1)}, f32[16,2048]{1,0:T(8,128)S(1)}, u32[]{:S(2)}, u32[]{:S(2)}) collective-permute-start(f32[16,2048]{1,0:T(8,128)S(1)} %add.536), channel_id=1, source_target_pairs={{0,1},{1,0},{2,3},{3,2},{4,5},{5,4},{6,7},{7,6},{8,9},{9,8},{10,11... | collective-permute-start | bytes 393224 | tf_op jit(solution)/shard_map/ppermute | solution.py:73
  166.0 10.5 %collective-permute-start.18 = (f32[16,2048]{1,0:T(8,128)S(1)}, f32[16,2048]{1,0:T(8,128)S(1)}, u32[]{:S(2)}, u32[]{:S(2)}) collective-permute-start(f32[16,2048]{1,0:T(8,128)S(1)} %add.537), channel_id=1, source_target_pairs={{0,2},{1,3},{2,0},{3,1},{4,6},{5,7},{6,4},{7,5},{8,10},{9,11},{10,... | collective-permute-start | bytes 393224 | tf_op jit(solution)/shard_map/ppermute | solution.py:73
  176.4 16.3 %collective-permute-start.19 = (f32[16,2048]{1,0:T(8,128)S(1)}, f32[16,2048]{1,0:T(8,128)S(1)}, u32[]{:S(2)}, u32[]{:S(2)}) collective-permute-start(f32[16,2048]{1,0:T(8,128)S(1)} %add.538), channel_id=1, source_target_pairs={{0,4},{1,5},{2,6},{3,7},{4,0},{5,1},{6,2},{7,3},{8,12},{9,13},{10,... | collective-permute-start | bytes 393224 | tf_op jit(solution)/shard_map/ppermute | solution.py:73
  192.8 18.0 %collective-permute-start.20 = (f32[16,2048]{1,0:T(8,128)S(1)}, f32[16,2048]{1,0:T(8,128)S(1)}, u32[]{:S(2)}, u32[]{:S(2)}) collective-permute-start(f32[16,2048]{1,0:T(8,128)S(1)} %add.539), channel_id=1, source_target_pairs={{0,8},{1,9},{2,10},{3,11},{4,12},{5,13},{6,14},{7,15},{8,0},{9,1},... | collective-permute-start | bytes 393224 | tf_op jit(solution)/shard_map/ppermute | solution.py:73
  (2 other events, 1.5 us)

commit v2 on v1

--- a/solution.py
+++ b/solution.py
@@ -66,6 +66,29 @@
     return extended(state_now, (("gx", 2), ("gy", 3)), 1)
 
 
+def exchange(parts, axis, width):
+    count = lax.axis_size(axis)
+    ends = count - 1
+    heads = [lax.slice_in_dim(a, 0, width, axis=d) for a, d in parts]
+    tails = [lax.slice_in_dim(a, a.shape[d] - width, a.shape[d], axis=d) for a, d in parts]
+
+    def pack(pieces):
+        return jnp.concatenate([p.reshape(-1) for p in pieces])
+
+    def unpack(flat, like):
+        out, offset = [], 0
+        for p in like:
+            out.append(flat[offset : offset + p.size].reshape(p.shape))
+            offset += p.size
+        return out
+
+    from_prev = unpack(lax.ppermute(pack(tails), axis, [(i, i + 1) for i in range(ends)]), tails)
+    from_next = unpack(lax.ppermute(pack(heads), axis, [(i + 1, i) for i in range(ends)]), heads)
+    return [
+        jnp.concatenate([p, a, n], axis=d) for (a, d), p, n in zip(parts, from_prev, from_next)
+    ]
+
+
 def butterfly(values, axis):
     count = lax.axis_size(axis)
     stride = 1
@@ -73,6 +96,19 @@
         values = values + lax.ppermute(values, axis, [(i, i ^ stride) for i in range(count)])
         stride *= 2
     return values
+
+
+def all_sum(values):
+    count = lax.axis_size("gx")
+    flat = values.reshape(count, -1, 128)
+    part = lax.all_to_all(flat, "gx", 0, 0, tiled=True).sum(0)
+    part = butterfly(part, "gy")
+    spread_out = jnp.broadcast_to(part[None], (count,) + part.shape)
+    return lax.all_to_all(spread_out, "gx", 0, 0, tiled=True).reshape(values.shape)
+
+
+def pad_sides(field, width):
+    return jnp.pad(field, [(0, 0)] * (field.ndim - 2) + [(width, width), (width, width)])
 
 
 def local(
@@ -89,22 +125,24 @@
     noise_precision,
 ):
     rim_depth = STEPS
+    reach = rim_depth + 1
     height, breadth = diffusivity.shape
     n_dirs = directions.shape[0]
     static = jnp.stack([diffusivity, base_humidity, coupling, jnp.ones_like(diffusivity)])
-    static_wide = extended(static, (("gx", 1), ("gy", 2)), rim_depth)
-    static_near = window(static_wide, rim_depth, 1)
-    rows_wide = extended(basis_rows, (("gx", 0),), rim_depth)
-    cols_wide = extended(basis_cols, (("gy", 0),), rim_depth)
-    perturb = jnp.einsum("xa,rab->rxb", rows_wide, directions, precision=exact)
-    perturb = jnp.einsum("rxb,yb->rxy", perturb, cols_wide, precision=exact)
-    param_wide = static_wide[0] * perturb
-    source = make_source(param_wide, static_wide)
+    static_gx, rows_wide = exchange(((static, 1), (basis_rows, 0)), "gx", reach)
+    static_wide, cols_wide = exchange(((static_gx, 2), (basis_cols, 0)), "gy", reach)
+    static_six = window(static_wide, reach, rim_depth)
+    rows_six = rows_wide[1:-1]
+    cols_six = cols_wide[1:-1]
+    perturb = jnp.einsum("xa,rab->rxb", rows_six, directions, precision=exact)
+    perturb = jnp.einsum("rxb,yb->rxy", perturb, cols_six, precision=exact)
+    param_wide = static_six[0] * perturb
+    source = make_source(param_wide, static_six)
     src_depth = rim_depth - 1
     state_now = jnp.stack([jnp.zeros_like(source), step_ratio * source])
     for i in range(rim_depth - 1):
         depth = src_depth - i
-        state_now = advance(state_now, window(static_wide, rim_depth, depth), 1.0)
+        state_now = advance(state_now, window(static_wide, reach, depth), 1.0)
         state_now = jnp.stack(
             [state_now[0], state_now[1] + step_ratio * window(source, src_depth, depth - 1)]
         )
@@ -139,25 +177,21 @@
     adjoint_load = (
         jnp.zeros((n_dirs, height * breadth), jnp.float32).at[:, cell_ids].add(load_values)
     )
-    adjoint_load = adjoint_load.reshape(n_dirs, height, breadth)
-    load_wide = extended(adjoint_load, (("gx", 1), ("gy", 2)), rim_depth)
+    load_wide = pad_sides(adjoint_load.reshape(n_dirs, height, breadth), rim_depth)
     state_now = jnp.stack([jnp.zeros_like(load_wide), load_wide])
-    summed = window(load_wide, rim_depth, 1)
+    summed = load_wide
     for i in range(rim_depth - 1):
-        depth = rim_depth - i
-        state_now = advance(state_now, window(static_wide, rim_depth, depth), -1.0)
-        summed = summed + window(state_now[1], depth - 1, 1)
-    lam_wide = step_ratio * summed
+        state_now = pad_sides(advance(state_now, static_six, -1.0), 1)
+        summed = summed + state_now[1]
+    lam_wide = pad_sides(step_ratio * summed, 1)
     lam_mid, lam_near = spread(lam_wide)
-    hum_mid, hum_near = spread(static_near[1])
-    gradient = diffusivity * sum(
+    hum_mid, hum_near = spread(static_wide[1])
+    gradient = static_six[0] * sum(
         (0.5 * (h - hum_mid) * (lam_mid - l) for h, l in zip(hum_near, lam_near))
     )
-    projected = jnp.einsum("rxy,yb->rxb", gradient, basis_cols, precision=exact)
-    projected = jnp.einsum("xa,rxb->rab", basis_rows, projected, precision=exact).reshape(
-        n_dirs, -1
-    )
-    summed_modes = butterfly(butterfly(projected, "gx"), "gy")
+    projected = jnp.einsum("rxy,yb->rxb", gradient, cols_six, precision=exact)
+    projected = jnp.einsum("xa,rxb->rab", rows_six, projected, precision=exact)
+    summed_modes = all_sum(projected.reshape(n_dirs, -1))
     hess_action = directions + summed_modes.reshape(directions.shape)
     return (gauge_read.reshape(1, 1, n_dirs, gauges), hess_action)
 

time: 214 us -> 149 us (0.70)
  the two profiles are of different devices: /device:TPU:2 before, /device:TPU:1 now
where the time goes in v2:
time: 149 us; the launch traced here: 148 us
  starting transfers between devices  61.5 us (41%)
  waiting for transfers between devices  29.1 us (20%)
  other arithmetic  26 us (17%)
  local copies, waits for them, and re-layouts  13.5 us (9%)
  blocking collectives  11.3 us (8%)
  matrix products  5 us (3%)
    ppermute x4, starting transfers between devices, butterfly(): lax.ppermute(values, axis, [(i, i ^ stride) for i in range(count)])  29.5 us
    all_to_all x1, blocking collectives, all_sum(): part = lax.all_to_all(flat, 'gx', 0, 0, tiled=True).sum(0)  11.3 us
    another operation x9, other arithmetic, advance(): return jnp.stack([new_temp * inside, new_hum * inside])  10 us
    all_to_all x1, starting transfers between devices, all_sum(): lax.all_to_all(spread_out, 'gx', 0, 0, tiled=True).reshape(values.shape)  7.68 us
    all_to_all x1, starting transfers between devices, local(): lax.all_to_all(picked, 'gx', split_axis=1, concat_axis=1, tiled=True)  7.65 us
    all_to_all x1, waiting for transfers between devices, all_sum(): lax.all_to_all(spread_out, 'gx', 0, 0, tiled=True).reshape(values.shape)  7.5 us
    all_to_all x1, waiting for transfers between devices, local(): lax.all_to_all(backward, 'gx', split_axis=1, concat_axis=1, tiled=True)  6.91 us
    ppermute x2, starting transfers between devices, exchange(): lax.ppermute(pack(heads), axis, [(i + 1, i) for i in range(ends)])  6.81 us
  transfers between devices with their start and end apart: 11, of which 8 were waited for; matrix products, arithmetic and copies ran while one was open for 5% of the time, Pallas kernels for 0%

profile of v2, /device:TPU:1, one launch (start us, length us, event | category | flops | bytes accessed | tf_op | source)
XLA Modules:
  0.0 147.8 jit_solution(1715925223878090026)
XLA Ops:
  2.3 4.5 %collective-permute-start = (f32[4032]{0:T(1024)S(1)}, f32[4032]{0:T(1024)S(1)}, u32[]{:S(2)}, u32[]{:S(2)}) collective-permute-start(f32[4032]{0:T(1024)S(1)} %pad_maximum_fusion.12), channel_id=1, source_target_pairs={{0,16},{16,32},{32,48},{48,64},{64,80},{80,96},{96,112},{112,128},... | collective-permute-start | bytes 48392 | tf_op jit(solution)/shard_map/ppermute | solution.py:85
  6.9 5.5 %collective-permute-start.1 = (f32[4032]{0:T(1024)S(1)}, f32[4032]{0:T(1024)S(1)}, u32[]{:S(2)}, u32[]{:S(2)}) collective-permute-start(f32[4032]{0:T(1024)S(1)} %pad_maximum_fusion.13), channel_id=1, source_target_pairs={{16,0},{32,16},{48,32},{64,48},{80,64},{96,80},{112,96},{128,112},... | collective-permute-start | bytes 48392 | tf_op jit(solution)/shard_map/ppermute | solution.py:86
  18.1 1.3 collective-permute-start.2
  19.7 1.3 collective-permute-start.3
  21.1 1.1 fusion.263
  22.4 1.8 %collective-permute-done.3 = f32[1512]{0:T(1024)S(1)} collective-permute-done((f32[1512]{0:T(1024)S(1)}, f32[1512]{0:T(1024)S(1)}, u32[]{:S(2)}, u32[]{:S(2)}) %collective-permute-start.3) | collective-permute-done | bytes 6080 | tf_op jit(solution)/shard_map/ppermute | solution.py:86
  28.2 0.9 multiply_multiply_fusion
  29.1 1.6 %fusion.164 = (f32[16,38,134]{2,1,0:T(8,128)S(1)}, f32[16,38,134]{2,1,0:T(8,128)S(1)}) fusion(f32[16,40,136]{2,1,0:T(8,128)S(1)} %get-tuple-element.26, f32[16,40,136]{2,1,0:T(8,128)S(1)} %get-tuple-element.27, f32[38,134]{1,0:T(8,128)S(1)} %get-tuple-element.44, f32[38,134]{1,0:T(8,128)S(1)} %get-tuple-element.45, f32[16,42,138]{2,1,0:T(8,128)S(1)} %get-tuple-element.5, ...), kind=kLoop, calls=%fused_computation.248 | loop fusion | flops 2444160 | bytes 4358752 | tf_op jit(solution)/shard_map/mul | solution.py:53
  30.8 1.6 %fusion.145 = (f32[16,36,132]{2,1,0:T(8,128)S(1)}, f32[16,36,132]{2,1,0:T(8,128)S(1)}) fusion(f32[16,38,134]{2,1,0:T(8,128)S(1)} %get-tuple-element.24, f32[16,38,134]{2,1,0:T(8,128)S(1)} %get-tuple-element.25, f32[36,132]{1,0:T(8,128)S(1)} %get-tuple-element.41, f32[36,132]{1,0:T(8,128)S(1)} %get-tuple-element.42, f32[16,42,138]{2,1,0:T(8,128)S(1)} %get-tuple-element.5, ...), kind=kLoop, calls=%fused_computation.220 | loop fusion | flops 2280960 | bytes 4067712 | tf_op jit(solution)/shard_map/mul | solution.py:53
  33.1 1.6 %fusion.140 = (f32[16,34,130]{2,1,0:T(8,128)S(1)}, f32[16,34,130]{2,1,0:T(8,128)S(1)}, f32[16,34,130]{2,1,0:T(8,128)S(1)}, f32[16,34,130]{2,1,0:T(8,128)S(1)}) fusion(f32[16,42,138]{2,1,0:T(8,128)S(1)} %get-tuple-element.5, f32[16,36,132]{2,1,0:T(8,128)S(1)} %get-tuple-element.23, f32[34,130]{1,0:T(8,128)S(1)} %get-tuple-element.38, ...), kind=kLoop, calls=%fused_computation.214 | loop fusion | flops 1555840 | bytes 4349280 | tf_op jit(solution)/shard_map/add | solution.py:147
  37.8 7.7 %all-to-all-start = ((f32[32,1,128]{2,1,0:T(1,128)}), f32[32,1,128]{2,1,0:T(1,128)S(1)}, u32[]{:S(2)}, u32[]{:S(2)}) async-start(f32[32,1,128]{2,1,0:T(1,128)} %reshape.239), calls=%async_computation | async-start | bytes 32768 | tf_op jit(solution)/shard_map/all_to_all | solution.py:169
  45.6 6.8 %all-to-all-done = f32[32,1,128]{2,1,0:T(1,128)S(1)} async-done(((f32[32,1,128]{2,1,0:T(1,128)}), f32[32,1,128]{2,1,0:T(1,128)S(1)}, u32[]{:S(2)}, u32[]{:S(2)}) %all-to-all-start) | async-done | bytes 16416 | tf_op jit(solution)/shard_map/all_to_all | solution.py:169
  55.0 4.1 %all-to-all-start.1 = ((f32[32,1,128]{2,1,0:T(1,128)}), f32[32,1,128]{2,1,0:T(1,128)S(1)}, u32[]{:S(2)}, u32[]{:S(2)}) async-start(f32[32,1,128]{2,1,0:T(1,128)} %reshape.241), calls=%async_computation.1 | async-start | bytes 32768 | tf_op jit(solution)/shard_map/all_to_all | solution.py:175
  59.2 6.9 %all-to-all-done.1 = f32[32,1,128]{2,1,0:T(1,128)S(1)} async-done(((f32[32,1,128]{2,1,0:T(1,128)}), f32[32,1,128]{2,1,0:T(1,128)S(1)}, u32[]{:S(2)}, u32[]{:S(2)}) %all-to-all-start.1) | async-done | bytes 16416 | tf_op jit(solution)/shard_map/all_to_all | solution.py:175
  66.9 2.0 %scatter_custom_fusion = f32[16,4096]{0,1:T(8,128)S(1)} fusion(s32[256]{0:T(256)S(1)} %bitcast.182, f32[]{:T(128)} %constant.15.clone.1, f32[32,8]{1,0:T(8,128)S(1)} %copy.26, f32[32,8,16]{2,1,0:T(8,128)S(1)} %reshape.242), kind=kCustom, calls=%fused_computation.26 | custom fusion | flops 8192 | bytes 409604 | tf_op jit(solution)/shard_map/scatter-add | solution.py:178
  69.6 1.1 multiply_bitcast_fusion
  71.3 1.7 %fusion.107 = (f32[1,16,42,138]{3,2,1,0:T(8,128)S(1)}, f32[1,16,42,138]{3,2,1,0:T(8,128)S(1)}) fusion(f32[16,44,140]{2,1,0:T(8,128)S(1)} %get-tuple-element.20, f32[16,44,140]{2,1,0:T(8,128)S(1)} %get-tuple-element.21, f32[42,138]{1,0:T(8,128)S(1)} %get-tuple-element.34, f32[42,138]{1,0:T(8,128)S(1)} %get-tuple-element.36, ...), kind=kLoop, calls=%fused_computation.167 | loop fusion | flops 2596608 | bytes 4590432 | tf_op jit(solution)/shard_map/stack | solution.py:53
  73.7 1.7 %fusion.87 = (f32[1,16,42,138]{3,2,1,0:T(8,128)S(1)}, f32[1,16,42,138]{3,2,1,0:T(8,128)S(1)}) fusion(f32[16,44,140]{2,1,0:T(8,128)S(1)} %get-tuple-element.18, f32[16,44,140]{2,1,0:T(8,128)S(1)} %get-tuple-element.19, f32[42,138]{1,0:T(8,128)S(1)} %get-tuple-element.34, f32[42,138]{1,0:T(8,128)S(1)} %get-tuple-element.36, ...), kind=kLoop, calls=%fused_computation.137 | loop fusion | flops 2596608 | bytes 4590432 | tf_op jit(solution)/shard_map/stack | solution.py:53
  76.0 1.7 %fusion.67 = (f32[1,16,42,138]{3,2,1,0:T(8,128)S(1)}, f32[1,16,42,138]{3,2,1,0:T(8,128)S(1)}) fusion(f32[16,44,140]{2,1,0:T(8,128)S(1)} %get-tuple-element.16, f32[16,44,140]{2,1,0:T(8,128)S(1)} %get-tuple-element.17, f32[42,138]{1,0:T(8,128)S(1)} %get-tuple-element.34, f32[42,138]{1,0:T(8,128)S(1)} %get-tuple-element.36, ...), kind=kLoop, calls=%fused_computation.107 | loop fusion | flops 2596608 | bytes 4590432 | tf_op jit(solution)/shard_map/stack | solution.py:53
  78.4 1.7 %fusion.47 = (f32[1,16,42,138]{3,2,1,0:T(8,128)S(1)}, f32[1,16,42,138]{3,2,1,0:T(8,128)S(1)}) fusion(f32[16,44,140]{2,1,0:T(8,128)S(1)} %get-tuple-element.14, f32[16,44,140]{2,1,0:T(8,128)S(1)} %get-tuple-element.15, f32[42,138]{1,0:T(8,128)S(1)} %get-tuple-element.34, f32[42,138]{1,0:T(8,128)S(1)} %get-tuple-element.36, ...), kind=kLoop, calls=%fused_computation.77 | loop fusion | flops 2596608 | bytes 4590432 | tf_op jit(solution)/shard_map/stack | solution.py:53
  80.7 2.1 %fusion.118 = f32[16,44,32]{1,2,0:T(8,128)S(1)} fusion(f32[16,44,140]{2,1,0:T(8,128)S(1)} %fusion.25, f32[44,140]{1,0:T(8,128)S(1)} %get-tuple-element.58, f32[44,140]{1,0:T(8,128)S(1)} %get-tuple-element.56, f32[44,140]{1,0:T(8,128)S(1)} %get-tuple-element.57, f32[44,140]{1,0:T(8,128)S(1)} %get-tuple-element.55, f32[44,140]{1,0:T(8,128)S(1)} %get-tuple-element.49, ...), kind=kOutput, calls=%fused_computation.187 | convolution fusion | flops 39038720 | bytes 625728 | tf_op jit(solution)/shard_map/rxy,yb->rxb/dot_general | solution.py:192
  83.5 11.3 %all_to_all.20 = f32[32,8,128]{2,1,0:T(8,128)S(1)} all-to-all(f32[32,8,128]{2,1,0:T(8,128)S(1)} %reshape_reshape.6), channel_id=1, replica_groups=mesh['gx'=32,'gy'=16] {'gx'}, dimensions={0} | all-to-all | bytes 262144 | tf_op jit(solution)/shard_map/all_to_all | solution.py:104
  94.9 3.5 %collective-permute-start.4 = (f32[8,128]{1,0:T(8,128)S(1)}, f32[8,128]{1,0:T(8,128)S(1)}, u32[]{:S(2)}, u32[]{:S(2)}) collective-permute-start(f32[8,128]{1,0:T(8,128)S(1)} %reduce_sum.9), channel_id=1, source_target_pairs={{0,1},{1,0},{2,3},{3,2},{4,5},{5,4},{6,7},{7,6},{8,9},{9,8},{10,11... | collective-permute-start | bytes 12296 | tf_op jit(solution)/shard_map/ppermute | solution.py:96
  98.5 1.0 collective-permute-done.4
  99.5 7.3 %collective-permute-start.5 = (f32[8,128]{1,0:T(8,128)S(1)}, f32[8,128]{1,0:T(8,128)S(1)}, u32[]{:S(2)}, u32[]{:S(2)}) collective-permute-start(f32[8,128]{1,0:T(8,128)S(1)} %add.551), channel_id=1, source_target_pairs={{0,2},{1,3},{2,0},{3,1},{4,6},{5,7},{6,4},{7,5},{8,10},{9,11},{10,... | collective-permute-start | bytes 12296 | tf_op jit(solution)/shard_map/ppermute | solution.py:96
  106.8 1.0 collective-permute-done.5
  107.8 8.8 %collective-permute-start.6 = (f32[8,128]{1,0:T(8,128)S(1)}, f32[8,128]{1,0:T(8,128)S(1)}, u32[]{:S(2)}, u32[]{:S(2)}) collective-permute-start(f32[8,128]{1,0:T(8,128)S(1)} %add.552), channel_id=1, source_target_pairs={{0,4},{1,5},{2,6},{3,7},{4,0},{5,1},{6,2},{7,3},{8,12},{9,13},{10,... | collective-permute-start | bytes 12296 | tf_op jit(solution)/shard_map/ppermute | solution.py:96
  116.6 1.0 collective-permute-done.6
  117.5 9.8 %collective-permute-start.7 = (f32[8,128]{1,0:T(8,128)S(1)}, f32[8,128]{1,0:T(8,128)S(1)}, u32[]{:S(2)}, u32[]{:S(2)}) collective-permute-start(f32[8,128]{1,0:T(8,128)S(1)} %add.553), channel_id=1, source_target_pairs={{0,8},{1,9},{2,10},{3,11},{4,12},{5,13},{6,14},{7,15},{8,0},{9,1},... | collective-permute-start | bytes 12296 | tf_op jit(solution)/shard_map/ppermute | solution.py:96
  127.4 3.2 %collective-permute-done.7 = f32[8,128]{1,0:T(8,128)S(1)} collective-permute-done((f32[8,128]{1,0:T(8,128)S(1)}, f32[8,128]{1,0:T(8,128)S(1)}, u32[]{:S(2)}, u32[]{:S(2)}) %collective-permute-start.7) | collective-permute-done | bytes 4128 | tf_op jit(solution)/shard_map/ppermute | solution.py:96
  131.3 7.7 %all-to-all-start.3 = ((f32[32,8,128]{2,1,0:T(8,128)}), f32[32,8,128]{2,1,0:T(8,128)S(1)}, u32[]{:S(2)}, u32[]{:S(2)}) async-start(f32[32,8,128]{2,1,0:T(8,128)} %broadcast_in_dim.14), calls=%async_computation.3 | async-start | bytes 262144 | tf_op jit(solution)/shard_map/all_to_all | solution.py:107
  139.2 7.5 %all-to-all-done.3 = f32[32,8,128]{2,1,0:T(8,128)S(1)} async-done(((f32[32,8,128]{2,1,0:T(8,128)}), f32[32,8,128]{2,1,0:T(8,128)S(1)}, u32[]{:S(2)}, u32[]{:S(2)}) %all-to-all-start.3) | async-done | bytes 131104 | tf_op jit(solution)/shard_map/all_to_all | solution.py:107
  (121 shorter events, 25.6 us)
Async XLA Ops:
  0.6 23.8 %copy-start.4 = (f32[32,128]{1,0:T(8,128)S(1)}, f32[32,128]{1,0:T(8,128)}, u32[]{:S(2)}) copy-start(f32[32,128]{1,0:T(8,128)} %param.11) | copy-start | bytes 49156
  0.6 23.8 %copy-start.3 = (f32[32,128]{1,0:T(8,128)S(1)}, f32[32,128]{1,0:T(8,128)}, u32[]{:S(2)}) copy-start(f32[32,128]{1,0:T(8,128)} %param.12) | copy-start | bytes 49156
  0.7 23.8 %copy-start.1 = (f32[32,128]{1,0:T(8,128)S(1)}, f32[32,128]{1,0:T(8,128)}, u32[]{:S(2)}) copy-start(f32[32,128]{1,0:T(8,128)} %param.13) | copy-start | bytes 49156
  0.7 20.5 %copy-start = (f32[16,64,32]{1,2,0:T(8,128)S(1)}, f32[16,64,32]{1,2,0:T(8,128)}, u32[]{:S(2)}) copy-start(f32[16,64,32]{1,2,0:T(8,128)} %param.16) | copy-start | bytes 393220
  2.3 14.6 %collective-permute-start = (f32[4032]{0:T(1024)S(1)}, f32[4032]{0:T(1024)S(1)}, u32[]{:S(2)}, u32[]{:S(2)}) collective-permute-start(f32[4032]{0:T(1024)S(1)} %pad_maximum_fusion.12), channel_id=1, source_target_pairs={{0,16},{16,32},{32,48},{48,64},{64,80},{80,96},{96,112},{112,128},... | collective-permute-start | bytes 48392 | tf_op jit(solution)/shard_map/ppermute | solution.py:85
  6.9 10.0 %collective-permute-start.1 = (f32[4032]{0:T(1024)S(1)}, f32[4032]{0:T(1024)S(1)}, u32[]{:S(2)}, u32[]{:S(2)}) collective-permute-start(f32[4032]{0:T(1024)S(1)} %pad_maximum_fusion.13), channel_id=1, source_target_pairs={{16,0},{32,16},{48,32},{64,48},{80,64},{96,80},{112,96},{128,112},... | collective-permute-start | bytes 48392 | tf_op jit(solution)/shard_map/ppermute | solution.py:86
  18.1 4.1 %collective-permute-start.2 = (f32[1512]{0:T(1024)S(1)}, f32[1512]{0:T(1024)S(1)}, u32[]{:S(2)}, u32[]{:S(2)}) collective-permute-start(f32[1512]{0:T(1024)S(1)} %pad_maximum_fusion.14), channel_id=1, source_target_pairs={{0,1},{1,2},{2,3},{3,4},{4,5},{5,6},{6,7},{7,8},{8,9},{9,10},{10,1... | collective-permute-start | bytes 18152 | tf_op jit(solution)/shard_map/ppermute | solution.py:85
  19.7 4.5 %collective-permute-start.3 = (f32[1512]{0:T(1024)S(1)}, f32[1512]{0:T(1024)S(1)}, u32[]{:S(2)}, u32[]{:S(2)}) collective-permute-start(f32[1512]{0:T(1024)S(1)} %pad_maximum_fusion.15), channel_id=1, source_target_pairs={{1,0},{2,1},{3,2},{4,3},{5,4},{6,5},{7,6},{8,7},{9,8},{10,9},{11,1... | collective-permute-start | bytes 18152 | tf_op jit(solution)/shard_map/ppermute | solution.py:86
  25.0 1.4 copy-start.2
  35.6 18.4 %copy-start.7 = (f32[1,1,40]{2,1,0:T(1,128)S(1)}, f32[1,1,40]{2,1,0:T(1,128)}, u32[]{:S(2)}) copy-start(f32[1,1,40]{2,1,0:T(1,128)} %param.21) | copy-start | bytes 484
  37.8 14.6 %all-to-all-start = ((f32[32,1,128]{2,1,0:T(1,128)}), f32[32,1,128]{2,1,0:T(1,128)S(1)}, u32[]{:S(2)}, u32[]{:S(2)}) async-start(f32[32,1,128]{2,1,0:T(1,128)} %reshape.239), calls=%async_computation | async-start | bytes 32768 | tf_op jit(solution)/shard_map/all_to_all | solution.py:169
  54.0 15.6 %copy-start.6 = (f32[16,40]{1,0:T(8,128)}, f32[16,40]{1,0:T(8,128)S(1)}, u32[]{:S(2)}) copy-start(f32[16,40]{1,0:T(8,128)S(1)} %fusion.226) | copy-start | bytes 7684
  55.0 11.1 %all-to-all-start.1 = ((f32[32,1,128]{2,1,0:T(1,128)}), f32[32,1,128]{2,1,0:T(1,128)S(1)}, u32[]{:S(2)}, u32[]{:S(2)}) async-start(f32[32,1,128]{2,1,0:T(1,128)} %reshape.241), calls=%async_computation.1 | async-start | bytes 32768 | tf_op jit(solution)/shard_map/all_to_all | solution.py:175
  80.7 2.1 %copy-start.5 = (f32[32,64]{1,0:T(8,128)S(1)}, f32[32,64]{1,0:T(8,128)}, u32[]{:S(2)}) copy-start(f32[32,64]{1,0:T(8,128)} %param.14) | copy-start | bytes 24580
  94.9 4.5 %collective-permute-start.4 = (f32[8,128]{1,0:T(8,128)S(1)}, f32[8,128]{1,0:T(8,128)S(1)}, u32[]{:S(2)}, u32[]{:S(2)}) collective-permute-start(f32[8,128]{1,0:T(8,128)S(1)} %reduce_sum.9), channel_id=1, source_target_pairs={{0,1},{1,0},{2,3},{3,2},{4,5},{5,4},{6,7},{7,6},{8,9},{9,8},{10,11... | collective-permute-start | bytes 12296 | tf_op jit(solution)/shard_map/ppermute | solution.py:96
  99.5 8.3 %collective-permute-start.5 = (f32[8,128]{1,0:T(8,128)S(1)}, f32[8,128]{1,0:T(8,128)S(1)}, u32[]{:S(2)}, u32[]{:S(2)}) collective-permute-start(f32[8,128]{1,0:T(8,128)S(1)} %add.551), channel_id=1, source_target_pairs={{0,2},{1,3},{2,0},{3,1},{4,6},{5,7},{6,4},{7,5},{8,10},{9,11},{10,... | collective-permute-start | bytes 12296 | tf_op jit(solution)/shard_map/ppermute | solution.py:96
  107.8 9.8 %collective-permute-start.6 = (f32[8,128]{1,0:T(8,128)S(1)}, f32[8,128]{1,0:T(8,128)S(1)}, u32[]{:S(2)}, u32[]{:S(2)}) collective-permute-start(f32[8,128]{1,0:T(8,128)S(1)} %add.552), channel_id=1, source_target_pairs={{0,4},{1,5},{2,6},{3,7},{4,0},{5,1},{6,2},{7,3},{8,12},{9,13},{10,... | collective-permute-start | bytes 12296 | tf_op jit(solution)/shard_map/ppermute | solution.py:96
  117.5 13.1 %collective-permute-start.7 = (f32[8,128]{1,0:T(8,128)S(1)}, f32[8,128]{1,0:T(8,128)S(1)}, u32[]{:S(2)}, u32[]{:S(2)}) collective-permute-start(f32[8,128]{1,0:T(8,128)S(1)} %add.553), channel_id=1, source_target_pairs={{0,8},{1,9},{2,10},{3,11},{4,12},{5,13},{6,14},{7,15},{8,0},{9,1},... | collective-permute-start | bytes 12296 | tf_op jit(solution)/shard_map/ppermute | solution.py:96
  131.3 15.4 %all-to-all-start.3 = ((f32[32,8,128]{2,1,0:T(8,128)}), f32[32,8,128]{2,1,0:T(8,128)S(1)}, u32[]{:S(2)}, u32[]{:S(2)}) async-start(f32[32,8,128]{2,1,0:T(8,128)} %broadcast_in_dim.14), calls=%async_computation.3 | async-start | bytes 262144 | tf_op jit(solution)/shard_map/all_to_all | solution.py:107

commit v3 on v2

--- a/solution.py
+++ b/solution.py
@@ -66,7 +66,46 @@
     return extended(state_now, (("gx", 2), ("gy", 3)), 1)
 
 
-def exchange(parts, axis, width):
+def all_sum(values):
+    count = lax.axis_size("gx")
+    rows = lax.axis_size("gy")
+    flat = values.reshape(count, -1, 128)
+    part = lax.all_to_all(flat, "gx", 0, 0, tiled=True).sum(0)
+    copies = jnp.broadcast_to(part[None], (rows,) + part.shape)
+    part = lax.all_to_all(copies, "gy", 0, 0, tiled=True).sum(0)
+    spread_out = jnp.broadcast_to(part[None], (count,) + part.shape)
+    return lax.all_to_all(spread_out, "gx", 0, 0, tiled=True).reshape(values.shape)
+
+
+def halo_round(static, rows, cols, width):
+    n_gx = lax.axis_size("gx")
+    n_gy = lax.axis_size("gy")
+    w = width
+
+    def corner(block, step_x, step_y):
+        pairs = []
+        for a in range(n_gx):
+            for b in range(n_gy):
+                if 0 <= a + step_x < n_gx and 0 <= b + step_y < n_gy:
+                    pairs.append((a * n_gy + b, (a + step_x) * n_gy + b + step_y))
+        return lax.ppermute(block, ("gx", "gy"), pairs)
+
+    (_, up, down), (row_up, row_down) = edge_pair(((static, 1), (rows, 0)), "gx", w)
+    (_, left, right), (col_left, col_right) = edge_pair(((static, 2), (cols, 0)), "gy", w)
+    up_left = corner(static[:, -w:, -w:], 1, 1)
+    up_right = corner(static[:, -w:, :w], 1, -1)
+    down_left = corner(static[:, :w, -w:], -1, 1)
+    down_right = corner(static[:, :w, :w], -1, -1)
+    top = jnp.concatenate([up_left, up, up_right], axis=2)
+    middle = jnp.concatenate([left, static, right], axis=2)
+    bottom = jnp.concatenate([down_left, down, down_right], axis=2)
+    wide = jnp.concatenate([top, middle, bottom], axis=1)
+    rows_wide = jnp.concatenate([row_up, rows, row_down], axis=0)
+    cols_wide = jnp.concatenate([col_left, cols, col_right], axis=0)
+    return wide, rows_wide, cols_wide
+
+
+def edge_pair(parts, axis, width):
     count = lax.axis_size(axis)
     ends = count - 1
     heads = [lax.slice_in_dim(a, 0, width, axis=d) for a, d in parts]
@@ -84,27 +123,7 @@
 
     from_prev = unpack(lax.ppermute(pack(tails), axis, [(i, i + 1) for i in range(ends)]), tails)
     from_next = unpack(lax.ppermute(pack(heads), axis, [(i + 1, i) for i in range(ends)]), heads)
-    return [
-        jnp.concatenate([p, a, n], axis=d) for (a, d), p, n in zip(parts, from_prev, from_next)
-    ]
-
-
-def butterfly(values, axis):
-    count = lax.axis_size(axis)
-    stride = 1
-    while stride < count:
-        values = values + lax.ppermute(values, axis, [(i, i ^ stride) for i in range(count)])
-        stride *= 2
-    return values
-
-
-def all_sum(values):
-    count = lax.axis_size("gx")
-    flat = values.reshape(count, -1, 128)
-    part = lax.all_to_all(flat, "gx", 0, 0, tiled=True).sum(0)
-    part = butterfly(part, "gy")
-    spread_out = jnp.broadcast_to(part[None], (count,) + part.shape)
-    return lax.all_to_all(spread_out, "gx", 0, 0, tiled=True).reshape(values.shape)
+    return (None, from_prev[0], from_next[0]), (from_prev[1], from_next[1])
 
 
 def pad_sides(field, width):
@@ -129,8 +148,7 @@
     height, breadth = diffusivity.shape
     n_dirs = directions.shape[0]
     static = jnp.stack([diffusivity, base_humidity, coupling, jnp.ones_like(diffusivity)])
-    static_gx, rows_wide = exchange(((static, 1), (basis_rows, 0)), "gx", reach)
-    static_wide, cols_wide = exchange(((static_gx, 2), (basis_cols, 0)), "gy", reach)
+    static_wide, rows_wide, cols_wide = halo_round(static, basis_rows, basis_cols, reach)
     static_six = window(static_wide, reach, rim_depth)
     rows_six = rows_wide[1:-1]
     cols_six = cols_wide[1:-1]

time: 149 us -> 156 us (1.047)
  blocking collectives: 11.3 us -> 38.7 us
  starting transfers between devices: 61.5 us -> 44.8 us
  waiting for transfers between devices: 29.1 us -> 26.5 us
    all_to_all x0 -> x1, blocking collectives: none -> 27.4 us  [all_sum(): part = lax.all_to_all(copies, 'gy', 0, 0, tiled=True).sum(0)]
    ppermute x8, starting transfers between devices: 42 us -> 24.1 us  [the longest x4 11.5 us: corner(): return lax.ppermute(block, ('gx', 'gy'), pairs)]
    all_to_all x1, starting transfers between devices: 7.65 us -> 10.9 us  [local(): lax.all_to_all(picked, 'gx', split_axis=1, concat_axis=1, tiled=True)]
    ppermute x8, waiting for transfers between devices: 7.94 us -> 5.28 us  [the longest x4 5.27 us: corner(): return lax.ppermute(block, ('gx', 'gy'), pairs)]
    all_to_all x1, starting transfers between devices: 7.68 us -> 5.71 us  [all_sum(): lax.all_to_all(spread_out, 'gx', 0, 0, tiled=True).reshape(values.shape)]
    unnamed x24 -> x20, local copies, waits for them, and re-layouts: 4.3 us -> 4.28 us
  transfers between devices with their start and end apart: 11 -> 11, of which waited for: 8 -> 4; matrix products, arithmetic and copies ran while one was open for 5% -> 4% of each run, Pallas kernels for 0% -> 0%
where the time goes in v3:
time: 156 us; the launch traced here: 155 us
  starting transfers between devices  44.8 us (29%)
  blocking collectives  38.7 us (25%)
  waiting for transfers between devices  26.5 us (17%)
  other arithmetic  25.9 us (17%)
  local copies, waits for them, and re-layouts  13.5 us (9%)
  matrix products  4.29 us (3%)
    all_to_all x1, blocking collectives, all_sum(): part = lax.all_to_all(copies, 'gy', 0, 0, tiled=True).sum(0)  27.4 us
    ppermute x4, starting transfers between devices, corner(): return lax.ppermute(block, ('gx', 'gy'), pairs)  11.5 us
    all_to_all x1, blocking collectives, all_sum(): part = lax.all_to_all(flat, 'gx', 0, 0, tiled=True).sum(0)  11.3 us
    all_to_all x1, starting transfers between devices, local(): lax.all_to_all(picked, 'gx', split_axis=1, concat_axis=1, tiled=True)  10.9 us
    another operation x9, other arithmetic, advance(): return jnp.stack([new_temp * inside, new_hum * inside])  10 us
    ppermute x2, starting transfers between devices, edge_pair(): lax.ppermute(pack(tails), axis, [(i, i + 1) for i in range(ends)])  8.31 us
    all_to_all x1, waiting for transfers between devices, all_sum(): lax.all_to_all(spread_out, 'gx', 0, 0, tiled=True).reshape(values.shape)  7.5 us
    all_to_all x1, waiting for transfers between devices, local(): lax.all_to_all(backward, 'gx', split_axis=1, concat_axis=1, tiled=True)  6.91 us
  transfers between devices with their start and end apart: 11, of which 4 were waited for; matrix products, arithmetic and copies ran while one was open for 4% of the time, Pallas kernels for 0%

profile of v3, /device:TPU:1, one launch (start us, length us, event | category | flops | bytes accessed | tf_op | source)
XLA Modules:
  0.0 155.0 jit_solution(17068614816286874620)
XLA Ops:
  2.7 4.4 %collective-permute-start.3 = (f32[1120]{0:T(1024)S(1)}, f32[1120]{0:T(1024)S(1)}, u32[]{:S(2)}, u32[]{:S(2)}) collective-permute-start(f32[1120]{0:T(1024)S(1)} %pad_maximum_fusion.9), channel_id=1, source_target_pairs={{0,1},{1,2},{2,3},{3,4},{4,5},{5,6},{6,7},{7,8},{8,9},{9,10},{10,1... | collective-permute-start | bytes 13448 | tf_op jit(solution)/shard_map/ppermute | solution.py:124
  7.5 1.3 collective-permute-start.4
  9.6 3.9 %collective-permute-start.1 = (f32[4032]{0:T(1024)S(1)}, f32[4032]{0:T(1024)S(1)}, u32[]{:S(2)}, u32[]{:S(2)}) collective-permute-start(f32[4032]{0:T(1024)S(1)} %pad_maximum_fusion.7), channel_id=1, source_target_pairs={{0,16},{16,32},{32,48},{48,64},{64,80},{80,96},{96,112},{112,128},... | collective-permute-start | bytes 48392 | tf_op jit(solution)/shard_map/ppermute | solution.py:124
  13.6 3.0 %collective-permute-start.6 = (f32[4032]{0:T(1024)S(1)}, f32[4032]{0:T(1024)S(1)}, u32[]{:S(2)}, u32[]{:S(2)}) collective-permute-start(f32[4032]{0:T(1024)S(1)} %pad_maximum_fusion.8), channel_id=1, source_target_pairs={{16,0},{32,16},{48,32},{64,48},{80,64},{96,80},{112,96},{128,112},... | collective-permute-start | bytes 48392 | tf_op jit(solution)/shard_map/ppermute | solution.py:125
  16.7 4.6 %collective-permute-start = (f32[4,7,7]{2,1,0:T(8,128)S(1)}, f32[4,7,7]{2,1,0:T(8,128)S(1)}, u32[]{:S(2)}, u32[]{:S(2)}) collective-permute-start(f32[4,7,7]{2,1,0:T(8,128)S(1)} %get-tuple-element.53), channel_id=1, source_target_pairs={{0,17},{1,18},{2,19},{3,20},{4,21},{5,22},{6,23},{7,24},{8,25},{9,... | collective-permute-start | bytes 2360 | tf_op jit(solution)/shard_map/ppermute | solution.py:91
  24.6 1.3 collective-permute-start.2
  26.2 4.3 %collective-permute-start.5 = (f32[4,7,7]{2,1,0:T(8,128)S(1)}, f32[4,7,7]{2,1,0:T(8,128)S(1)}, u32[]{:S(2)}, u32[]{:S(2)}) collective-permute-start(f32[4,7,7]{2,1,0:T(8,128)S(1)} %get-tuple-element.54), channel_id=1, source_target_pairs={{16,1},{17,2},{18,3},{19,4},{20,5},{21,6},{22,7},{23,8},{24,9},{25... | collective-permute-start | bytes 2360 | tf_op jit(solution)/shard_map/ppermute | solution.py:91
  30.5 1.3 collective-permute-start.7
  32.4 5.3 %collective-permute-done.7 = f32[4,7,7]{2,1,0:T(8,128)S(1)} collective-permute-done((f32[4,7,7]{2,1,0:T(8,128)S(1)}, f32[4,7,7]{2,1,0:T(8,128)S(1)}, u32[]{:S(2)}, u32[]{:S(2)}) %collective-permute-start.7) | collective-permute-done | bytes 816 | tf_op jit(solution)/shard_map/ppermute | solution.py:91
  37.6 0.9 maximum_maximum_fusion
  40.5 0.9 convolution_multiply_fusion
  41.3 0.9 broadcast_multiply_fusion
  42.3 0.9 multiply_multiply_fusion
  43.2 1.6 %fusion.164 = (f32[16,38,134]{2,1,0:T(8,128)S(1)}, f32[16,38,134]{2,1,0:T(8,128)S(1)}) fusion(f32[16,40,136]{2,1,0:T(8,128)S(1)} %get-tuple-element.28, f32[16,40,136]{2,1,0:T(8,128)S(1)} %get-tuple-element.29, f32[38,134]{1,0:T(8,128)S(1)} %get-tuple-element.46, f32[38,134]{1,0:T(8,128)S(1)} %get-tuple-element.47, f32[16,42,138]{2,1,0:T(8,128)S(1)} %get-tuple-element.7, ...), kind=kLoop, calls=%fused_computation.248 | loop fusion | flops 2444160 | bytes 4358752 | tf_op jit(solution)/shard_map/mul | solution.py:53
  44.8 1.6 %fusion.145 = (f32[16,36,132]{2,1,0:T(8,128)S(1)}, f32[16,36,132]{2,1,0:T(8,128)S(1)}) fusion(f32[16,38,134]{2,1,0:T(8,128)S(1)} %get-tuple-element.26, f32[16,38,134]{2,1,0:T(8,128)S(1)} %get-tuple-element.27, f32[36,132]{1,0:T(8,128)S(1)} %get-tuple-element.43, f32[36,132]{1,0:T(8,128)S(1)} %get-tuple-element.44, f32[16,42,138]{2,1,0:T(8,128)S(1)} %get-tuple-element.7, ...), kind=kLoop, calls=%fused_computation.220 | loop fusion | flops 2280960 | bytes 4067712 | tf_op jit(solution)/shard_map/mul | solution.py:53
  47.2 1.6 %fusion.140 = (f32[16,34,130]{2,1,0:T(8,128)S(1)}, f32[16,34,130]{2,1,0:T(8,128)S(1)}, f32[16,34,130]{2,1,0:T(8,128)S(1)}, f32[16,34,130]{2,1,0:T(8,128)S(1)}) fusion(f32[16,42,138]{2,1,0:T(8,128)S(1)} %get-tuple-element.7, f32[16,36,132]{2,1,0:T(8,128)S(1)} %get-tuple-element.25, f32[34,130]{1,0:T(8,128)S(1)} %get-tuple-element.40, ...), kind=kLoop, calls=%fused_computation.214 | loop fusion | flops 1555840 | bytes 4349280 | tf_op jit(solution)/shard_map/add | solution.py:165
  51.9 10.9 %all-to-all-start = ((f32[32,1,128]{2,1,0:T(1,128)}), f32[32,1,128]{2,1,0:T(1,128)S(1)}, u32[]{:S(2)}, u32[]{:S(2)}) async-start(f32[32,1,128]{2,1,0:T(1,128)} %reshape.272), calls=%async_computation | async-start | bytes 32768 | tf_op jit(solution)/shard_map/all_to_all | solution.py:187
  62.9 6.8 %all-to-all-done = f32[32,1,128]{2,1,0:T(1,128)S(1)} async-done(((f32[32,1,128]{2,1,0:T(1,128)}), f32[32,1,128]{2,1,0:T(1,128)S(1)}, u32[]{:S(2)}, u32[]{:S(2)}) %all-to-all-start) | async-done | bytes 16416 | tf_op jit(solution)/shard_map/all_to_all | solution.py:187
  72.3 4.1 %all-to-all-start.1 = ((f32[32,1,128]{2,1,0:T(1,128)}), f32[32,1,128]{2,1,0:T(1,128)S(1)}, u32[]{:S(2)}, u32[]{:S(2)}) async-start(f32[32,1,128]{2,1,0:T(1,128)} %reshape.274), calls=%async_computation.1 | async-start | bytes 32768 | tf_op jit(solution)/shard_map/all_to_all | solution.py:193
  76.6 6.9 %all-to-all-done.1 = f32[32,1,128]{2,1,0:T(1,128)S(1)} async-done(((f32[32,1,128]{2,1,0:T(1,128)}), f32[32,1,128]{2,1,0:T(1,128)S(1)}, u32[]{:S(2)}, u32[]{:S(2)}) %all-to-all-start.1) | async-done | bytes 16416 | tf_op jit(solution)/shard_map/all_to_all | solution.py:193
  84.3 2.0 %scatter_custom_fusion = f32[16,4096]{0,1:T(8,128)S(1)} fusion(s32[256]{0:T(256)S(1)} %bitcast.175, f32[]{:T(128)} %constant.15.clone.1, f32[32,8]{1,0:T(8,128)S(1)} %copy.40, f32[32,8,16]{2,1,0:T(8,128)S(1)} %reshape.275), kind=kCustom, calls=%fused_computation.26 | custom fusion | flops 8192 | bytes 409604 | tf_op jit(solution)/shard_map/scatter-add | solution.py:196
  87.0 1.1 multiply_bitcast_fusion
  88.7 1.7 %fusion.107 = (f32[1,16,42,138]{3,2,1,0:T(8,128)S(1)}, f32[1,16,42,138]{3,2,1,0:T(8,128)S(1)}) fusion(f32[16,44,140]{2,1,0:T(8,128)S(1)} %get-tuple-element.22, f32[16,44,140]{2,1,0:T(8,128)S(1)} %get-tuple-element.23, f32[42,138]{1,0:T(8,128)S(1)} %get-tuple-element.36, f32[42,138]{1,0:T(8,128)S(1)} %get-tuple-element.38, ...), kind=kLoop, calls=%fused_computation.167 | loop fusion | flops 2596608 | bytes 4590432 | tf_op jit(solution)/shard_map/stack | solution.py:53
  91.1 1.7 %fusion.87 = (f32[1,16,42,138]{3,2,1,0:T(8,128)S(1)}, f32[1,16,42,138]{3,2,1,0:T(8,128)S(1)}) fusion(f32[16,44,140]{2,1,0:T(8,128)S(1)} %get-tuple-element.20, f32[16,44,140]{2,1,0:T(8,128)S(1)} %get-tuple-element.21, f32[42,138]{1,0:T(8,128)S(1)} %get-tuple-element.36, f32[42,138]{1,0:T(8,128)S(1)} %get-tuple-element.38, ...), kind=kLoop, calls=%fused_computation.137 | loop fusion | flops 2596608 | bytes 4590432 | tf_op jit(solution)/shard_map/stack | solution.py:53
  93.4 1.7 %fusion.67 = (f32[1,16,42,138]{3,2,1,0:T(8,128)S(1)}, f32[1,16,42,138]{3,2,1,0:T(8,128)S(1)}) fusion(f32[16,44,140]{2,1,0:T(8,128)S(1)} %get-tuple-element.18, f32[16,44,140]{2,1,0:T(8,128)S(1)} %get-tuple-element.19, f32[42,138]{1,0:T(8,128)S(1)} %get-tuple-element.36, f32[42,138]{1,0:T(8,128)S(1)} %get-tuple-element.38, ...), kind=kLoop, calls=%fused_computation.107 | loop fusion | flops 2596608 | bytes 4590432 | tf_op jit(solution)/shard_map/stack | solution.py:53
  95.8 1.7 %fusion.47 = (f32[1,16,42,138]{3,2,1,0:T(8,128)S(1)}, f32[1,16,42,138]{3,2,1,0:T(8,128)S(1)}) fusion(f32[16,44,140]{2,1,0:T(8,128)S(1)} %get-tuple-element.16, f32[16,44,140]{2,1,0:T(8,128)S(1)} %get-tuple-element.17, f32[42,138]{1,0:T(8,128)S(1)} %get-tuple-element.36, f32[42,138]{1,0:T(8,128)S(1)} %get-tuple-element.38, ...), kind=kLoop, calls=%fused_computation.77 | loop fusion | flops 2596608 | bytes 4590432 | tf_op jit(solution)/shard_map/stack | solution.py:53
  98.1 2.1 %fusion.118 = f32[16,44,32]{1,2,0:T(8,128)S(1)} fusion(f32[16,44,140]{2,1,0:T(8,128)S(1)} %fusion.25, f32[44,140]{1,0:T(8,128)S(1)} %get-tuple-element.64, f32[44,140]{1,0:T(8,128)S(1)} %get-tuple-element.62, f32[44,140]{1,0:T(8,128)S(1)} %get-tuple-element.63, f32[44,140]{1,0:T(8,128)S(1)} %get-tuple-element.61, f32[44,140]{1,0:T(8,128)S(1)} %get-tuple-element.51, ...), kind=kOutput, calls=%fused_computation.187 | convolution fusion | flops 39038720 | bytes 625728 | tf_op jit(solution)/shard_map/rxy,yb->rxb/dot_general | solution.py:210
  100.9 11.3 %all_to_all.25 = f32[32,8,128]{2,1,0:T(8,128)S(1)} all-to-all(f32[32,8,128]{2,1,0:T(8,128)S(1)} %reshape_reshape.6), channel_id=1, replica_groups=mesh['gx'=32,'gy'=16] {'gx'}, dimensions={0} | all-to-all | bytes 262144 | tf_op jit(solution)/shard_map/all_to_all | solution.py:73
  112.3 27.4 %all_to_all.26 = f32[16,8,128]{2,1,0:T(8,128)S(1)} all-to-all(f32[16,8,128]{2,1,0:T(8,128)S(1)} %broadcast_in_dim.16), channel_id=1, replica_groups=mesh['gx'=32,'gy'=16] {'gy'}, dimensions={0} | all-to-all | bytes 131072 | tf_op jit(solution)/shard_map/all_to_all | solution.py:75
  140.4 5.7 %all-to-all-start.4 = ((f32[32,8,128]{2,1,0:T(8,128)}), f32[32,8,128]{2,1,0:T(8,128)S(1)}, u32[]{:S(2)}, u32[]{:S(2)}) async-start(f32[32,8,128]{2,1,0:T(8,128)} %broadcast_in_dim.17), calls=%async_computation.4 | async-start | bytes 262144 | tf_op jit(solution)/shard_map/all_to_all | solution.py:77
  146.3 7.5 %all-to-all-done.4 = f32[32,8,128]{2,1,0:T(8,128)S(1)} async-done(((f32[32,8,128]{2,1,0:T(8,128)}), f32[32,8,128]{2,1,0:T(8,128)S(1)}, u32[]{:S(2)}, u32[]{:S(2)}) %all-to-all-start.4) | async-done | bytes 131104 | tf_op jit(solution)/shard_map/all_to_all | solution.py:77
  154.1 0.9 copy.46
  (119 shorter events, 22.2 us)
Async XLA Ops:
  2.7 21.9 %collective-permute-start.3 = (f32[1120]{0:T(1024)S(1)}, f32[1120]{0:T(1024)S(1)}, u32[]{:S(2)}, u32[]{:S(2)}) collective-permute-start(f32[1120]{0:T(1024)S(1)} %pad_maximum_fusion.9), channel_id=1, source_target_pairs={{0,1},{1,2},{2,3},{3,4},{4,5},{5,6},{6,7},{7,8},{8,9},{9,10},{10,1... | collective-permute-start | bytes 13448 | tf_op jit(solution)/shard_map/ppermute | solution.py:124
  7.5 18.7 %collective-permute-start.4 = (f32[1120]{0:T(1024)S(1)}, f32[1120]{0:T(1024)S(1)}, u32[]{:S(2)}, u32[]{:S(2)}) collective-permute-start(f32[1120]{0:T(1024)S(1)} %pad_maximum_fusion.10), channel_id=1, source_target_pairs={{1,0},{2,1},{3,2},{4,3},{5,4},{6,5},{7,6},{8,7},{9,8},{10,9},{11,1... | collective-permute-start | bytes 13448 | tf_op jit(solution)/shard_map/ppermute | solution.py:125
  9.6 20.9 %collective-permute-start.1 = (f32[4032]{0:T(1024)S(1)}, f32[4032]{0:T(1024)S(1)}, u32[]{:S(2)}, u32[]{:S(2)}) collective-permute-start(f32[4032]{0:T(1024)S(1)} %pad_maximum_fusion.7), channel_id=1, source_target_pairs={{0,16},{16,32},{32,48},{48,64},{64,80},{80,96},{96,112},{112,128},... | collective-permute-start | bytes 48392 | tf_op jit(solution)/shard_map/ppermute | solution.py:124
  13.6 18.7 %collective-permute-start.6 = (f32[4032]{0:T(1024)S(1)}, f32[4032]{0:T(1024)S(1)}, u32[]{:S(2)}, u32[]{:S(2)}) collective-permute-start(f32[4032]{0:T(1024)S(1)} %pad_maximum_fusion.8), channel_id=1, source_target_pairs={{16,0},{32,16},{48,32},{64,48},{80,64},{96,80},{112,96},{128,112},... | collective-permute-start | bytes 48392 | tf_op jit(solution)/shard_map/ppermute | solution.py:125
  16.7 15.6 %collective-permute-start = (f32[4,7,7]{2,1,0:T(8,128)S(1)}, f32[4,7,7]{2,1,0:T(8,128)S(1)}, u32[]{:S(2)}, u32[]{:S(2)}) collective-permute-start(f32[4,7,7]{2,1,0:T(8,128)S(1)} %get-tuple-element.53), channel_id=1, source_target_pairs={{0,17},{1,18},{2,19},{3,20},{4,21},{5,22},{6,23},{7,24},{8,25},{9,... | collective-permute-start | bytes 2360 | tf_op jit(solution)/shard_map/ppermute | solution.py:91
  24.6 7.7 %collective-permute-start.2 = (f32[4,7,7]{2,1,0:T(8,128)S(1)}, f32[4,7,7]{2,1,0:T(8,128)S(1)}, u32[]{:S(2)}, u32[]{:S(2)}) collective-permute-start(f32[4,7,7]{2,1,0:T(8,128)S(1)} %get-tuple-element.56), channel_id=1, source_target_pairs={{1,16},{2,17},{3,18},{4,19},{5,20},{6,21},{7,22},{8,23},{9,24},{10... | collective-permute-start | bytes 2360 | tf_op jit(solution)/shard_map/ppermute | solution.py:91
  26.2 6.2 %collective-permute-start.5 = (f32[4,7,7]{2,1,0:T(8,128)S(1)}, f32[4,7,7]{2,1,0:T(8,128)S(1)}, u32[]{:S(2)}, u32[]{:S(2)}) collective-permute-start(f32[4,7,7]{2,1,0:T(8,128)S(1)} %get-tuple-element.54), channel_id=1, source_target_pairs={{16,1},{17,2},{18,3},{19,4},{20,5},{21,6},{22,7},{23,8},{24,9},{25... | collective-permute-start | bytes 2360 | tf_op jit(solution)/shard_map/ppermute | solution.py:91
  30.5 7.2 %collective-permute-start.7 = (f32[4,7,7]{2,1,0:T(8,128)S(1)}, f32[4,7,7]{2,1,0:T(8,128)S(1)}, u32[]{:S(2)}, u32[]{:S(2)}) collective-permute-start(f32[4,7,7]{2,1,0:T(8,128)S(1)} %get-tuple-element.55), channel_id=1, source_target_pairs={{17,0},{18,1},{19,2},{20,3},{21,4},{22,5},{23,6},{24,7},{25,8},{26... | collective-permute-start | bytes 2360 | tf_op jit(solution)/shard_map/ppermute | solution.py:91
  39.0 1.1 copy-start
  39.0 1.1 copy-start.3
  39.2 1.2 copy-start.1
  47.2 1.6 %copy-start.2 = (f32[32,128]{1,0:T(8,128)S(1)}, f32[32,128]{1,0:T(8,128)}, u32[]{:S(2)}) copy-start(f32[32,128]{1,0:T(8,128)} %param.13) | copy-start | bytes 49156
  49.7 21.7 %copy-start.5 = (f32[1,1,40]{2,1,0:T(1,128)S(1)}, f32[1,1,40]{2,1,0:T(1,128)}, u32[]{:S(2)}) copy-start(f32[1,1,40]{2,1,0:T(1,128)} %param.21) | copy-start | bytes 484
  51.9 17.8 %all-to-all-start = ((f32[32,1,128]{2,1,0:T(1,128)}), f32[32,1,128]{2,1,0:T(1,128)S(1)}, u32[]{:S(2)}, u32[]{:S(2)}) async-start(f32[32,1,128]{2,1,0:T(1,128)} %reshape.272), calls=%async_computation | async-start | bytes 32768 | tf_op jit(solution)/shard_map/all_to_all | solution.py:187
  71.3 15.6 %copy-start.4 = (f32[16,40]{1,0:T(8,128)}, f32[16,40]{1,0:T(8,128)S(1)}, u32[]{:S(2)}) copy-start(f32[16,40]{1,0:T(8,128)S(1)} %fusion.226) | copy-start | bytes 7684
  72.3 11.1 %all-to-all-start.1 = ((f32[32,1,128]{2,1,0:T(1,128)}), f32[32,1,128]{2,1,0:T(1,128)S(1)}, u32[]{:S(2)}, u32[]{:S(2)}) async-start(f32[32,1,128]{2,1,0:T(1,128)} %reshape.274), calls=%async_computation.1 | async-start | bytes 32768 | tf_op jit(solution)/shard_map/all_to_all | solution.py:193
  140.4 13.4 %all-to-all-start.4 = ((f32[32,8,128]{2,1,0:T(8,128)}), f32[32,8,128]{2,1,0:T(8,128)S(1)}, u32[]{:S(2)}, u32[]{:S(2)}) async-start(f32[32,8,128]{2,1,0:T(8,128)} %broadcast_in_dim.17), calls=%async_computation.4 | async-start | bytes 262144 | tf_op jit(solution)/shard_map/all_to_all | solution.py:77

commit v4 on v2

--- a/solution.py
+++ b/solution.py
@@ -89,20 +89,13 @@
     ]
 
 
-def butterfly(values, axis):
-    count = lax.axis_size(axis)
-    stride = 1
-    while stride < count:
-        values = values + lax.ppermute(values, axis, [(i, i ^ stride) for i in range(count)])
-        stride *= 2
-    return values
-
-
 def all_sum(values):
     count = lax.axis_size("gx")
+    rows = lax.axis_size("gy")
     flat = values.reshape(count, -1, 128)
     part = lax.all_to_all(flat, "gx", 0, 0, tiled=True).sum(0)
-    part = butterfly(part, "gy")
+    copies = jnp.broadcast_to(part[None], (rows,) + part.shape)
+    part = lax.all_to_all(copies, "gy", 0, 0, tiled=True).sum(0)
     spread_out = jnp.broadcast_to(part[None], (count,) + part.shape)
     return lax.all_to_all(spread_out, "gx", 0, 0, tiled=True).reshape(values.shape)
 

time: 149 us -> 137 us (0.919)
  starting transfers between devices: 61.5 us -> 30.1 us
  blocking collectives: 11.3 us -> 37.5 us
  waiting for transfers between devices: 29.1 us -> 22.9 us
    ppermute x4 -> x0, starting transfers between devices: 29.5 us -> none  [butterfly(): lax.ppermute(values, axis, [(i, i ^ stride) for i in range(count)])]
    all_to_all x0 -> x1, blocking collectives: none -> 26.2 us  [all_sum(): part = lax.all_to_all(copies, 'gy', 0, 0, tiled=True).sum(0)]
    ppermute x4 -> x0, waiting for transfers between devices: 6.17 us -> none  [butterfly(): lax.ppermute(values, axis, [(i, i ^ stride) for i in range(count)])]
    all_to_all x1, starting transfers between devices: 7.68 us -> 5.7 us  [all_sum(): lax.all_to_all(spread_out, 'gx', 0, 0, tiled=True).reshape(values.shape)]
  transfers between devices with their start and end apart: 11 -> 7, of which waited for: 8 -> 4; matrix products, arithmetic and copies ran while one was open for 5% -> 5% of each run, Pallas kernels for 0% -> 0%
where the time goes in v4:
time: 137 us; the launch traced here: 136 us
  blocking collectives  37.5 us (27%)
  starting transfers between devices  30.1 us (22%)
  other arithmetic  26 us (19%)
  waiting for transfers between devices  22.9 us (17%)
  local copies, waits for them, and re-layouts  13.5 us (10%)
  matrix products  5 us (4%)
    all_to_all x1, blocking collectives, all_sum(): part = lax.all_to_all(copies, 'gy', 0, 0, tiled=True).sum(0)  26.2 us
    all_to_all x1, blocking collectives, all_sum(): part = lax.all_to_all(flat, 'gx', 0, 0, tiled=True).sum(0)  11.3 us
    another operation x9, other arithmetic, advance(): return jnp.stack([new_temp * inside, new_hum * inside])  10 us
    all_to_all x1, starting transfers between devices, local(): lax.all_to_all(picked, 'gx', split_axis=1, concat_axis=1, tiled=True)  7.65 us
    all_to_all x1, waiting for transfers between devices, all_sum(): lax.all_to_all(spread_out, 'gx', 0, 0, tiled=True).reshape(values.shape)  7.5 us
    all_to_all x1, waiting for transfers between devices, local(): lax.all_to_all(backward, 'gx', split_axis=1, concat_axis=1, tiled=True)  6.91 us
    ppermute x2, starting transfers between devices, exchange(): lax.ppermute(pack(heads), axis, [(i + 1, i) for i in range(ends)])  6.81 us
    all_to_all x1, waiting for transfers between devices, local(): lax.all_to_all(picked, 'gx', split_axis=1, concat_axis=1, tiled=True)  6.76 us
  transfers between devices with their start and end apart: 7, of which 4 were waited for; matrix products, arithmetic and copies ran while one was open for 5% of the time, Pallas kernels for 0%

profile of v4, /device:TPU:1, one launch (start us, length us, event | category | flops | bytes accessed | tf_op | source)
XLA Modules:
  0.0 136.3 jit_solution(11789240077805971128)
XLA Ops:
  0.7 0.8 pad_maximum_fusion.11
  2.3 4.5 %collective-permute-start = (f32[4032]{0:T(1024)S(1)}, f32[4032]{0:T(1024)S(1)}, u32[]{:S(2)}, u32[]{:S(2)}) collective-permute-start(f32[4032]{0:T(1024)S(1)} %pad_maximum_fusion.12), channel_id=1, source_target_pairs={{0,16},{16,32},{32,48},{48,64},{64,80},{80,96},{96,112},{112,128},... | collective-permute-start | bytes 48392 | tf_op jit(solution)/shard_map/ppermute | solution.py:85
  6.9 5.5 %collective-permute-start.1 = (f32[4032]{0:T(1024)S(1)}, f32[4032]{0:T(1024)S(1)}, u32[]{:S(2)}, u32[]{:S(2)}) collective-permute-start(f32[4032]{0:T(1024)S(1)} %pad_maximum_fusion.13), channel_id=1, source_target_pairs={{16,0},{32,16},{48,32},{64,48},{80,64},{96,80},{112,96},{128,112},... | collective-permute-start | bytes 48392 | tf_op jit(solution)/shard_map/ppermute | solution.py:86
  13.9 0.9 fusion.279
  16.0 0.8 copy.41
  18.1 1.3 collective-permute-start.2
  19.7 1.3 collective-permute-start.3
  21.1 1.1 fusion.263
  22.4 1.8 %collective-permute-done.3 = f32[1512]{0:T(1024)S(1)} collective-permute-done((f32[1512]{0:T(1024)S(1)}, f32[1512]{0:T(1024)S(1)}, u32[]{:S(2)}, u32[]{:S(2)}) %collective-permute-start.3) | collective-permute-done | bytes 6080 | tf_op jit(solution)/shard_map/ppermute | solution.py:86
  26.4 0.9 convolution_multiply_fusion
  27.3 0.9 broadcast_multiply_fusion
  28.2 0.9 multiply_multiply_fusion
  29.1 1.6 %fusion.164 = (f32[16,38,134]{2,1,0:T(8,128)S(1)}, f32[16,38,134]{2,1,0:T(8,128)S(1)}) fusion(f32[16,40,136]{2,1,0:T(8,128)S(1)} %get-tuple-element.28, f32[16,40,136]{2,1,0:T(8,128)S(1)} %get-tuple-element.29, f32[38,134]{1,0:T(8,128)S(1)} %get-tuple-element.46, f32[38,134]{1,0:T(8,128)S(1)} %get-tuple-element.47, f32[16,42,138]{2,1,0:T(8,128)S(1)} %get-tuple-element.7, ...), kind=kLoop, calls=%fused_computation.248 | loop fusion | flops 2444160 | bytes 4358752 | tf_op jit(solution)/shard_map/mul | solution.py:53
  30.8 1.6 %fusion.145 = (f32[16,36,132]{2,1,0:T(8,128)S(1)}, f32[16,36,132]{2,1,0:T(8,128)S(1)}) fusion(f32[16,38,134]{2,1,0:T(8,128)S(1)} %get-tuple-element.26, f32[16,38,134]{2,1,0:T(8,128)S(1)} %get-tuple-element.27, f32[36,132]{1,0:T(8,128)S(1)} %get-tuple-element.43, f32[36,132]{1,0:T(8,128)S(1)} %get-tuple-element.44, f32[16,42,138]{2,1,0:T(8,128)S(1)} %get-tuple-element.7, ...), kind=kLoop, calls=%fused_computation.220 | loop fusion | flops 2280960 | bytes 4067712 | tf_op jit(solution)/shard_map/mul | solution.py:53
  33.1 1.6 %fusion.140 = (f32[16,34,130]{2,1,0:T(8,128)S(1)}, f32[16,34,130]{2,1,0:T(8,128)S(1)}, f32[16,34,130]{2,1,0:T(8,128)S(1)}, f32[16,34,130]{2,1,0:T(8,128)S(1)}) fusion(f32[16,42,138]{2,1,0:T(8,128)S(1)} %get-tuple-element.7, f32[16,36,132]{2,1,0:T(8,128)S(1)} %get-tuple-element.25, f32[34,130]{1,0:T(8,128)S(1)} %get-tuple-element.40, ...), kind=kLoop, calls=%fused_computation.214 | loop fusion | flops 1555840 | bytes 4349280 | tf_op jit(solution)/shard_map/add | solution.py:140
  34.8 0.8 fusion.207
  37.8 7.7 %all-to-all-start = ((f32[32,1,128]{2,1,0:T(1,128)}), f32[32,1,128]{2,1,0:T(1,128)S(1)}, u32[]{:S(2)}, u32[]{:S(2)}) async-start(f32[32,1,128]{2,1,0:T(1,128)} %reshape.240), calls=%async_computation | async-start | bytes 32768 | tf_op jit(solution)/shard_map/all_to_all | solution.py:162
  45.6 6.8 %all-to-all-done = f32[32,1,128]{2,1,0:T(1,128)S(1)} async-done(((f32[32,1,128]{2,1,0:T(1,128)}), f32[32,1,128]{2,1,0:T(1,128)S(1)}, u32[]{:S(2)}, u32[]{:S(2)}) %all-to-all-start) | async-done | bytes 16416 | tf_op jit(solution)/shard_map/all_to_all | solution.py:162
  55.0 4.1 %all-to-all-start.1 = ((f32[32,1,128]{2,1,0:T(1,128)}), f32[32,1,128]{2,1,0:T(1,128)S(1)}, u32[]{:S(2)}, u32[]{:S(2)}) async-start(f32[32,1,128]{2,1,0:T(1,128)} %reshape.242), calls=%async_computation.1 | async-start | bytes 32768 | tf_op jit(solution)/shard_map/all_to_all | solution.py:168
  59.2 6.9 %all-to-all-done.1 = f32[32,1,128]{2,1,0:T(1,128)S(1)} async-done(((f32[32,1,128]{2,1,0:T(1,128)}), f32[32,1,128]{2,1,0:T(1,128)S(1)}, u32[]{:S(2)}, u32[]{:S(2)}) %all-to-all-start.1) | async-done | bytes 16416 | tf_op jit(solution)/shard_map/all_to_all | solution.py:168
  66.8 2.0 %scatter_custom_fusion = f32[16,4096]{0,1:T(8,128)S(1)} fusion(s32[256]{0:T(256)S(1)} %bitcast.182, f32[]{:T(128)} %constant.15.clone.1, f32[32,8]{1,0:T(8,128)S(1)} %copy.40, f32[32,8,16]{2,1,0:T(8,128)S(1)} %reshape.243), kind=kCustom, calls=%fused_computation.26 | custom fusion | flops 8192 | bytes 409604 | tf_op jit(solution)/shard_map/scatter-add | solution.py:171
  69.5 1.1 multiply_bitcast_fusion
  71.2 1.7 %fusion.107 = (f32[1,16,42,138]{3,2,1,0:T(8,128)S(1)}, f32[1,16,42,138]{3,2,1,0:T(8,128)S(1)}) fusion(f32[16,44,140]{2,1,0:T(8,128)S(1)} %get-tuple-element.22, f32[16,44,140]{2,1,0:T(8,128)S(1)} %get-tuple-element.23, f32[42,138]{1,0:T(8,128)S(1)} %get-tuple-element.36, f32[42,138]{1,0:T(8,128)S(1)} %get-tuple-element.38, ...), kind=kLoop, calls=%fused_computation.167 | loop fusion | flops 2596608 | bytes 4590432 | tf_op jit(solution)/shard_map/stack | solution.py:53
  73.6 1.7 %fusion.87 = (f32[1,16,42,138]{3,2,1,0:T(8,128)S(1)}, f32[1,16,42,138]{3,2,1,0:T(8,128)S(1)}) fusion(f32[16,44,140]{2,1,0:T(8,128)S(1)} %get-tuple-element.20, f32[16,44,140]{2,1,0:T(8,128)S(1)} %get-tuple-element.21, f32[42,138]{1,0:T(8,128)S(1)} %get-tuple-element.36, f32[42,138]{1,0:T(8,128)S(1)} %get-tuple-element.38, ...), kind=kLoop, calls=%fused_computation.137 | loop fusion | flops 2596608 | bytes 4590432 | tf_op jit(solution)/shard_map/stack | solution.py:53
  76.0 1.7 %fusion.67 = (f32[1,16,42,138]{3,2,1,0:T(8,128)S(1)}, f32[1,16,42,138]{3,2,1,0:T(8,128)S(1)}) fusion(f32[16,44,140]{2,1,0:T(8,128)S(1)} %get-tuple-element.18, f32[16,44,140]{2,1,0:T(8,128)S(1)} %get-tuple-element.19, f32[42,138]{1,0:T(8,128)S(1)} %get-tuple-element.36, f32[42,138]{1,0:T(8,128)S(1)} %get-tuple-element.38, ...), kind=kLoop, calls=%fused_computation.107 | loop fusion | flops 2596608 | bytes 4590432 | tf_op jit(solution)/shard_map/stack | solution.py:53
  78.3 1.7 %fusion.47 = (f32[1,16,42,138]{3,2,1,0:T(8,128)S(1)}, f32[1,16,42,138]{3,2,1,0:T(8,128)S(1)}) fusion(f32[16,44,140]{2,1,0:T(8,128)S(1)} %get-tuple-element.16, f32[16,44,140]{2,1,0:T(8,128)S(1)} %get-tuple-element.17, f32[42,138]{1,0:T(8,128)S(1)} %get-tuple-element.36, f32[42,138]{1,0:T(8,128)S(1)} %get-tuple-element.38, ...), kind=kLoop, calls=%fused_computation.77 | loop fusion | flops 2596608 | bytes 4590432 | tf_op jit(solution)/shard_map/stack | solution.py:53
  80.6 2.1 %fusion.118 = f32[16,44,32]{1,2,0:T(8,128)S(1)} fusion(f32[16,44,140]{2,1,0:T(8,128)S(1)} %fusion.25, f32[44,140]{1,0:T(8,128)S(1)} %get-tuple-element.60, f32[44,140]{1,0:T(8,128)S(1)} %get-tuple-element.58, f32[44,140]{1,0:T(8,128)S(1)} %get-tuple-element.59, f32[44,140]{1,0:T(8,128)S(1)} %get-tuple-element.57, f32[44,140]{1,0:T(8,128)S(1)} %get-tuple-element.51, ...), kind=kOutput, calls=%fused_computation.187 | convolution fusion | flops 39038720 | bytes 625728 | tf_op jit(solution)/shard_map/rxy,yb->rxb/dot_general | solution.py:185
  83.5 11.3 %all_to_all.25 = f32[32,8,128]{2,1,0:T(8,128)S(1)} all-to-all(f32[32,8,128]{2,1,0:T(8,128)S(1)} %reshape_reshape.6), channel_id=1, replica_groups=mesh['gx'=32,'gy'=16] {'gx'}, dimensions={0} | all-to-all | bytes 262144 | tf_op jit(solution)/shard_map/all_to_all | solution.py:96
  94.9 26.2 %all_to_all.26 = f32[16,8,128]{2,1,0:T(8,128)S(1)} all-to-all(f32[16,8,128]{2,1,0:T(8,128)S(1)} %broadcast_in_dim.16), channel_id=1, replica_groups=mesh['gx'=32,'gy'=16] {'gy'}, dimensions={0} | all-to-all | bytes 131072 | tf_op jit(solution)/shard_map/all_to_all | solution.py:98
  121.7 5.7 %all-to-all-start.4 = ((f32[32,8,128]{2,1,0:T(8,128)}), f32[32,8,128]{2,1,0:T(8,128)S(1)}, u32[]{:S(2)}, u32[]{:S(2)}) async-start(f32[32,8,128]{2,1,0:T(8,128)} %broadcast_in_dim.17), calls=%async_computation.4 | async-start | bytes 262144 | tf_op jit(solution)/shard_map/all_to_all | solution.py:100
  127.6 7.5 %all-to-all-done.4 = f32[32,8,128]{2,1,0:T(8,128)S(1)} async-done(((f32[32,8,128]{2,1,0:T(8,128)}), f32[32,8,128]{2,1,0:T(8,128)S(1)}, u32[]{:S(2)}, u32[]{:S(2)}) %all-to-all-start.4) | async-done | bytes 131104 | tf_op jit(solution)/shard_map/all_to_all | solution.py:100
  135.4 0.9 copy.46
  (112 shorter events, 19.6 us)
Async XLA Ops:
  0.6 23.8 %copy-start.4 = (f32[32,128]{1,0:T(8,128)S(1)}, f32[32,128]{1,0:T(8,128)}, u32[]{:S(2)}) copy-start(f32[32,128]{1,0:T(8,128)} %param.11) | copy-start | bytes 49156
  0.6 23.8 %copy-start.3 = (f32[32,128]{1,0:T(8,128)S(1)}, f32[32,128]{1,0:T(8,128)}, u32[]{:S(2)}) copy-start(f32[32,128]{1,0:T(8,128)} %param.12) | copy-start | bytes 49156
  0.7 23.8 %copy-start.1 = (f32[32,128]{1,0:T(8,128)S(1)}, f32[32,128]{1,0:T(8,128)}, u32[]{:S(2)}) copy-start(f32[32,128]{1,0:T(8,128)} %param.13) | copy-start | bytes 49156
  0.7 20.5 %copy-start = (f32[16,64,32]{1,2,0:T(8,128)S(1)}, f32[16,64,32]{1,2,0:T(8,128)}, u32[]{:S(2)}) copy-start(f32[16,64,32]{1,2,0:T(8,128)} %param.16) | copy-start | bytes 393220
  2.3 14.6 %collective-permute-start = (f32[4032]{0:T(1024)S(1)}, f32[4032]{0:T(1024)S(1)}, u32[]{:S(2)}, u32[]{:S(2)}) collective-permute-start(f32[4032]{0:T(1024)S(1)} %pad_maximum_fusion.12), channel_id=1, source_target_pairs={{0,16},{16,32},{32,48},{48,64},{64,80},{80,96},{96,112},{112,128},... | collective-permute-start | bytes 48392 | tf_op jit(solution)/shard_map/ppermute | solution.py:85
  6.9 10.0 %collective-permute-start.1 = (f32[4032]{0:T(1024)S(1)}, f32[4032]{0:T(1024)S(1)}, u32[]{:S(2)}, u32[]{:S(2)}) collective-permute-start(f32[4032]{0:T(1024)S(1)} %pad_maximum_fusion.13), channel_id=1, source_target_pairs={{16,0},{32,16},{48,32},{64,48},{80,64},{96,80},{112,96},{128,112},... | collective-permute-start | bytes 48392 | tf_op jit(solution)/shard_map/ppermute | solution.py:86
  18.1 4.1 %collective-permute-start.2 = (f32[1512]{0:T(1024)S(1)}, f32[1512]{0:T(1024)S(1)}, u32[]{:S(2)}, u32[]{:S(2)}) collective-permute-start(f32[1512]{0:T(1024)S(1)} %pad_maximum_fusion.14), channel_id=1, source_target_pairs={{0,1},{1,2},{2,3},{3,4},{4,5},{5,6},{6,7},{7,8},{8,9},{9,10},{10,1... | collective-permute-start | bytes 18152 | tf_op jit(solution)/shard_map/ppermute | solution.py:85
  19.7 4.5 %collective-permute-start.3 = (f32[1512]{0:T(1024)S(1)}, f32[1512]{0:T(1024)S(1)}, u32[]{:S(2)}, u32[]{:S(2)}) collective-permute-start(f32[1512]{0:T(1024)S(1)} %pad_maximum_fusion.15), channel_id=1, source_target_pairs={{1,0},{2,1},{3,2},{4,3},{5,4},{6,5},{7,6},{8,7},{9,8},{10,9},{11,1... | collective-permute-start | bytes 18152 | tf_op jit(solution)/shard_map/ppermute | solution.py:86
  25.0 1.4 %copy-start.2 = (f32[128,32]{0,1:T(8,128)S(1)}, f32[128,32]{0,1:T(8,128)}, u32[]{:S(2)}) copy-start(f32[128,32]{0,1:T(8,128)} %param.15) | copy-start | bytes 49156
  35.6 18.4 %copy-start.7 = (f32[1,1,40]{2,1,0:T(1,128)S(1)}, f32[1,1,40]{2,1,0:T(1,128)}, u32[]{:S(2)}) copy-start(f32[1,1,40]{2,1,0:T(1,128)} %param.21) | copy-start | bytes 484
  37.8 14.6 %all-to-all-start = ((f32[32,1,128]{2,1,0:T(1,128)}), f32[32,1,128]{2,1,0:T(1,128)S(1)}, u32[]{:S(2)}, u32[]{:S(2)}) async-start(f32[32,1,128]{2,1,0:T(1,128)} %reshape.240), calls=%async_computation | async-start | bytes 32768 | tf_op jit(solution)/shard_map/all_to_all | solution.py:162
  54.0 15.5 %copy-start.6 = (f32[16,40]{1,0:T(8,128)}, f32[16,40]{1,0:T(8,128)S(1)}, u32[]{:S(2)}) copy-start(f32[16,40]{1,0:T(8,128)S(1)} %fusion.226) | copy-start | bytes 7684
  55.0 11.1 %all-to-all-start.1 = ((f32[32,1,128]{2,1,0:T(1,128)}), f32[32,1,128]{2,1,0:T(1,128)S(1)}, u32[]{:S(2)}, u32[]{:S(2)}) async-start(f32[32,1,128]{2,1,0:T(1,128)} %reshape.242), calls=%async_computation.1 | async-start | bytes 32768 | tf_op jit(solution)/shard_map/all_to_all | solution.py:168
  80.6 2.1 %copy-start.5 = (f32[32,64]{1,0:T(8,128)S(1)}, f32[32,64]{1,0:T(8,128)}, u32[]{:S(2)}) copy-start(f32[32,64]{1,0:T(8,128)} %param.14) | copy-start | bytes 24580
  121.7 13.4 %all-to-all-start.4 = ((f32[32,8,128]{2,1,0:T(8,128)}), f32[32,8,128]{2,1,0:T(8,128)S(1)}, u32[]{:S(2)}, u32[]{:S(2)}) async-start(f32[32,8,128]{2,1,0:T(8,128)} %broadcast_in_dim.17), calls=%async_computation.4 | async-start | bytes 262144 | tf_op jit(solution)/shard_map/all_to_all | solution.py:100

commit v5 on v4

--- a/solution.py
+++ b/solution.py
@@ -102,6 +102,49 @@
 
 def pad_sides(field, width):
     return jnp.pad(field, [(0, 0)] * (field.ndim - 2) + [(width, width), (width, width)])
+
+
+def neighbours(field):
+    rows, cols = field.shape[-2:]
+    lead = [(0, 0)] * (field.ndim - 2)
+    return (
+        jnp.pad(field[..., : rows - 1, :], lead + [(1, 0), (0, 0)]),
+        jnp.pad(field[..., 1:, :], lead + [(0, 1), (0, 0)]),
+        jnp.pad(field[..., :, : cols - 1], lead + [(0, 0), (1, 0)]),
+        jnp.pad(field[..., :, 1:], lead + [(0, 0), (0, 1)]),
+    )
+
+
+def adjoint_projection(adjoint_load, static_six, rows_six, cols_six, depth):
+    n_dirs = adjoint_load.shape[0]
+    load_wide = pad_sides(adjoint_load, depth)
+    tall, wide = load_wide.shape[1:]
+    load_flat = jnp.transpose(load_wide, (1, 0, 2)).reshape(tall, n_dirs * wide)
+    ring = pad_sides(jnp.ones((tall - 2, wide - 2), jnp.float32), 1)
+    fields = jnp.tile(jnp.concatenate([static_six, ring[None]]), (1, 1, n_dirs))
+    diff, humid, couple = fields[0], fields[1], fields[2]
+    keep = fields[3] * fields[4]
+    diff_near = neighbours(diff)
+    temper = jnp.zeros_like(load_flat)
+    moist = load_flat
+    summed = load_flat
+    for i in range(depth - 1):
+        lap_temp = sum((n - temper for n in neighbours(temper)))
+        lap_hum = sum(
+            (0.5 * (diff + k) * (n - moist) for k, n in zip(diff_near, neighbours(moist)))
+        )
+        temper, moist = (
+            (temper + step_ratio * lap_temp - couple * moist) * keep,
+            (moist + step_ratio * lap_hum + couple * temper) * keep,
+        )
+        summed = summed + moist
+    lam = step_ratio * summed
+    gradient = diff * sum(
+        (0.5 * (h - humid) * (lam - l) for h, l in zip(neighbours(humid), neighbours(lam)))
+    )
+    gradient = gradient.reshape(tall, n_dirs, wide)
+    projected = jnp.einsum("xry,yb->rxb", gradient, cols_six, precision=exact)
+    return jnp.einsum("xa,rxb->rab", rows_six, projected, precision=exact)
 
 
 def local(
@@ -170,20 +213,9 @@
     adjoint_load = (
         jnp.zeros((n_dirs, height * breadth), jnp.float32).at[:, cell_ids].add(load_values)
     )
-    load_wide = pad_sides(adjoint_load.reshape(n_dirs, height, breadth), rim_depth)
-    state_now = jnp.stack([jnp.zeros_like(load_wide), load_wide])
-    summed = load_wide
-    for i in range(rim_depth - 1):
-        state_now = pad_sides(advance(state_now, static_six, -1.0), 1)
-        summed = summed + state_now[1]
-    lam_wide = pad_sides(step_ratio * summed, 1)
-    lam_mid, lam_near = spread(lam_wide)
-    hum_mid, hum_near = spread(static_wide[1])
-    gradient = static_six[0] * sum(
-        (0.5 * (h - hum_mid) * (lam_mid - l) for h, l in zip(hum_near, lam_near))
-    )
-    projected = jnp.einsum("rxy,yb->rxb", gradient, cols_six, precision=exact)
-    projected = jnp.einsum("xa,rxb->rab", rows_six, projected, precision=exact)
+    projected = adjoint_projection(
+        adjoint_load.reshape(n_dirs, height, breadth), static_six, rows_six, cols_six, rim_depth
+    )
     summed_modes = all_sum(projected.reshape(n_dirs, -1))
     hess_action = directions + summed_modes.reshape(directions.shape)
     return (gauge_read.reshape(1, 1, n_dirs, gauges), hess_action)

time: 137 us -> 146 us (1.066)
  local copies, waits for them, and re-layouts: 13.5 us -> 34.4 us
  waiting for transfers between devices: 22.9 us -> 13.8 us
  other arithmetic: 26 us -> 19.7 us
  blocking collectives: 37.5 us -> 40 us
    another operation x9 -> x0, other arithmetic: 10 us -> none  [advance(): return jnp.stack([new_temp * inside, new_hum * inside])]
    slice x0 -> x24, local copies, waits for them, and re-layouts: none -> 8.99 us  [the longest x11 3.92 us: neighbours(): field[..., :rows - 1, :]]
    another operation x0 -> x17, local copies, waits for them, and re-layouts: none -> 6.31 us  [the longest x15 6.25 us: adjoint_projection(): fields = jnp.tile(jnp.concatenate([static_six, ring[None]]), (1, 1, n_dirs))]
    all_to_all x1, waiting for transfers between devices: 6.91 us -> 1.07 us  [local(): lax.all_to_all(backward, 'gx', split_axis=1, concat_axis=1, tiled=True)]
    mul x4 -> x8, other arithmetic: 0.87 us -> 4.55 us  [the longest x4 2.82 us: adjoint_projection(): (moist + step_ratio * lap_hum + couple * temper) * keep]
    all_to_all x1, waiting for transfers between devices: 6.76 us -> 3.73 us  [local(): lax.all_to_all(picked, 'gx', split_axis=1, concat_axis=1, tiled=True)]
    all_to_all x1, blocking collectives: 11.3 us -> 13.8 us  [all_sum(): part = lax.all_to_all(flat, 'gx', 0, 0, tiled=True).sum(0)]
    unnamed x24 -> x70, local copies, waits for them, and re-layouts: 4.3 us -> 6.74 us
  transfers between devices with their start and end apart: 7 -> 7, of which waited for: 4 -> 4; matrix products, arithmetic and copies ran while one was open for 5% -> 11% of each run, Pallas kernels for 0% -> 0%
where the time goes in v5:
time: 146 us; the launch traced here: 144 us
  blocking collectives  40 us (27%)
  local copies, waits for them, and re-layouts  34.4 us (24%)
  starting transfers between devices  30.1 us (21%)
  other arithmetic  19.7 us (13%)
  waiting for transfers between devices  13.8 us (9%)
  matrix products  4.85 us (3%)
  between operations  1.58 us (1%)
    all_to_all x1, blocking collectives, all_sum(): part = lax.all_to_all(copies, 'gy', 0, 0, tiled=True).sum(0)  26.2 us
    all_to_all x1, blocking collectives, all_sum(): part = lax.all_to_all(flat, 'gx', 0, 0, tiled=True).sum(0)  13.8 us
    all_to_all x1, starting transfers between devices, local(): lax.all_to_all(picked, 'gx', split_axis=1, concat_axis=1, tiled=True)  7.65 us
    all_to_all x1, waiting for transfers between devices, all_sum(): lax.all_to_all(spread_out, 'gx', 0, 0, tiled=True).reshape(values.shape)  7.49 us
    ppermute x2, starting transfers between devices, exchange(): lax.ppermute(pack(heads), axis, [(i + 1, i) for i in range(ends)])  6.81 us
    unnamed x70, local copies, waits for them, and re-layouts  6.74 us
    another operation x15, local copies, waits for them, and re-layouts, adjoint_projection(): fields = jnp.tile(jnp.concatenate([static_six, ring[None]]), (1, 1, n_dirs))  6.25 us
    ppermute x2, starting transfers between devices, exchange(): lax.ppermute(pack(tails), axis, [(i, i + 1) for i in range(ends)])  5.77 us
  transfers between devices with their start and end apart: 7, of which 4 were waited for; matrix products, arithmetic and copies ran while one was open for 11% of the time, Pallas kernels for 0%

profile of v5, /device:TPU:1, one launch (start us, length us, event | category | flops | bytes accessed | tf_op | source)
XLA Modules:
  0.0 144.4 jit_solution(13427204133916443376)
XLA Ops:
  2.3 4.5 %collective-permute-start = (f32[4032]{0:T(1024)S(1)}, f32[4032]{0:T(1024)S(1)}, u32[]{:S(2)}, u32[]{:S(2)}) collective-permute-start(f32[4032]{0:T(1024)S(1)} %pad_maximum_fusion.12), channel_id=1, source_target_pairs={{0,16},{16,32},{32,48},{48,64},{64,80},{80,96},{96,112},{112,128},... | collective-permute-start | bytes 48392 | tf_op jit(solution)/shard_map/ppermute | solution.py:85
  6.8 5.5 %collective-permute-start.1 = (f32[4032]{0:T(1024)S(1)}, f32[4032]{0:T(1024)S(1)}, u32[]{:S(2)}, u32[]{:S(2)}) collective-permute-start(f32[4032]{0:T(1024)S(1)} %pad_maximum_fusion.13), channel_id=1, source_target_pairs={{16,0},{32,16},{48,32},{64,48},{80,64},{96,80},{112,96},{128,112},... | collective-permute-start | bytes 48392 | tf_op jit(solution)/shard_map/ppermute | solution.py:86
  18.1 1.3 collective-permute-start.2
  19.6 1.3 collective-permute-start.3
  21.1 1.3 fusion.122
  22.7 1.5 %collective-permute-done.3 = f32[1512]{0:T(1024)S(1)} collective-permute-done((f32[1512]{0:T(1024)S(1)}, f32[1512]{0:T(1024)S(1)}, u32[]{:S(2)}, u32[]{:S(2)}) %collective-permute-start.3) | collective-permute-done | bytes 6080 | tf_op jit(solution)/shard_map/ppermute | solution.py:86
  29.1 1.6 %fusion.36 = (f32[16,38,134]{2,1,0:T(8,128)S(1)}, f32[16,38,134]{2,1,0:T(8,128)S(1)}) fusion(f32[16,40,136]{2,1,0:T(8,128)S(1)} %get-tuple-element.22, f32[16,40,136]{2,1,0:T(8,128)S(1)} %get-tuple-element.23, f32[38,134]{1,0:T(8,128)S(1)} %get-tuple-element.82, f32[38,134]{1,0:T(8,128)S(1)} %get-tuple-element.83, f32[16,42,138]{2,1,0:T(8,128)S(1)} %get-tuple-element.16, ...), kind=kLoop, calls=%fused_computation.61 | loop fusion | flops 2444160 | bytes 4358752 | tf_op jit(solution)/shard_map/mul | solution.py:53
  30.7 1.6 %fusion.17 = (f32[16,36,132]{2,1,0:T(8,128)S(1)}, f32[16,36,132]{2,1,0:T(8,128)S(1)}) fusion(f32[16,38,134]{2,1,0:T(8,128)S(1)} %get-tuple-element.19, f32[16,38,134]{2,1,0:T(8,128)S(1)} %get-tuple-element.20, f32[36,132]{1,0:T(8,128)S(1)} %get-tuple-element.79, f32[36,132]{1,0:T(8,128)S(1)} %get-tuple-element.80, f32[16,42,138]{2,1,0:T(8,128)S(1)} %get-tuple-element.16, ...), kind=kLoop, calls=%fused_computation.33 | loop fusion | flops 2280960 | bytes 4067712 | tf_op jit(solution)/shard_map/mul | solution.py:53
  33.1 1.6 %fusion.12 = (f32[16,34,130]{2,1,0:T(8,128)S(1)}, f32[16,34,130]{2,1,0:T(8,128)S(1)}, f32[16,34,130]{2,1,0:T(8,128)S(1)}, f32[16,34,130]{2,1,0:T(8,128)S(1)}) fusion(f32[16,42,138]{2,1,0:T(8,128)S(1)} %get-tuple-element.16, f32[16,36,132]{2,1,0:T(8,128)S(1)} %get-tuple-element.18, f32[34,130]{1,0:T(8,128)S(1)} %get-tuple-element.76, ...), kind=kLoop, calls=%fused_computation.27 | loop fusion | flops 1555840 | bytes 4349280 | tf_op jit(solution)/shard_map/add | solution.py:183
  37.7 7.7 %all-to-all-start = ((f32[32,1,128]{2,1,0:T(1,128)}), f32[32,1,128]{2,1,0:T(1,128)S(1)}, u32[]{:S(2)}, u32[]{:S(2)}) async-start(f32[32,1,128]{2,1,0:T(1,128)} %reshape.283), calls=%async_computation | async-start | bytes 32768 | tf_op jit(solution)/shard_map/all_to_all | solution.py:205
  45.8 1.0 fusion.154
  47.3 1.1 fusion.138
  48.5 3.7 %all-to-all-done = f32[32,1,128]{2,1,0:T(1,128)S(1)} async-done(((f32[32,1,128]{2,1,0:T(1,128)}), f32[32,1,128]{2,1,0:T(1,128)S(1)}, u32[]{:S(2)}, u32[]{:S(2)}) %all-to-all-start) | async-done | bytes 16416 | tf_op jit(solution)/shard_map/all_to_all | solution.py:205
  54.9 4.1 %all-to-all-start.1 = ((f32[32,1,128]{2,1,0:T(1,128)}), f32[32,1,128]{2,1,0:T(1,128)S(1)}, u32[]{:S(2)}, u32[]{:S(2)}) async-start(f32[32,1,128]{2,1,0:T(1,128)} %reshape.285), calls=%async_computation.1 | async-start | bytes 32768 | tf_op jit(solution)/shard_map/all_to_all | solution.py:211
  60.2 1.2 tile.42
  61.4 1.2 tile.44
  62.6 1.2 tile.38
  63.9 1.1 tile.49
  65.0 1.1 all-to-all-done.1
  66.9 2.2 %scatter_custom_fusion = f32[16,4096]{0,1:T(8,128)S(1)} fusion(s32[256]{0:T(256)} %bitcast.146, f32[]{:T(128)} %constant.14.clone.1, f32[32,8]{1,0:T(8,128)} %copy-done.20, f32[32,8,16]{2,1,0:T(8,128)S(1)} %reshape.286), kind=kCustom, calls=%fused_computation.6 | custom fusion | flops 8192 | bytes 295424 | tf_op jit(solution)/shard_map/scatter-add | solution.py:214
  69.1 1.3 copy.42
  70.4 1.2 pad_bitcast_fusion
  71.6 1.1 fusion.136
  73.0 2.3 %slice.709 = f32[43,2240]{1,0:T(8,128)} reshape(f32[43,16,140]{2,1,0:T(8,128)} %get-tuple-element.24) | data formatting | bytes 770560 | tf_op jit(solution)/shard_map/slice | solution.py:111
  75.3 1.2 slice.713
  82.5 1.0 add_multiply_fusion.1
  85.6 0.9 reshape.260
  86.6 1.7 %convolution_bitcast_fusion = f32[16,44,32]{1,2,0:T(8,128)S(1)} fusion(f32[44,16,140]{2,1,0:T(8,128)S(1)} %reshape.260, f32[7,32]{0,1:T(8,128)S(1)} %copy-done.19, f32[128,32]{0,1:T(8,128)S(1)} %copy-done.14, f32[7,32]{0,1:T(8,128)S(1)} %copy-done.17), kind=kOutput, calls=%fused_computation.3 | convolution fusion | flops 37856000 | bytes 502528 | tf_op jit(solution)/shard_map/xry,yb->rxb/dot_general | solution.py:146
  89.1 13.8 %all_to_all.25 = f32[32,8,128]{2,1,0:T(8,128)S(1)} all-to-all(f32[32,8,128]{2,1,0:T(8,128)S(1)} %reshape_reshape.6), channel_id=1, replica_groups=mesh['gx'=32,'gy'=16] {'gx'}, dimensions={0} | all-to-all | bytes 262144 | tf_op jit(solution)/shard_map/all_to_all | solution.py:96
  103.0 26.2 %all_to_all.26 = f32[16,8,128]{2,1,0:T(8,128)S(1)} all-to-all(f32[16,8,128]{2,1,0:T(8,128)S(1)} %broadcast_in_dim.22), channel_id=1, replica_groups=mesh['gx'=32,'gy'=16] {'gy'}, dimensions={0} | all-to-all | bytes 131072 | tf_op jit(solution)/shard_map/all_to_all | solution.py:98
  129.8 5.7 %all-to-all-start.4 = ((f32[32,8,128]{2,1,0:T(8,128)}), f32[32,8,128]{2,1,0:T(8,128)S(1)}, u32[]{:S(2)}, u32[]{:S(2)}) async-start(f32[32,8,128]{2,1,0:T(8,128)} %broadcast_in_dim.23), calls=%async_computation.4 | async-start | bytes 262144 | tf_op jit(solution)/shard_map/all_to_all | solution.py:100
  135.8 7.5 %all-to-all-done.4 = f32[32,8,128]{2,1,0:T(8,128)S(1)} async-done(((f32[32,8,128]{2,1,0:T(8,128)}), f32[32,8,128]{2,1,0:T(8,128)S(1)}, u32[]{:S(2)}, u32[]{:S(2)}) %all-to-all-start.4) | async-done | bytes 131104 | tf_op jit(solution)/shard_map/all_to_all | solution.py:100
  (193 shorter events, 33.2 us)
Async XLA Ops:
  0.6 23.7 %copy-start.22 = (f32[32,128]{1,0:T(8,128)S(1)}, f32[32,128]{1,0:T(8,128)}, u32[]{:S(2)}) copy-start(f32[32,128]{1,0:T(8,128)} %param.11) | copy-start | bytes 49156
  0.6 23.7 %copy-start.21 = (f32[32,128]{1,0:T(8,128)S(1)}, f32[32,128]{1,0:T(8,128)}, u32[]{:S(2)}) copy-start(f32[32,128]{1,0:T(8,128)} %param.12) | copy-start | bytes 49156
  0.7 23.7 %copy-start.15 = (f32[32,128]{1,0:T(8,128)S(1)}, f32[32,128]{1,0:T(8,128)}, u32[]{:S(2)}) copy-start(f32[32,128]{1,0:T(8,128)} %param.13) | copy-start | bytes 49156
  2.3 14.6 %collective-permute-start = (f32[4032]{0:T(1024)S(1)}, f32[4032]{0:T(1024)S(1)}, u32[]{:S(2)}, u32[]{:S(2)}) collective-permute-start(f32[4032]{0:T(1024)S(1)} %pad_maximum_fusion.12), channel_id=1, source_target_pairs={{0,16},{16,32},{32,48},{48,64},{64,80},{80,96},{96,112},{112,128},... | collective-permute-start | bytes 48392 | tf_op jit(solution)/shard_map/ppermute | solution.py:85
  6.8 10.1 %collective-permute-start.1 = (f32[4032]{0:T(1024)S(1)}, f32[4032]{0:T(1024)S(1)}, u32[]{:S(2)}, u32[]{:S(2)}) collective-permute-start(f32[4032]{0:T(1024)S(1)} %pad_maximum_fusion.13), channel_id=1, source_target_pairs={{16,0},{32,16},{48,32},{64,48},{80,64},{96,80},{112,96},{128,112},... | collective-permute-start | bytes 48392 | tf_op jit(solution)/shard_map/ppermute | solution.py:86
  15.9 20.9 %copy-start.20 = (f32[32,8]{1,0:T(8,128)}, f32[32,8]{1,0:T(8,128)S(1)}, u32[]{:S(2)}) copy-start(f32[32,8]{1,0:T(8,128)S(1)} %copy.39) | copy-start | bytes 3076
  18.1 4.4 %collective-permute-start.2 = (f32[1512]{0:T(1024)S(1)}, f32[1512]{0:T(1024)S(1)}, u32[]{:S(2)}, u32[]{:S(2)}) collective-permute-start(f32[1512]{0:T(1024)S(1)} %pad_maximum_fusion.14), channel_id=1, source_target_pairs={{0,1},{1,2},{2,3},{3,4},{4,5},{5,6},{6,7},{7,8},{8,9},{9,10},{10,1... | collective-permute-start | bytes 18152 | tf_op jit(solution)/shard_map/ppermute | solution.py:85
  19.6 4.5 %collective-permute-start.3 = (f32[1512]{0:T(1024)S(1)}, f32[1512]{0:T(1024)S(1)}, u32[]{:S(2)}, u32[]{:S(2)}) collective-permute-start(f32[1512]{0:T(1024)S(1)} %pad_maximum_fusion.15), channel_id=1, source_target_pairs={{1,0},{2,1},{3,2},{4,3},{5,4},{6,5},{7,6},{8,7},{9,8},{10,9},{11,1... | collective-permute-start | bytes 18152 | tf_op jit(solution)/shard_map/ppermute | solution.py:86
  21.0 1.4 copy-start.24
  21.1 1.4 copy-start.26
  22.7 3.6 %copy-start.13 = (f32[128,32]{0,1:T(8,128)S(1)}, f32[128,32]{0,1:T(8,128)}, u32[]{:S(2)}) copy-start(f32[128,32]{0,1:T(8,128)} %param.15) | copy-start | bytes 49156
  25.4 2.7 %copy-start.16 = (f32[7,32]{0,1:T(8,128)}, f32[7,32]{0,1:T(8,128)S(1)}, u32[]{:S(2)}) copy-start(f32[7,32]{0,1:T(8,128)S(1)} %copy.35) | copy-start | bytes 2692
  25.7 2.4 %copy-start.18 = (f32[7,32]{0,1:T(8,128)}, f32[7,32]{0,1:T(8,128)S(1)}, u32[]{:S(2)}) copy-start(f32[7,32]{0,1:T(8,128)S(1)} %copy.36) | copy-start | bytes 2692
  37.7 14.6 %all-to-all-start = ((f32[32,1,128]{2,1,0:T(1,128)}), f32[32,1,128]{2,1,0:T(1,128)S(1)}, u32[]{:S(2)}, u32[]{:S(2)}) async-start(f32[32,1,128]{2,1,0:T(1,128)} %reshape.283), calls=%async_computation | async-start | bytes 32768 | tf_op jit(solution)/shard_map/all_to_all | solution.py:205
  46.8 7.1 %copy-start.30 = (f32[1,1,40]{2,1,0:T(1,128)S(1)}, f32[1,1,40]{2,1,0:T(1,128)}, u32[]{:S(2)}) copy-start(f32[1,1,40]{2,1,0:T(1,128)} %param.21) | copy-start | bytes 484
  47.3 11.9 %copy-start = (f32[44,2240]{1,0:T(8,128)}, f32[44,2240]{1,0:T(8,128)S(1)}, u32[]{:S(2)}) copy-start(f32[44,2240]{1,0:T(8,128)S(1)} %tile.40) | copy-start | bytes 1182724
  53.9 5.1 %copy-start.28 = (f32[16,40]{1,0:T(8,128)}, f32[16,40]{1,0:T(8,128)S(1)}, u32[]{:S(2)}) copy-start(f32[16,40]{1,0:T(8,128)S(1)} %fusion.93) | copy-start | bytes 7684
  54.9 11.1 %all-to-all-start.1 = ((f32[32,1,128]{2,1,0:T(1,128)}), f32[32,1,128]{2,1,0:T(1,128)S(1)}, u32[]{:S(2)}, u32[]{:S(2)}) async-start(f32[32,1,128]{2,1,0:T(1,128)} %reshape.285), calls=%async_computation.1 | async-start | bytes 32768 | tf_op jit(solution)/shard_map/all_to_all | solution.py:211
  75.3 1.4 %copy-start.4 = (f32[44,2239]{1,0:T(8,128)S(1)}, f32[44,2239]{1,0:T(8,128)}, u32[]{:S(2)}) copy-start(f32[44,2239]{1,0:T(8,128)} %get-tuple-element.64) | copy-start | bytes 1182196
  75.3 1.5 %copy-start.5 = (f32[44,2239]{1,0:T(8,128)S(1)}, f32[44,2239]{1,0:T(8,128)}, u32[]{:S(2)}) copy-start(f32[44,2239]{1,0:T(8,128)} %get-tuple-element.65) | copy-start | bytes 1182196
  76.5 1.3 copy-start.10
  76.5 1.4 copy-start.11
  83.6 1.4 copy-start.6
  83.6 1.5 %copy-start.7 = (f32[43,2240]{1,0:T(8,128)S(1)}, f32[43,2240]{1,0:T(8,128)}, u32[]{:S(2)}) copy-start(f32[43,2240]{1,0:T(8,128)} %tile.49) | copy-start | bytes 1155844
  85.1 1.5 %copy-start.14 = (f32[128,32]{0,1:T(8,128)S(1)}, f32[128,32]{0,1:T(8,128)}, u32[]{:S(2)}) copy-start(f32[128,32]{0,1:T(8,128)} %param.15) | copy-start | bytes 49156
  85.1 1.5 %copy-start.17 = (f32[7,32]{0,1:T(8,128)S(1)}, f32[7,32]{0,1:T(8,128)}, u32[]{:S(2)}) copy-start(f32[7,32]{0,1:T(8,128)} %copy-done.16) | copy-start | bytes 2692
  85.1 1.5 %copy-start.19 = (f32[7,32]{0,1:T(8,128)S(1)}, f32[7,32]{0,1:T(8,128)}, u32[]{:S(2)}) copy-start(f32[7,32]{0,1:T(8,128)} %copy-done.18) | copy-start | bytes 2692
  85.6 2.7 %copy-start.23 = (f32[32,64]{1,0:T(8,128)S(1)}, f32[32,64]{1,0:T(8,128)}, u32[]{:S(2)}) copy-start(f32[32,64]{1,0:T(8,128)} %param.14) | copy-start | bytes 24580
  85.6 2.7 %copy-start.25 = (f32[7,64]{1,0:T(8,128)S(1)}, f32[7,64]{1,0:T(8,128)}, u32[]{:S(2)}) copy-start(f32[7,64]{1,0:T(8,128)} %copy-done.24) | copy-start | bytes 5380
  85.6 2.7 %copy-start.27 = (f32[7,64]{1,0:T(8,128)S(1)}, f32[7,64]{1,0:T(8,128)}, u32[]{:S(2)}) copy-start(f32[7,64]{1,0:T(8,128)} %copy-done.26) | copy-start | bytes 5380
  86.6 48.9 %copy-start.12 = (f32[16,64,32]{1,2,0:T(8,128)S(1)}, f32[16,64,32]{1,2,0:T(8,128)}, u32[]{:S(2)}) copy-start(f32[16,64,32]{1,2,0:T(8,128)} %param.16) | copy-start | bytes 393220
  129.8 13.4 %all-to-all-start.4 = ((f32[32,8,128]{2,1,0:T(8,128)}), f32[32,8,128]{2,1,0:T(8,128)S(1)}, u32[]{:S(2)}, u32[]{:S(2)}) async-start(f32[32,8,128]{2,1,0:T(8,128)} %broadcast_in_dim.23), calls=%async_computation.4 | async-start | bytes 262144 | tf_op jit(solution)/shard_map/all_to_all | solution.py:100
  (6 other events, 6.3 us)

commit v6 on v5

--- a/solution.py
+++ b/solution.py
@@ -116,18 +116,15 @@
 
 
 def adjoint_projection(adjoint_load, static_six, rows_six, cols_six, depth):
-    n_dirs = adjoint_load.shape[0]
     load_wide = pad_sides(adjoint_load, depth)
     tall, wide = load_wide.shape[1:]
-    load_flat = jnp.transpose(load_wide, (1, 0, 2)).reshape(tall, n_dirs * wide)
     ring = pad_sides(jnp.ones((tall - 2, wide - 2), jnp.float32), 1)
-    fields = jnp.tile(jnp.concatenate([static_six, ring[None]]), (1, 1, n_dirs))
-    diff, humid, couple = fields[0], fields[1], fields[2]
-    keep = fields[3] * fields[4]
+    diff, humid, couple = static_six[0], static_six[1], static_six[2]
+    keep = static_six[3] * ring
     diff_near = neighbours(diff)
-    temper = jnp.zeros_like(load_flat)
-    moist = load_flat
-    summed = load_flat
+    temper = jnp.zeros_like(load_wide)
+    moist = load_wide
+    summed = load_wide
     for i in range(depth - 1):
         lap_temp = sum((n - temper for n in neighbours(temper)))
         lap_hum = sum(
@@ -142,8 +139,7 @@
     gradient = diff * sum(
         (0.5 * (h - humid) * (lam - l) for h, l in zip(neighbours(humid), neighbours(lam)))
     )
-    gradient = gradient.reshape(tall, n_dirs, wide)
-    projected = jnp.einsum("xry,yb->rxb", gradient, cols_six, precision=exact)
+    projected = jnp.einsum("rxy,yb->rxb", gradient, cols_six, precision=exact)
     return jnp.einsum("xa,rxb->rab", rows_six, projected, precision=exact)
 
 

time: 146 us -> 137 us (0.938)
  local copies, waits for them, and re-layouts: 34.4 us -> 17.7 us
  waiting for transfers between devices: 13.8 us -> 22.6 us
  blocking collectives: 40 us -> 37.5 us
  other arithmetic: 19.7 us -> 21.5 us
    another operation x17 -> x2, local copies, waits for them, and re-layouts: 6.31 us -> 0.14 us  [the longest x15 6.25 us: adjoint_projection(): fields = jnp.tile(jnp.concatenate([static_six, ring[None]]), (1, 1, n_dirs))]
    all_to_all x1, waiting for transfers between devices: 1.07 us -> 6.82 us  [local(): lax.all_to_all(backward, 'gx', split_axis=1, concat_axis=1, tiled=True)]
    all_to_all x1, waiting for transfers between devices: 3.73 us -> 6.77 us  [local(): lax.all_to_all(picked, 'gx', split_axis=1, concat_axis=1, tiled=True)]
    all_to_all x1, blocking collectives: 13.8 us -> 11.3 us  [all_sum(): part = lax.all_to_all(flat, 'gx', 0, 0, tiled=True).sum(0)]
    unnamed x70 -> x24, local copies, waits for them, and re-layouts: 6.74 us -> 4.31 us
    slice x3 -> x0, local copies, waits for them, and re-layouts: 2.31 us -> none  [the longest x1 1.17 us: neighbours(): field[..., 1:, :]]
    slice x11 -> x10, local copies, waits for them, and re-layouts: 3.92 us -> 1.71 us  [neighbours(): field[..., :rows - 1, :]]
    mul x4 -> x3, other arithmetic: 2.82 us -> 3.96 us  [adjoint_projection(): (moist + step_ratio * lap_hum + couple * temper) * keep]
  transfers between devices with their start and end apart: 7 -> 7, of which waited for: 4 -> 4; matrix products, arithmetic and copies ran while one was open for 11% -> 5% of each run, Pallas kernels for 0% -> 0%
where the time goes in v6:
time: 137 us; the launch traced here: 136 us
  blocking collectives  37.5 us (27%)
  starting transfers between devices  30.1 us (22%)
  waiting for transfers between devices  22.6 us (16%)
  other arithmetic  21.5 us (16%)
  local copies, waits for them, and re-layouts  17.7 us (13%)
  matrix products  4.99 us (4%)
  between operations  1.37 us (1%)
    all_to_all x1, blocking collectives, all_sum(): part = lax.all_to_all(copies, 'gy', 0, 0, tiled=True).sum(0)  26.2 us
    all_to_all x1, blocking collectives, all_sum(): part = lax.all_to_all(flat, 'gx', 0, 0, tiled=True).sum(0)  11.3 us
    all_to_all x1, starting transfers between devices, local(): lax.all_to_all(picked, 'gx', split_axis=1, concat_axis=1, tiled=True)  7.65 us
    all_to_all x1, waiting for transfers between devices, all_sum(): lax.all_to_all(spread_out, 'gx', 0, 0, tiled=True).reshape(values.shape)  7.49 us
    all_to_all x1, waiting for transfers between devices, local(): lax.all_to_all(backward, 'gx', split_axis=1, concat_axis=1, tiled=True)  6.82 us
    ppermute x2, starting transfers between devices, exchange(): lax.ppermute(pack(heads), axis, [(i + 1, i) for i in range(ends)])  6.81 us
    all_to_all x1, waiting for transfers between devices, local(): lax.all_to_all(picked, 'gx', split_axis=1, concat_axis=1, tiled=True)  6.77 us
    ppermute x2, starting transfers between devices, exchange(): lax.ppermute(pack(tails), axis, [(i, i + 1) for i in range(ends)])  5.77 us
  transfers between devices with their start and end apart: 7, of which 4 were waited for; matrix products, arithmetic and copies ran while one was open for 5% of the time, Pallas kernels for 0%

profile of v6, /device:TPU:1, one launch (start us, length us, event | category | flops | bytes accessed | tf_op | source)
XLA Modules:
  0.0 135.7 jit_solution(3851397887004091223)
XLA Ops:
  0.7 0.8 pad_maximum_fusion.11
  2.3 4.5 %collective-permute-start = (f32[4032]{0:T(1024)S(1)}, f32[4032]{0:T(1024)S(1)}, u32[]{:S(2)}, u32[]{:S(2)}) collective-permute-start(f32[4032]{0:T(1024)S(1)} %pad_maximum_fusion.12), channel_id=1, source_target_pairs={{0,16},{16,32},{32,48},{48,64},{64,80},{80,96},{96,112},{112,128},... | collective-permute-start | bytes 48392 | tf_op jit(solution)/shard_map/ppermute | solution.py:85
  6.8 5.5 %collective-permute-start.1 = (f32[4032]{0:T(1024)S(1)}, f32[4032]{0:T(1024)S(1)}, u32[]{:S(2)}, u32[]{:S(2)}) collective-permute-start(f32[4032]{0:T(1024)S(1)} %pad_maximum_fusion.13), channel_id=1, source_target_pairs={{16,0},{32,16},{48,32},{64,48},{80,64},{96,80},{112,96},{128,112},... | collective-permute-start | bytes 48392 | tf_op jit(solution)/shard_map/ppermute | solution.py:86
  13.8 0.9 fusion.192
  16.0 0.8 copy.41
  18.0 1.3 collective-permute-start.2
  19.6 1.3 collective-permute-start.3
  21.1 1.3 fusion.158
  22.6 1.5 %collective-permute-done.3 = f32[1512]{0:T(1024)S(1)} collective-permute-done((f32[1512]{0:T(1024)S(1)}, f32[1512]{0:T(1024)S(1)}, u32[]{:S(2)}, u32[]{:S(2)}) %collective-permute-start.3) | collective-permute-done | bytes 6080 | tf_op jit(solution)/shard_map/ppermute | solution.py:86
  26.4 0.9 convolution_multiply_fusion
  27.3 0.9 broadcast_multiply_fusion
  28.2 0.9 multiply_multiply_fusion
  29.1 1.6 %fusion.67 = (f32[16,38,134]{2,1,0:T(8,128)S(1)}, f32[16,38,134]{2,1,0:T(8,128)S(1)}) fusion(f32[16,40,136]{2,1,0:T(8,128)S(1)} %get-tuple-element.16, f32[16,40,136]{2,1,0:T(8,128)S(1)} %get-tuple-element.17, f32[38,134]{1,0:T(8,128)S(1)} %get-tuple-element.84, f32[38,134]{1,0:T(8,128)S(1)} %get-tuple-element.85, f32[16,42,138]{2,1,0:T(8,128)S(1)} %get-tuple-element.11, ...), kind=kLoop, calls=%fused_computation.107 | loop fusion | flops 2444160 | bytes 4358752 | tf_op jit(solution)/shard_map/mul | solution.py:53
  30.7 1.6 %fusion.48 = (f32[16,36,132]{2,1,0:T(8,128)S(1)}, f32[16,36,132]{2,1,0:T(8,128)S(1)}) fusion(f32[16,38,134]{2,1,0:T(8,128)S(1)} %get-tuple-element.14, f32[16,38,134]{2,1,0:T(8,128)S(1)} %get-tuple-element.15, f32[36,132]{1,0:T(8,128)S(1)} %get-tuple-element.81, f32[36,132]{1,0:T(8,128)S(1)} %get-tuple-element.82, f32[16,42,138]{2,1,0:T(8,128)S(1)} %get-tuple-element.11, ...), kind=kLoop, calls=%fused_computation.79 | loop fusion | flops 2280960 | bytes 4067712 | tf_op jit(solution)/shard_map/mul | solution.py:53
  33.1 1.6 %fusion.43 = (f32[16,34,130]{2,1,0:T(8,128)S(1)}, f32[16,34,130]{2,1,0:T(8,128)S(1)}, f32[16,34,130]{2,1,0:T(8,128)S(1)}, f32[16,34,130]{2,1,0:T(8,128)S(1)}) fusion(f32[16,42,138]{2,1,0:T(8,128)S(1)} %get-tuple-element.11, f32[16,36,132]{2,1,0:T(8,128)S(1)} %get-tuple-element.13, f32[34,130]{1,0:T(8,128)S(1)} %get-tuple-element.78, ...), kind=kLoop, calls=%fused_computation.73 | loop fusion | flops 1555840 | bytes 4349280 | tf_op jit(solution)/shard_map/add | solution.py:179
  34.7 0.8 fusion.110
  37.8 7.7 %all-to-all-start = ((f32[32,1,128]{2,1,0:T(1,128)}), f32[32,1,128]{2,1,0:T(1,128)S(1)}, u32[]{:S(2)}, u32[]{:S(2)}) async-start(f32[32,1,128]{2,1,0:T(1,128)} %reshape.245), calls=%async_computation | async-start | bytes 32768 | tf_op jit(solution)/shard_map/all_to_all | solution.py:201
  45.6 6.8 %all-to-all-done = f32[32,1,128]{2,1,0:T(1,128)S(1)} async-done(((f32[32,1,128]{2,1,0:T(1,128)}), f32[32,1,128]{2,1,0:T(1,128)S(1)}, u32[]{:S(2)}, u32[]{:S(2)}) %all-to-all-start) | async-done | bytes 16416 | tf_op jit(solution)/shard_map/all_to_all | solution.py:201
  54.8 4.1 %all-to-all-start.1 = ((f32[32,1,128]{2,1,0:T(1,128)}), f32[32,1,128]{2,1,0:T(1,128)S(1)}, u32[]{:S(2)}, u32[]{:S(2)}) async-start(f32[32,1,128]{2,1,0:T(1,128)} %reshape.247), calls=%async_computation.1 | async-start | bytes 32768 | tf_op jit(solution)/shard_map/all_to_all | solution.py:207
  59.1 6.8 %all-to-all-done.1 = f32[32,1,128]{2,1,0:T(1,128)S(1)} async-done(((f32[32,1,128]{2,1,0:T(1,128)}), f32[32,1,128]{2,1,0:T(1,128)S(1)}, u32[]{:S(2)}, u32[]{:S(2)}) %all-to-all-start.1) | async-done | bytes 16416 | tf_op jit(solution)/shard_map/all_to_all | solution.py:207
  66.6 2.0 %scatter_custom_fusion = f32[16,4096]{0,1:T(8,128)S(1)} fusion(s32[256]{0:T(256)S(1)} %bitcast.160, f32[]{:T(128)} %constant.14.clone.1, f32[32,8]{1,0:T(8,128)S(1)} %copy.40, f32[32,8,16]{2,1,0:T(8,128)S(1)} %reshape.248), kind=kCustom, calls=%fused_computation.16 | custom fusion | flops 8192 | bytes 409604 | tf_op jit(solution)/shard_map/scatter-add | solution.py:210
  70.3 1.0 fusion.16
  71.8 1.1 add_multiply_fusion.2
  73.7 1.6 %add_multiply_fusion.1 = (f32[16,44,140]{2,1,0:T(8,128)S(1)}, f32[16,44,140]{2,1,0:T(8,128)S(1)}) fusion(f32[16,44,140]{2,1,0:T(8,128)S(1)} %add_multiply_fusion.2, f32[16,44,139]{2,1,0:T(8,128)S(1)} %get-tuple-element.45, f32[16,44,139]{2,1,0:T(8,128)S(1)} %get-tuple-element.44, f32[16,43,140]{2,1,0:T(8,128)S(1)} %get-tuple-element.43, ...), kind=kLoop, calls=%fused_computation.64 | loop fusion | flops 3449600 | bytes 5870464 | tf_op jit(solution)/shard_map/mul | solution.py:135
  76.2 1.3 add_multiply_fusion
  78.4 1.5 %fusion.14 = f32[16,44,140]{2,1,0:T(8,128)S(1)} fusion(f32[16,44,140]{2,1,0:T(8,128)S(1)} %get-tuple-element.6, f32[16,44,140]{2,1,0:T(8,128)S(1)} %get-tuple-element.8, f32[16,44,140]{2,1,0:T(8,128)S(1)} %add_multiply_fusion.2, f32[16,44,140]{2,1,0:T(8,128)S(1)} %get-tuple-element.55, f32[16,32,128]{2,1,0:T(8,128)S(1)} %copy.49, ...), kind=kLoop, calls=%fused_computation.30 | loop fusion | flops 3351040 | bytes 5882240 | tf_op jit(solution)/shard_map/mul | solution.py:138
  80.3 1.8 %fusion.25 = f32[16,44,32]{1,2,0:T(8,128)S(1)} fusion(f32[16,44,140]{2,1,0:T(8,128)S(1)} %fusion.14, f32[16,44,139]{2,1,0:T(8,128)S(1)} %get-tuple-element.21, f32[16,44,139]{2,1,0:T(8,128)S(1)} %get-tuple-element.20, f32[16,43,140]{2,1,0:T(8,128)S(1)} %get-tuple-element.19, f32[16,43,140]{2,1,0:T(8,128)S(1)} %get-tuple-element.18, ...), kind=kOutput, calls=%fused_computation.45 | convolution fusion | flops 39038720 | bytes 2179136 | tf_op jit(solution)/shard_map/rxy,yb->rxb/dot_general | solution.py:142
  82.9 11.3 %all_to_all.25 = f32[32,8,128]{2,1,0:T(8,128)S(1)} all-to-all(f32[32,8,128]{2,1,0:T(8,128)S(1)} %reshape_reshape.6), channel_id=1, replica_groups=mesh['gx'=32,'gy'=16] {'gx'}, dimensions={0} | all-to-all | bytes 262144 | tf_op jit(solution)/shard_map/all_to_all | solution.py:96
  94.3 26.2 %all_to_all.26 = f32[16,8,128]{2,1,0:T(8,128)S(1)} all-to-all(f32[16,8,128]{2,1,0:T(8,128)S(1)} %broadcast_in_dim.22), channel_id=1, replica_groups=mesh['gx'=32,'gy'=16] {'gy'}, dimensions={0} | all-to-all | bytes 131072 | tf_op jit(solution)/shard_map/all_to_all | solution.py:98
  121.1 5.7 %all-to-all-start.4 = ((f32[32,8,128]{2,1,0:T(8,128)}), f32[32,8,128]{2,1,0:T(8,128)S(1)}, u32[]{:S(2)}, u32[]{:S(2)}) async-start(f32[32,8,128]{2,1,0:T(8,128)} %broadcast_in_dim.23), calls=%async_computation.4 | async-start | bytes 262144 | tf_op jit(solution)/shard_map/all_to_all | solution.py:100
  127.1 7.5 %all-to-all-done.4 = f32[32,8,128]{2,1,0:T(8,128)S(1)} async-done(((f32[32,8,128]{2,1,0:T(8,128)}), f32[32,8,128]{2,1,0:T(8,128)S(1)}, u32[]{:S(2)}, u32[]{:S(2)}) %all-to-all-start.4) | async-done | bytes 131104 | tf_op jit(solution)/shard_map/all_to_all | solution.py:100
  134.8 0.9 copy.46
  (124 shorter events, 20.8 us)
Async XLA Ops:
  0.6 23.7 %copy-start.4 = (f32[32,128]{1,0:T(8,128)S(1)}, f32[32,128]{1,0:T(8,128)}, u32[]{:S(2)}) copy-start(f32[32,128]{1,0:T(8,128)} %param.11) | copy-start | bytes 49156
  0.6 23.7 %copy-start.3 = (f32[32,128]{1,0:T(8,128)S(1)}, f32[32,128]{1,0:T(8,128)}, u32[]{:S(2)}) copy-start(f32[32,128]{1,0:T(8,128)} %param.12) | copy-start | bytes 49156
  0.7 23.7 %copy-start.2 = (f32[32,128]{1,0:T(8,128)S(1)}, f32[32,128]{1,0:T(8,128)}, u32[]{:S(2)}) copy-start(f32[32,128]{1,0:T(8,128)} %param.13) | copy-start | bytes 49156
  2.3 14.6 %collective-permute-start = (f32[4032]{0:T(1024)S(1)}, f32[4032]{0:T(1024)S(1)}, u32[]{:S(2)}, u32[]{:S(2)}) collective-permute-start(f32[4032]{0:T(1024)S(1)} %pad_maximum_fusion.12), channel_id=1, source_target_pairs={{0,16},{16,32},{32,48},{48,64},{64,80},{80,96},{96,112},{112,128},... | collective-permute-start | bytes 48392 | tf_op jit(solution)/shard_map/ppermute | solution.py:85
  6.8 10.0 %collective-permute-start.1 = (f32[4032]{0:T(1024)S(1)}, f32[4032]{0:T(1024)S(1)}, u32[]{:S(2)}, u32[]{:S(2)}) collective-permute-start(f32[4032]{0:T(1024)S(1)} %pad_maximum_fusion.13), channel_id=1, source_target_pairs={{16,0},{32,16},{48,32},{64,48},{80,64},{96,80},{112,96},{128,112},... | collective-permute-start | bytes 48392 | tf_op jit(solution)/shard_map/ppermute | solution.py:86
  18.0 4.4 %collective-permute-start.2 = (f32[1512]{0:T(1024)S(1)}, f32[1512]{0:T(1024)S(1)}, u32[]{:S(2)}, u32[]{:S(2)}) collective-permute-start(f32[1512]{0:T(1024)S(1)} %pad_maximum_fusion.14), channel_id=1, source_target_pairs={{0,1},{1,2},{2,3},{3,4},{4,5},{5,6},{6,7},{7,8},{8,9},{9,10},{10,1... | collective-permute-start | bytes 18152 | tf_op jit(solution)/shard_map/ppermute | solution.py:85
  19.6 4.5 %collective-permute-start.3 = (f32[1512]{0:T(1024)S(1)}, f32[1512]{0:T(1024)S(1)}, u32[]{:S(2)}, u32[]{:S(2)}) collective-permute-start(f32[1512]{0:T(1024)S(1)} %pad_maximum_fusion.15), channel_id=1, source_target_pairs={{1,0},{2,1},{3,2},{4,3},{5,4},{6,5},{7,6},{8,7},{9,8},{10,9},{11,1... | collective-permute-start | bytes 18152 | tf_op jit(solution)/shard_map/ppermute | solution.py:86
  24.4 2.0 %copy-start.1 = (f32[128,32]{0,1:T(8,128)S(1)}, f32[128,32]{0,1:T(8,128)}, u32[]{:S(2)}) copy-start(f32[128,32]{0,1:T(8,128)} %param.15) | copy-start | bytes 49156
  35.6 18.3 %copy-start.7 = (f32[1,1,40]{2,1,0:T(1,128)S(1)}, f32[1,1,40]{2,1,0:T(1,128)}, u32[]{:S(2)}) copy-start(f32[1,1,40]{2,1,0:T(1,128)} %param.21) | copy-start | bytes 484
  37.8 14.6 %all-to-all-start = ((f32[32,1,128]{2,1,0:T(1,128)}), f32[32,1,128]{2,1,0:T(1,128)S(1)}, u32[]{:S(2)}, u32[]{:S(2)}) async-start(f32[32,1,128]{2,1,0:T(1,128)} %reshape.245), calls=%async_computation | async-start | bytes 32768 | tf_op jit(solution)/shard_map/all_to_all | solution.py:201
  53.8 15.5 %copy-start.6 = (f32[16,40]{1,0:T(8,128)}, f32[16,40]{1,0:T(8,128)S(1)}, u32[]{:S(2)}) copy-start(f32[16,40]{1,0:T(8,128)S(1)} %fusion.129) | copy-start | bytes 7684
  54.8 11.1 %all-to-all-start.1 = ((f32[32,1,128]{2,1,0:T(1,128)}), f32[32,1,128]{2,1,0:T(1,128)S(1)}, u32[]{:S(2)}, u32[]{:S(2)}) async-start(f32[32,1,128]{2,1,0:T(1,128)} %reshape.247), calls=%async_computation.1 | async-start | bytes 32768 | tf_op jit(solution)/shard_map/all_to_all | solution.py:207
  80.3 1.9 %copy-start.5 = (f32[32,64]{1,0:T(8,128)S(1)}, f32[32,64]{1,0:T(8,128)}, u32[]{:S(2)}) copy-start(f32[32,64]{1,0:T(8,128)} %param.14) | copy-start | bytes 24580
  82.1 44.7 %copy-start = (f32[16,64,32]{1,2,0:T(8,128)S(1)}, f32[16,64,32]{1,2,0:T(8,128)}, u32[]{:S(2)}) copy-start(f32[16,64,32]{1,2,0:T(8,128)} %param.16) | copy-start | bytes 393220
  121.1 13.4 %all-to-all-start.4 = ((f32[32,8,128]{2,1,0:T(8,128)}), f32[32,8,128]{2,1,0:T(8,128)S(1)}, u32[]{:S(2)}, u32[]{:S(2)}) async-start(f32[32,8,128]{2,1,0:T(8,128)} %broadcast_in_dim.23), calls=%async_computation.4 | async-start | bytes 262144 | tf_op jit(solution)/shard_map/all_to_all | solution.py:100

commit v7 on v4

--- a/solution.py
+++ b/solution.py
@@ -121,9 +121,22 @@
     reach = rim_depth + 1
     height, breadth = diffusivity.shape
     n_dirs = directions.shape[0]
-    static = jnp.stack([diffusivity, base_humidity, coupling, jnp.ones_like(diffusivity)])
-    static_gx, rows_wide = exchange(((static, 1), (basis_rows, 0)), "gx", reach)
-    static_wide, cols_wide = exchange(((static_gx, 2), (basis_cols, 0)), "gy", reach)
+    static = jnp.stack([diffusivity, base_humidity, coupling])
+    static_gy, cols_wide = exchange(((static, 2), (basis_cols, 0)), "gy", reach)
+    static_both, rows_wide = exchange(((static_gy, 1), (basis_rows, 0)), "gx", reach)
+    row_at = lax.axis_index("gx") * height - reach + lax.broadcasted_iota(
+        jnp.int32, (height + 2 * reach, breadth + 2 * reach), 0
+    )
+    col_at = lax.axis_index("gy") * breadth - reach + lax.broadcasted_iota(
+        jnp.int32, (height + 2 * reach, breadth + 2 * reach), 1
+    )
+    inside_grid = (
+        (row_at >= 0)
+        & (row_at < height * lax.axis_size("gx"))
+        & (col_at >= 0)
+        & (col_at < breadth * lax.axis_size("gy"))
+    ).astype(jnp.float32)
+    static_wide = jnp.concatenate([static_both, inside_grid[None]])
     static_six = window(static_wide, reach, rim_depth)
     rows_six = rows_wide[1:-1]
     cols_six = cols_wide[1:-1]

time: 137 us -> 140 us (1.022)
  blocking collectives: 37.5 us -> 39.3 us
    ppermute x2, starting transfers between devices: 5.77 us -> 8.62 us  [exchange(): lax.ppermute(pack(tails), axis, [(i, i + 1) for i in range(ends)])]
    ppermute x2, starting transfers between devices: 6.81 us -> 4.28 us  [exchange(): lax.ppermute(pack(heads), axis, [(i + 1, i) for i in range(ends)])]
    all_to_all x1, blocking collectives: 26.2 us -> 27.9 us  [all_sum(): part = lax.all_to_all(copies, 'gy', 0, 0, tiled=True).sum(0)]
    unnamed x24 -> x26, local copies, waits for them, and re-layouts: 4.3 us -> 3.62 us
  transfers between devices with their start and end apart: 7 -> 7, of which waited for: 4 -> 4; matrix products, arithmetic and copies ran while one was open for 5% -> 4% of each run, Pallas kernels for 0% -> 0%
where the time goes in v7:
time: 140 us; the launch traced here: 139 us
  blocking collectives  39.3 us (28%)
  starting transfers between devices  31.5 us (22%)
  other arithmetic  26.4 us (19%)
  waiting for transfers between devices  22.2 us (16%)
  local copies, waits for them, and re-layouts  13.7 us (10%)
  matrix products  4.29 us (3%)
    all_to_all x1, blocking collectives, all_sum(): part = lax.all_to_all(copies, 'gy', 0, 0, tiled=True).sum(0)  27.9 us
    all_to_all x1, blocking collectives, all_sum(): part = lax.all_to_all(flat, 'gx', 0, 0, tiled=True).sum(0)  11.3 us
    another operation x9, other arithmetic, advance(): return jnp.stack([new_temp * inside, new_hum * inside])  10 us
    all_to_all x1, starting transfers between devices, local(): lax.all_to_all(picked, 'gx', split_axis=1, concat_axis=1, tiled=True)  8.76 us
    ppermute x2, starting transfers between devices, exchange(): lax.ppermute(pack(tails), axis, [(i, i + 1) for i in range(ends)])  8.62 us
    all_to_all x1, waiting for transfers between devices, all_sum(): lax.all_to_all(spread_out, 'gx', 0, 0, tiled=True).reshape(values.shape)  7.5 us
    all_to_all x1, waiting for transfers between devices, local(): lax.all_to_all(backward, 'gx', split_axis=1, concat_axis=1, tiled=True)  6.91 us
    all_to_all x1, waiting for transfers between devices, local(): lax.all_to_all(picked, 'gx', split_axis=1, concat_axis=1, tiled=True)  6.76 us
  transfers between devices with their start and end apart: 7, of which 4 were waited for; matrix products, arithmetic and copies ran while one was open for 4% of the time, Pallas kernels for 0%

profile of v7, /device:TPU:1, one launch (start us, length us, event | category | flops | bytes accessed | tf_op | source)
XLA Modules:
  0.0 138.6 jit_solution(10729923048715141564)
XLA Ops:
  0.7 0.8 pad_maximum_fusion.1
  1.7 0.9 fusion.283
  2.8 4.4 %collective-permute-start = (f32[896]{0:T(1024)S(1)}, f32[896]{0:T(1024)S(1)}, u32[]{:S(2)}, u32[]{:S(2)}) collective-permute-start(f32[896]{0:T(1024)S(1)} %pad_maximum_fusion.15), channel_id=1, source_target_pairs={{0,1},{1,2},{2,3},{3,4},{4,5},{5,6},{6,7},{7,8},{8,9},{9,10},{10,1... | collective-permute-start | bytes 10760 | tf_op jit(solution)/shard_map/ppermute | solution.py:85
  7.6 1.3 collective-permute-start.1
  9.5 0.8 copy.38
  12.9 0.9 pad_maximum_fusion.10
  14.0 4.3 %collective-permute-start.2 = (f32[3430]{0:T(1024)S(1)}, f32[3430]{0:T(1024)S(1)}, u32[]{:S(2)}, u32[]{:S(2)}) collective-permute-start(f32[3430]{0:T(1024)S(1)} %pad_maximum_fusion.13), channel_id=1, source_target_pairs={{0,16},{16,32},{32,48},{48,64},{64,80},{80,96},{96,112},{112,128},... | collective-permute-start | bytes 41168 | tf_op jit(solution)/shard_map/ppermute | solution.py:85
  18.4 3.0 %collective-permute-start.3 = (f32[3430]{0:T(1024)S(1)}, f32[3430]{0:T(1024)S(1)}, u32[]{:S(2)}, u32[]{:S(2)}) collective-permute-start(f32[3430]{0:T(1024)S(1)} %pad_maximum_fusion.14), channel_id=1, source_target_pairs={{16,0},{32,16},{48,32},{64,48},{80,64},{96,80},{112,96},{128,112},... | collective-permute-start | bytes 41168 | tf_op jit(solution)/shard_map/ppermute | solution.py:86
  22.5 1.0 collective-permute-done.3
  25.7 0.9 convolution_multiply_fusion
  26.6 0.9 broadcast_multiply_fusion
  27.5 0.9 multiply_multiply_fusion
  28.5 1.6 %fusion.164 = (f32[16,38,134]{2,1,0:T(8,128)S(1)}, f32[16,38,134]{2,1,0:T(8,128)S(1)}) fusion(f32[16,40,136]{2,1,0:T(8,128)S(1)} %get-tuple-element.28, f32[16,40,136]{2,1,0:T(8,128)S(1)} %get-tuple-element.29, f32[38,134]{1,0:T(8,128)S(1)} %slice_bitcast_fusion.20, f32[38,134]{1,0:T(8,128)S(1)} %get-tuple-element.43, ...), kind=kLoop, calls=%fused_computation.248 | loop fusion | flops 2444160 | bytes 4358752 | tf_op jit(solution)/shard_map/mul | solution.py:53
  30.1 1.6 %fusion.145 = (f32[16,36,132]{2,1,0:T(8,128)S(1)}, f32[16,36,132]{2,1,0:T(8,128)S(1)}) fusion(f32[16,38,134]{2,1,0:T(8,128)S(1)} %get-tuple-element.26, f32[16,38,134]{2,1,0:T(8,128)S(1)} %get-tuple-element.27, f32[36,132]{1,0:T(8,128)S(1)} %slice_bitcast_fusion.17, f32[36,132]{1,0:T(8,128)S(1)} %get-tuple-element.41, ...), kind=kLoop, calls=%fused_computation.220 | loop fusion | flops 2280960 | bytes 4067712 | tf_op jit(solution)/shard_map/mul | solution.py:53
  32.4 1.6 %fusion.140 = (f32[16,34,130]{2,1,0:T(8,128)S(1)}, f32[16,34,130]{2,1,0:T(8,128)S(1)}, f32[16,34,130]{2,1,0:T(8,128)S(1)}, f32[16,34,130]{2,1,0:T(8,128)S(1)}) fusion(f32[16,42,138]{2,1,0:T(8,128)S(1)} %get-tuple-element.7, f32[16,36,132]{2,1,0:T(8,128)S(1)} %get-tuple-element.25, f32[34,130]{1,0:T(8,128)S(1)} %slice_bitcast_fusion.14, ...), kind=kLoop, calls=%fused_computation.214 | loop fusion | flops 1555840 | bytes 4349280 | tf_op jit(solution)/shard_map/add | solution.py:153
  34.0 0.8 fusion.207
  37.1 8.8 %all-to-all-start = ((f32[32,1,128]{2,1,0:T(1,128)}), f32[32,1,128]{2,1,0:T(1,128)S(1)}, u32[]{:S(2)}, u32[]{:S(2)}) async-start(f32[32,1,128]{2,1,0:T(1,128)} %reshape.325), calls=%async_computation | async-start | bytes 32768 | tf_op jit(solution)/shard_map/all_to_all | solution.py:175
  46.0 6.8 %all-to-all-done = f32[32,1,128]{2,1,0:T(1,128)S(1)} async-done(((f32[32,1,128]{2,1,0:T(1,128)}), f32[32,1,128]{2,1,0:T(1,128)S(1)}, u32[]{:S(2)}, u32[]{:S(2)}) %all-to-all-start) | async-done | bytes 16416 | tf_op jit(solution)/shard_map/all_to_all | solution.py:175
  55.4 4.1 %all-to-all-start.1 = ((f32[32,1,128]{2,1,0:T(1,128)}), f32[32,1,128]{2,1,0:T(1,128)S(1)}, u32[]{:S(2)}, u32[]{:S(2)}) async-start(f32[32,1,128]{2,1,0:T(1,128)} %reshape.327), calls=%async_computation.1 | async-start | bytes 32768 | tf_op jit(solution)/shard_map/all_to_all | solution.py:181
  59.7 6.9 %all-to-all-done.1 = f32[32,1,128]{2,1,0:T(1,128)S(1)} async-done(((f32[32,1,128]{2,1,0:T(1,128)}), f32[32,1,128]{2,1,0:T(1,128)S(1)}, u32[]{:S(2)}, u32[]{:S(2)}) %all-to-all-start.1) | async-done | bytes 16416 | tf_op jit(solution)/shard_map/all_to_all | solution.py:181
  67.4 2.0 %scatter_custom_fusion = f32[16,4096]{0,1:T(8,128)S(1)} fusion(s32[256]{0:T(256)S(1)} %bitcast.180, f32[]{:T(128)} %constant.29.clone.1, f32[32,8]{1,0:T(8,128)S(1)} %copy.40, f32[32,8,16]{2,1,0:T(8,128)S(1)} %reshape.328), kind=kCustom, calls=%fused_computation.26 | custom fusion | flops 8192 | bytes 409604 | tf_op jit(solution)/shard_map/scatter-add | solution.py:184
  70.1 1.1 multiply_bitcast_fusion
  71.8 1.7 %fusion.107 = (f32[1,16,42,138]{3,2,1,0:T(8,128)S(1)}, f32[1,16,42,138]{3,2,1,0:T(8,128)S(1)}) fusion(f32[16,44,140]{2,1,0:T(8,128)S(1)} %get-tuple-element.22, f32[16,44,140]{2,1,0:T(8,128)S(1)} %get-tuple-element.23, f32[42,138]{1,0:T(8,128)S(1)} %get-tuple-element.36, f32[42,138]{1,0:T(8,128)S(1)} %slice_bitcast_fusion.10, ...), kind=kLoop, calls=%fused_computation.167 | loop fusion | flops 2596608 | bytes 4590432 | tf_op jit(solution)/shard_map/stack | solution.py:53
  74.2 1.7 %fusion.87 = (f32[1,16,42,138]{3,2,1,0:T(8,128)S(1)}, f32[1,16,42,138]{3,2,1,0:T(8,128)S(1)}) fusion(f32[16,44,140]{2,1,0:T(8,128)S(1)} %get-tuple-element.20, f32[16,44,140]{2,1,0:T(8,128)S(1)} %get-tuple-element.21, f32[42,138]{1,0:T(8,128)S(1)} %get-tuple-element.36, f32[42,138]{1,0:T(8,128)S(1)} %slice_bitcast_fusion.10, ...), kind=kLoop, calls=%fused_computation.137 | loop fusion | flops 2596608 | bytes 4590432 | tf_op jit(solution)/shard_map/stack | solution.py:53
  76.5 1.7 %fusion.67 = (f32[1,16,42,138]{3,2,1,0:T(8,128)S(1)}, f32[1,16,42,138]{3,2,1,0:T(8,128)S(1)}) fusion(f32[16,44,140]{2,1,0:T(8,128)S(1)} %get-tuple-element.18, f32[16,44,140]{2,1,0:T(8,128)S(1)} %get-tuple-element.19, f32[42,138]{1,0:T(8,128)S(1)} %get-tuple-element.36, f32[42,138]{1,0:T(8,128)S(1)} %slice_bitcast_fusion.10, ...), kind=kLoop, calls=%fused_computation.107 | loop fusion | flops 2596608 | bytes 4590432 | tf_op jit(solution)/shard_map/stack | solution.py:53
  78.9 1.7 %fusion.47 = (f32[1,16,42,138]{3,2,1,0:T(8,128)S(1)}, f32[1,16,42,138]{3,2,1,0:T(8,128)S(1)}) fusion(f32[16,44,140]{2,1,0:T(8,128)S(1)} %get-tuple-element.16, f32[16,44,140]{2,1,0:T(8,128)S(1)} %get-tuple-element.17, f32[42,138]{1,0:T(8,128)S(1)} %get-tuple-element.36, f32[42,138]{1,0:T(8,128)S(1)} %slice_bitcast_fusion.10, ...), kind=kLoop, calls=%fused_computation.77 | loop fusion | flops 2596608 | bytes 4590432 | tf_op jit(solution)/shard_map/stack | solution.py:53
  81.2 2.1 %fusion.118 = f32[16,44,32]{1,2,0:T(8,128)S(1)} fusion(f32[16,44,140]{2,1,0:T(8,128)S(1)} %fusion.25, f32[44,140]{1,0:T(8,128)S(1)} %get-tuple-element.53, f32[44,140]{1,0:T(8,128)S(1)} %get-tuple-element.51, f32[44,140]{1,0:T(8,128)S(1)} %get-tuple-element.52, f32[44,140]{1,0:T(8,128)S(1)} %get-tuple-element.50, f32[44,140]{1,0:T(8,128)S(1)} %get-tuple-element.46, ...), kind=kOutput, calls=%fused_computation.187 | convolution fusion | flops 39038720 | bytes 625728 | tf_op jit(solution)/shard_map/rxy,yb->rxb/dot_general | solution.py:198
  84.0 11.3 %all_to_all.25 = f32[32,8,128]{2,1,0:T(8,128)S(1)} all-to-all(f32[32,8,128]{2,1,0:T(8,128)S(1)} %reshape_reshape.6), channel_id=1, replica_groups=mesh['gx'=32,'gy'=16] {'gx'}, dimensions={0} | all-to-all | bytes 262144 | tf_op jit(solution)/shard_map/all_to_all | solution.py:96
  95.4 27.9 %all_to_all.26 = f32[16,8,128]{2,1,0:T(8,128)S(1)} all-to-all(f32[16,8,128]{2,1,0:T(8,128)S(1)} %broadcast_in_dim.16), channel_id=1, replica_groups=mesh['gx'=32,'gy'=16] {'gy'}, dimensions={0} | all-to-all | bytes 131072 | tf_op jit(solution)/shard_map/all_to_all | solution.py:98
  124.0 5.7 %all-to-all-start.4 = ((f32[32,8,128]{2,1,0:T(8,128)}), f32[32,8,128]{2,1,0:T(8,128)S(1)}, u32[]{:S(2)}, u32[]{:S(2)}) async-start(f32[32,8,128]{2,1,0:T(8,128)} %broadcast_in_dim.17), calls=%async_computation.4 | async-start | bytes 262144 | tf_op jit(solution)/shard_map/all_to_all | solution.py:100
  130.0 7.5 %all-to-all-done.4 = f32[32,8,128]{2,1,0:T(8,128)S(1)} async-done(((f32[32,8,128]{2,1,0:T(8,128)}), f32[32,8,128]{2,1,0:T(8,128)S(1)}, u32[]{:S(2)}, u32[]{:S(2)}) %all-to-all-start.4) | async-done | bytes 131104 | tf_op jit(solution)/shard_map/all_to_all | solution.py:100
  137.7 0.9 copy.46
  (124 shorter events, 19.7 us)
Async XLA Ops:
  0.6 23.0 %copy-start.4 = (f32[32,128]{1,0:T(8,128)S(1)}, f32[32,128]{1,0:T(8,128)}, u32[]{:S(2)}) copy-start(f32[32,128]{1,0:T(8,128)} %param.11) | copy-start | bytes 49156
  0.6 23.0 %copy-start.3 = (f32[32,128]{1,0:T(8,128)S(1)}, f32[32,128]{1,0:T(8,128)}, u32[]{:S(2)}) copy-start(f32[32,128]{1,0:T(8,128)} %param.12) | copy-start | bytes 49156
  0.7 23.0 %copy-start.1 = (f32[32,128]{1,0:T(8,128)S(1)}, f32[32,128]{1,0:T(8,128)}, u32[]{:S(2)}) copy-start(f32[32,128]{1,0:T(8,128)} %param.13) | copy-start | bytes 49156
  0.7 21.0 %copy-start.7 = (s32[1,1,32,8]{2,3,1,0:T(8,128)S(1)}, s32[1,1,32,8]{2,3,1,0:T(8,128)}, u32[]{:S(2)}) copy-start(s32[1,1,32,8]{2,3,1,0:T(8,128)} %param.20) | copy-start | bytes 3076
  2.8 9.8 %collective-permute-start = (f32[896]{0:T(1024)S(1)}, f32[896]{0:T(1024)S(1)}, u32[]{:S(2)}, u32[]{:S(2)}) collective-permute-start(f32[896]{0:T(1024)S(1)} %pad_maximum_fusion.15), channel_id=1, source_target_pairs={{0,1},{1,2},{2,3},{3,4},{4,5},{5,6},{6,7},{7,8},{8,9},{9,10},{10,1... | collective-permute-start | bytes 10760 | tf_op jit(solution)/shard_map/ppermute | solution.py:85
  7.6 5.2 %collective-permute-start.1 = (f32[896]{0:T(1024)S(1)}, f32[896]{0:T(1024)S(1)}, u32[]{:S(2)}, u32[]{:S(2)}) collective-permute-start(f32[896]{0:T(1024)S(1)} %pad_maximum_fusion.16), channel_id=1, source_target_pairs={{1,0},{2,1},{3,2},{4,3},{5,4},{6,5},{7,6},{8,7},{9,8},{10,9},{11,1... | collective-permute-start | bytes 10760 | tf_op jit(solution)/shard_map/ppermute | solution.py:86
  14.0 8.4 %collective-permute-start.2 = (f32[3430]{0:T(1024)S(1)}, f32[3430]{0:T(1024)S(1)}, u32[]{:S(2)}, u32[]{:S(2)}) collective-permute-start(f32[3430]{0:T(1024)S(1)} %pad_maximum_fusion.13), channel_id=1, source_target_pairs={{0,16},{16,32},{32,48},{48,64},{64,80},{80,96},{96,112},{112,128},... | collective-permute-start | bytes 41168 | tf_op jit(solution)/shard_map/ppermute | solution.py:85
  18.4 5.0 %collective-permute-start.3 = (f32[3430]{0:T(1024)S(1)}, f32[3430]{0:T(1024)S(1)}, u32[]{:S(2)}, u32[]{:S(2)}) collective-permute-start(f32[3430]{0:T(1024)S(1)} %pad_maximum_fusion.14), channel_id=1, source_target_pairs={{16,0},{32,16},{48,32},{64,48},{80,64},{96,80},{112,96},{128,112},... | collective-permute-start | bytes 41168 | tf_op jit(solution)/shard_map/ppermute | solution.py:86
  24.1 1.3 copy-start
  24.1 1.3 copy-start.5
  24.4 1.4 copy-start.2
  34.9 19.6 %copy-start.8 = (f32[1,1,40]{2,1,0:T(1,128)S(1)}, f32[1,1,40]{2,1,0:T(1,128)}, u32[]{:S(2)}) copy-start(f32[1,1,40]{2,1,0:T(1,128)} %param.21) | copy-start | bytes 484
  37.1 15.7 %all-to-all-start = ((f32[32,1,128]{2,1,0:T(1,128)}), f32[32,1,128]{2,1,0:T(1,128)S(1)}, u32[]{:S(2)}, u32[]{:S(2)}) async-start(f32[32,1,128]{2,1,0:T(1,128)} %reshape.325), calls=%async_computation | async-start | bytes 32768 | tf_op jit(solution)/shard_map/all_to_all | solution.py:175
  54.4 15.6 %copy-start.6 = (f32[16,40]{1,0:T(8,128)}, f32[16,40]{1,0:T(8,128)S(1)}, u32[]{:S(2)}) copy-start(f32[16,40]{1,0:T(8,128)S(1)} %fusion.227) | copy-start | bytes 7684
  55.4 11.1 %all-to-all-start.1 = ((f32[32,1,128]{2,1,0:T(1,128)}), f32[32,1,128]{2,1,0:T(1,128)S(1)}, u32[]{:S(2)}, u32[]{:S(2)}) async-start(f32[32,1,128]{2,1,0:T(1,128)} %reshape.327), calls=%async_computation.1 | async-start | bytes 32768 | tf_op jit(solution)/shard_map/all_to_all | solution.py:181
  124.0 13.4 %all-to-all-start.4 = ((f32[32,8,128]{2,1,0:T(8,128)}), f32[32,8,128]{2,1,0:T(8,128)S(1)}, u32[]{:S(2)}, u32[]{:S(2)}) async-start(f32[32,8,128]{2,1,0:T(8,128)} %broadcast_in_dim.17), calls=%async_computation.4 | async-start | bytes 262144 | tf_op jit(solution)/shard_map/all_to_all | solution.py:100

commit v8 on v4

--- a/solution.py
+++ b/solution.py
@@ -148,6 +148,9 @@
         lax.broadcasted_iota(jnp.int32, (peers, slots), 1) < send_count.reshape(peers, 1)
     ).astype(jnp.float32)
     factor = send_weight.reshape(peers, slots) * live_mask
+    select = (
+        cell_ids[:, None] == lax.broadcasted_iota(jnp.int32, (1, height * breadth), 1)
+    ).astype(jnp.float32)
     picked = (
         jnp.take(humid.reshape(n_dirs, height * breadth), cell_ids, axis=1).reshape(
             n_dirs, peers, slots
@@ -167,9 +170,7 @@
     )
     returned = lax.all_to_all(backward, "gx", split_axis=1, concat_axis=1, tiled=True)
     load_values = (returned * factor).reshape(n_dirs, peers * slots)
-    adjoint_load = (
-        jnp.zeros((n_dirs, height * breadth), jnp.float32).at[:, cell_ids].add(load_values)
-    )
+    adjoint_load = jnp.dot(load_values, select, precision=exact)
     load_wide = pad_sides(adjoint_load.reshape(n_dirs, height, breadth), rim_depth)
     state_now = jnp.stack([jnp.zeros_like(load_wide), load_wide])
     summed = load_wide

time: 137 us -> 138 us (level)
  matrix products: 5 us -> 7.18 us
  other arithmetic: 26 us -> 24.3 us
    dot_general x0 -> x1, matrix products: none -> 2.41 us  [local(): adjoint_load = jnp.dot(load_values, select, precision=exact)]
    scatter-add x1 -> x0, other arithmetic: 2.03 us -> none  [local(): jnp.zeros((n_dirs, height * breadth), jnp.float32).at[:, cell_ids]]
where the time goes in v8:
time: 138 us; the launch traced here: 136 us
  blocking collectives  37.5 us (27%)
  starting transfers between devices  30.2 us (22%)
  other arithmetic  24.3 us (18%)
  waiting for transfers between devices  22.8 us (17%)
  local copies, waits for them, and re-layouts  13.1 us (9%)
  matrix products  7.18 us (5%)
    all_to_all x1, blocking collectives, all_sum(): part = lax.all_to_all(copies, 'gy', 0, 0, tiled=True).sum(0)  26.2 us
    all_to_all x1, blocking collectives, all_sum(): part = lax.all_to_all(flat, 'gx', 0, 0, tiled=True).sum(0)  11.3 us
    another operation x9, other arithmetic, advance(): return jnp.stack([new_temp * inside, new_hum * inside])  10.2 us
    all_to_all x1, starting transfers between devices, local(): lax.all_to_all(picked, 'gx', split_axis=1, concat_axis=1, tiled=True)  7.64 us
    all_to_all x1, waiting for transfers between devices, all_sum(): lax.all_to_all(spread_out, 'gx', 0, 0, tiled=True).reshape(values.shape)  7.5 us
    ppermute x2, starting transfers between devices, exchange(): lax.ppermute(pack(heads), axis, [(i + 1, i) for i in range(ends)])  6.81 us
    all_to_all x1, waiting for transfers between devices, local(): lax.all_to_all(picked, 'gx', split_axis=1, concat_axis=1, tiled=True)  6.76 us
    all_to_all x1, waiting for transfers between devices, local(): lax.all_to_all(backward, 'gx', split_axis=1, concat_axis=1, tiled=True)  6.73 us
  transfers between devices with their start and end apart: 7, of which 4 were waited for; matrix products, arithmetic and copies ran while one was open for 5% of the time, Pallas kernels for 0%

profile of v8, /device:TPU:1, one launch (start us, length us, event | category | flops | bytes accessed | tf_op | source)
XLA Modules:
  0.0 136.4 jit_solution(4584087973426716807)
XLA Ops:
  0.7 0.8 pad_maximum_fusion.11
  2.3 4.5 %collective-permute-start = (f32[4032]{0:T(1024)S(1)}, f32[4032]{0:T(1024)S(1)}, u32[]{:S(2)}, u32[]{:S(2)}) collective-permute-start(f32[4032]{0:T(1024)S(1)} %pad_maximum_fusion.12), channel_id=1, source_target_pairs={{0,16},{16,32},{32,48},{48,64},{64,80},{80,96},{96,112},{112,128},... | collective-permute-start | bytes 48392 | tf_op jit(solution)/shard_map/ppermute | solution.py:85
  6.9 5.5 %collective-permute-start.1 = (f32[4032]{0:T(1024)S(1)}, f32[4032]{0:T(1024)S(1)}, u32[]{:S(2)}, u32[]{:S(2)}) collective-permute-start(f32[4032]{0:T(1024)S(1)} %pad_maximum_fusion.13), channel_id=1, source_target_pairs={{16,0},{32,16},{48,32},{64,48},{80,64},{96,80},{112,96},{128,112},... | collective-permute-start | bytes 48392 | tf_op jit(solution)/shard_map/ppermute | solution.py:86
  13.9 0.9 fusion.281
  16.1 0.8 copy.42
  18.2 1.3 collective-permute-start.2
  19.8 1.3 collective-permute-start.3
  21.2 1.1 fusion.265
  22.5 1.8 %collective-permute-done.3 = f32[1512]{0:T(1024)S(1)} collective-permute-done((f32[1512]{0:T(1024)S(1)}, f32[1512]{0:T(1024)S(1)}, u32[]{:S(2)}, u32[]{:S(2)}) %collective-permute-start.3) | collective-permute-done | bytes 6080 | tf_op jit(solution)/shard_map/ppermute | solution.py:86
  26.5 0.9 convolution_multiply_fusion
  27.4 0.9 broadcast_multiply_fusion
  28.3 0.9 multiply_multiply_fusion
  29.2 1.6 %fusion.166 = (f32[16,38,134]{2,1,0:T(8,128)S(1)}, f32[16,38,134]{2,1,0:T(8,128)S(1)}) fusion(f32[16,40,136]{2,1,0:T(8,128)S(1)} %get-tuple-element.28, f32[16,40,136]{2,1,0:T(8,128)S(1)} %get-tuple-element.29, f32[38,134]{1,0:T(8,128)S(1)} %get-tuple-element.46, f32[38,134]{1,0:T(8,128)S(1)} %get-tuple-element.47, f32[16,42,138]{2,1,0:T(8,128)S(1)} %get-tuple-element.7, ...), kind=kLoop, calls=%fused_computation.249 | loop fusion | flops 2444160 | bytes 4358752 | tf_op jit(solution)/shard_map/mul | solution.py:53
  30.9 1.6 %fusion.147 = (f32[16,36,132]{2,1,0:T(8,128)S(1)}, f32[16,36,132]{2,1,0:T(8,128)S(1)}) fusion(f32[16,38,134]{2,1,0:T(8,128)S(1)} %get-tuple-element.26, f32[16,38,134]{2,1,0:T(8,128)S(1)} %get-tuple-element.27, f32[36,132]{1,0:T(8,128)S(1)} %get-tuple-element.43, f32[36,132]{1,0:T(8,128)S(1)} %get-tuple-element.44, f32[16,42,138]{2,1,0:T(8,128)S(1)} %get-tuple-element.7, ...), kind=kLoop, calls=%fused_computation.221 | loop fusion | flops 2280960 | bytes 4067712 | tf_op jit(solution)/shard_map/mul | solution.py:53
  33.2 1.6 %fusion.142 = (f32[16,34,130]{2,1,0:T(8,128)S(1)}, f32[16,34,130]{2,1,0:T(8,128)S(1)}, f32[16,34,130]{2,1,0:T(8,128)S(1)}, f32[16,34,130]{2,1,0:T(8,128)S(1)}) fusion(f32[16,42,138]{2,1,0:T(8,128)S(1)} %get-tuple-element.7, f32[16,36,132]{2,1,0:T(8,128)S(1)} %get-tuple-element.25, f32[34,130]{1,0:T(8,128)S(1)} %get-tuple-element.40, ...), kind=kLoop, calls=%fused_computation.215 | loop fusion | flops 1555840 | bytes 4349280 | tf_op jit(solution)/shard_map/add | solution.py:140
  34.8 0.8 fusion.209
  37.9 7.6 %all-to-all-start = ((f32[32,1,128]{2,1,0:T(1,128)}), f32[32,1,128]{2,1,0:T(1,128)S(1)}, u32[]{:S(2)}, u32[]{:S(2)}) async-start(f32[32,1,128]{2,1,0:T(1,128)} %reshape.247), calls=%async_computation | async-start | bytes 32768 | tf_op jit(solution)/shard_map/all_to_all | solution.py:165
  45.7 6.8 %all-to-all-done = f32[32,1,128]{2,1,0:T(1,128)S(1)} async-done(((f32[32,1,128]{2,1,0:T(1,128)}), f32[32,1,128]{2,1,0:T(1,128)S(1)}, u32[]{:S(2)}, u32[]{:S(2)}) %all-to-all-start) | async-done | bytes 16416 | tf_op jit(solution)/shard_map/all_to_all | solution.py:165
  55.1 4.3 %all-to-all-start.1 = ((f32[32,1,128]{2,1,0:T(1,128)}), f32[32,1,128]{2,1,0:T(1,128)S(1)}, u32[]{:S(2)}, u32[]{:S(2)}) async-start(f32[32,1,128]{2,1,0:T(1,128)} %reshape.249), calls=%async_computation.1 | async-start | bytes 32768 | tf_op jit(solution)/shard_map/all_to_all | solution.py:171
  59.5 6.7 %all-to-all-done.1 = f32[32,1,128]{2,1,0:T(1,128)S(1)} async-done(((f32[32,1,128]{2,1,0:T(1,128)}), f32[32,1,128]{2,1,0:T(1,128)S(1)}, u32[]{:S(2)}, u32[]{:S(2)}) %all-to-all-start.1) | async-done | bytes 16416 | tf_op jit(solution)/shard_map/all_to_all | solution.py:171
  67.1 2.4 %fusion = f32[16,32,128]{2,0,1:T(8,128)S(1)} fusion(s32[32,128]{1,0:T(8,128)S(1)} %multiply_add_fusion, s32[256]{0:T(256)S(1)} %eq.50, f32[32,8]{1,0:T(8,128)S(1)} %copy.41, f32[32,8,16]{2,1,0:T(8,128)S(1)} %reshape.250), kind=kOutput, calls=%fused_computation.1 | convolution fusion | flops 202379264 | bytes 296960 | tf_op jit(solution)/shard_map/dot_general | solution.py:173
  69.6 1.1 multiply_bitcast_fusion
  71.4 1.7 %fusion.109 = (f32[1,16,42,138]{3,2,1,0:T(8,128)S(1)}, f32[1,16,42,138]{3,2,1,0:T(8,128)S(1)}) fusion(f32[16,44,140]{2,1,0:T(8,128)S(1)} %get-tuple-element.22, f32[16,44,140]{2,1,0:T(8,128)S(1)} %get-tuple-element.23, f32[42,138]{1,0:T(8,128)S(1)} %get-tuple-element.36, f32[42,138]{1,0:T(8,128)S(1)} %get-tuple-element.38, ...), kind=kLoop, calls=%fused_computation.168 | loop fusion | flops 2596608 | bytes 4590432 | tf_op jit(solution)/shard_map/stack | solution.py:53
  73.7 1.7 %fusion.89 = (f32[1,16,42,138]{3,2,1,0:T(8,128)S(1)}, f32[1,16,42,138]{3,2,1,0:T(8,128)S(1)}) fusion(f32[16,44,140]{2,1,0:T(8,128)S(1)} %get-tuple-element.20, f32[16,44,140]{2,1,0:T(8,128)S(1)} %get-tuple-element.21, f32[42,138]{1,0:T(8,128)S(1)} %get-tuple-element.36, f32[42,138]{1,0:T(8,128)S(1)} %get-tuple-element.38, ...), kind=kLoop, calls=%fused_computation.138 | loop fusion | flops 2596608 | bytes 4590432 | tf_op jit(solution)/shard_map/stack | solution.py:53
  76.1 1.7 %fusion.69 = (f32[1,16,42,138]{3,2,1,0:T(8,128)S(1)}, f32[1,16,42,138]{3,2,1,0:T(8,128)S(1)}) fusion(f32[16,44,140]{2,1,0:T(8,128)S(1)} %get-tuple-element.18, f32[16,44,140]{2,1,0:T(8,128)S(1)} %get-tuple-element.19, f32[42,138]{1,0:T(8,128)S(1)} %get-tuple-element.36, f32[42,138]{1,0:T(8,128)S(1)} %get-tuple-element.38, ...), kind=kLoop, calls=%fused_computation.108 | loop fusion | flops 2596608 | bytes 4590432 | tf_op jit(solution)/shard_map/stack | solution.py:53
  78.4 1.9 %fusion.49 = (f32[1,16,42,138]{3,2,1,0:T(8,128)S(1)}, f32[1,16,42,138]{3,2,1,0:T(8,128)S(1)}) fusion(f32[16,44,140]{2,1,0:T(8,128)S(1)} %get-tuple-element.16, f32[16,44,140]{2,1,0:T(8,128)S(1)} %get-tuple-element.17, f32[42,138]{1,0:T(8,128)S(1)} %get-tuple-element.36, f32[42,138]{1,0:T(8,128)S(1)} %get-tuple-element.38, ...), kind=kLoop, calls=%fused_computation.78 | loop fusion | flops 2596608 | bytes 4590432 | tf_op jit(solution)/shard_map/stack | solution.py:53
  81.0 1.9 %fusion.120 = f32[16,44,32]{1,2,0:T(8,128)S(1)} fusion(f32[16,44,140]{2,1,0:T(8,128)S(1)} %fusion.27, f32[44,140]{1,0:T(8,128)S(1)} %get-tuple-element.60, f32[44,140]{1,0:T(8,128)S(1)} %get-tuple-element.58, f32[44,140]{1,0:T(8,128)S(1)} %get-tuple-element.59, f32[44,140]{1,0:T(8,128)S(1)} %get-tuple-element.57, f32[44,140]{1,0:T(8,128)S(1)} %get-tuple-element.51, ...), kind=kOutput, calls=%fused_computation.188 | convolution fusion | flops 39038720 | bytes 625728 | tf_op jit(solution)/shard_map/rxy,yb->rxb/dot_general | solution.py:186
  83.6 11.3 %all_to_all.25 = f32[32,8,128]{2,1,0:T(8,128)S(1)} all-to-all(f32[32,8,128]{2,1,0:T(8,128)S(1)} %reshape_reshape.6), channel_id=1, replica_groups=mesh['gx'=32,'gy'=16] {'gx'}, dimensions={0} | all-to-all | bytes 262144 | tf_op jit(solution)/shard_map/all_to_all | solution.py:96
  95.0 26.2 %all_to_all.26 = f32[16,8,128]{2,1,0:T(8,128)S(1)} all-to-all(f32[16,8,128]{2,1,0:T(8,128)S(1)} %broadcast_in_dim.13), channel_id=1, replica_groups=mesh['gx'=32,'gy'=16] {'gy'}, dimensions={0} | all-to-all | bytes 131072 | tf_op jit(solution)/shard_map/all_to_all | solution.py:98
  121.8 5.7 %all-to-all-start.4 = ((f32[32,8,128]{2,1,0:T(8,128)}), f32[32,8,128]{2,1,0:T(8,128)S(1)}, u32[]{:S(2)}, u32[]{:S(2)}) async-start(f32[32,8,128]{2,1,0:T(8,128)} %broadcast_in_dim.14), calls=%async_computation.4 | async-start | bytes 262144 | tf_op jit(solution)/shard_map/all_to_all | solution.py:100
  127.7 7.5 %all-to-all-done.4 = f32[32,8,128]{2,1,0:T(8,128)S(1)} async-done(((f32[32,8,128]{2,1,0:T(8,128)}), f32[32,8,128]{2,1,0:T(8,128)S(1)}, u32[]{:S(2)}, u32[]{:S(2)}) %all-to-all-start.4) | async-done | bytes 131104 | tf_op jit(solution)/shard_map/all_to_all | solution.py:100
  135.5 0.9 copy.49
  (114 shorter events, 19.3 us)
Async XLA Ops:
  0.6 23.9 %copy-start.4 = (f32[32,128]{1,0:T(8,128)S(1)}, f32[32,128]{1,0:T(8,128)}, u32[]{:S(2)}) copy-start(f32[32,128]{1,0:T(8,128)} %param.11) | copy-start | bytes 49156
  0.6 23.9 %copy-start.3 = (f32[32,128]{1,0:T(8,128)S(1)}, f32[32,128]{1,0:T(8,128)}, u32[]{:S(2)}) copy-start(f32[32,128]{1,0:T(8,128)} %param.12) | copy-start | bytes 49156
  0.7 23.9 %copy-start.1 = (f32[32,128]{1,0:T(8,128)S(1)}, f32[32,128]{1,0:T(8,128)}, u32[]{:S(2)}) copy-start(f32[32,128]{1,0:T(8,128)} %param.13) | copy-start | bytes 49156
  0.7 20.6 %copy-start = (f32[16,64,32]{1,2,0:T(8,128)S(1)}, f32[16,64,32]{1,2,0:T(8,128)}, u32[]{:S(2)}) copy-start(f32[16,64,32]{1,2,0:T(8,128)} %param.16) | copy-start | bytes 393220
  2.3 14.7 %collective-permute-start = (f32[4032]{0:T(1024)S(1)}, f32[4032]{0:T(1024)S(1)}, u32[]{:S(2)}, u32[]{:S(2)}) collective-permute-start(f32[4032]{0:T(1024)S(1)} %pad_maximum_fusion.12), channel_id=1, source_target_pairs={{0,16},{16,32},{32,48},{48,64},{64,80},{80,96},{96,112},{112,128},... | collective-permute-start | bytes 48392 | tf_op jit(solution)/shard_map/ppermute | solution.py:85
  6.9 10.1 %collective-permute-start.1 = (f32[4032]{0:T(1024)S(1)}, f32[4032]{0:T(1024)S(1)}, u32[]{:S(2)}, u32[]{:S(2)}) collective-permute-start(f32[4032]{0:T(1024)S(1)} %pad_maximum_fusion.13), channel_id=1, source_target_pairs={{16,0},{32,16},{48,32},{64,48},{80,64},{96,80},{112,96},{128,112},... | collective-permute-start | bytes 48392 | tf_op jit(solution)/shard_map/ppermute | solution.py:86
  18.2 4.1 %collective-permute-start.2 = (f32[1512]{0:T(1024)S(1)}, f32[1512]{0:T(1024)S(1)}, u32[]{:S(2)}, u32[]{:S(2)}) collective-permute-start(f32[1512]{0:T(1024)S(1)} %pad_maximum_fusion.14), channel_id=1, source_target_pairs={{0,1},{1,2},{2,3},{3,4},{4,5},{5,6},{6,7},{7,8},{8,9},{9,10},{10,1... | collective-permute-start | bytes 18152 | tf_op jit(solution)/shard_map/ppermute | solution.py:85
  19.8 4.5 %collective-permute-start.3 = (f32[1512]{0:T(1024)S(1)}, f32[1512]{0:T(1024)S(1)}, u32[]{:S(2)}, u32[]{:S(2)}) collective-permute-start(f32[1512]{0:T(1024)S(1)} %pad_maximum_fusion.15), channel_id=1, source_target_pairs={{1,0},{2,1},{3,2},{4,3},{5,4},{6,5},{7,6},{8,7},{9,8},{10,9},{11,1... | collective-permute-start | bytes 18152 | tf_op jit(solution)/shard_map/ppermute | solution.py:86
  25.1 1.4 %copy-start.2 = (f32[128,32]{0,1:T(8,128)S(1)}, f32[128,32]{0,1:T(8,128)}, u32[]{:S(2)}) copy-start(f32[128,32]{0,1:T(8,128)} %param.15) | copy-start | bytes 49156
  35.7 18.5 %copy-start.7 = (f32[1,1,40]{2,1,0:T(1,128)S(1)}, f32[1,1,40]{2,1,0:T(1,128)}, u32[]{:S(2)}) copy-start(f32[1,1,40]{2,1,0:T(1,128)} %param.21) | copy-start | bytes 484
  37.9 14.5 %all-to-all-start = ((f32[32,1,128]{2,1,0:T(1,128)}), f32[32,1,128]{2,1,0:T(1,128)S(1)}, u32[]{:S(2)}, u32[]{:S(2)}) async-start(f32[32,1,128]{2,1,0:T(1,128)} %reshape.247), calls=%async_computation | async-start | bytes 32768 | tf_op jit(solution)/shard_map/all_to_all | solution.py:165
  54.1 16.6 %copy-start.6 = (f32[16,40]{1,0:T(8,128)}, f32[16,40]{1,0:T(8,128)S(1)}, u32[]{:S(2)}) copy-start(f32[16,40]{1,0:T(8,128)S(1)} %fusion.228) | copy-start | bytes 7684
  55.1 11.1 %all-to-all-start.1 = ((f32[32,1,128]{2,1,0:T(1,128)}), f32[32,1,128]{2,1,0:T(1,128)S(1)}, u32[]{:S(2)}, u32[]{:S(2)}) async-start(f32[32,1,128]{2,1,0:T(1,128)} %reshape.249), calls=%async_computation.1 | async-start | bytes 32768 | tf_op jit(solution)/shard_map/all_to_all | solution.py:171
  80.9 1.9 %copy-start.5 = (f32[32,64]{1,0:T(8,128)S(1)}, f32[32,64]{1,0:T(8,128)}, u32[]{:S(2)}) copy-start(f32[32,64]{1,0:T(8,128)} %param.14) | copy-start | bytes 24580
  121.8 13.4 %all-to-all-start.4 = ((f32[32,8,128]{2,1,0:T(8,128)}), f32[32,8,128]{2,1,0:T(8,128)S(1)}, u32[]{:S(2)}, u32[]{:S(2)}) async-start(f32[32,8,128]{2,1,0:T(8,128)} %broadcast_in_dim.14), calls=%async_computation.4 | async-start | bytes 262144 | tf_op jit(solution)/shard_map/all_to_all | solution.py:100

commit v9 on v6

--- a/solution.py
+++ b/solution.py
@@ -157,15 +157,15 @@
     noise_precision,
 ):
     rim_depth = STEPS
-    reach = rim_depth + 1
+    reach = rim_depth
     height, breadth = diffusivity.shape
     n_dirs = directions.shape[0]
     static = jnp.stack([diffusivity, base_humidity, coupling, jnp.ones_like(diffusivity)])
     static_gx, rows_wide = exchange(((static, 1), (basis_rows, 0)), "gx", reach)
     static_wide, cols_wide = exchange(((static_gx, 2), (basis_cols, 0)), "gy", reach)
-    static_six = window(static_wide, reach, rim_depth)
-    rows_six = rows_wide[1:-1]
-    cols_six = cols_wide[1:-1]
+    static_six = static_wide
+    rows_six = rows_wide
+    cols_six = cols_wide
     perturb = jnp.einsum("xa,rab->rxb", rows_six, directions, precision=exact)
     perturb = jnp.einsum("rxb,yb->rxy", perturb, cols_six, precision=exact)
     param_wide = static_six[0] * perturb

time: 137 us -> 137 us (level)
  no operation moved by 1% of the time
where the time goes in v9:
time: 137 us; the launch traced here: 136 us
  blocking collectives  37.5 us (27%)
  starting transfers between devices  30.1 us (22%)
  waiting for transfers between devices  22.8 us (17%)
  other arithmetic  21.6 us (16%)
  local copies, waits for them, and re-layouts  17.2 us (13%)
  matrix products  4.98 us (4%)
  between operations  1.39 us (1%)
    all_to_all x1, blocking collectives, all_sum(): part = lax.all_to_all(copies, 'gy', 0, 0, tiled=True).sum(0)  26.2 us
    all_to_all x1, blocking collectives, all_sum(): part = lax.all_to_all(flat, 'gx', 0, 0, tiled=True).sum(0)  11.3 us
    all_to_all x1, starting transfers between devices, local(): lax.all_to_all(picked, 'gx', split_axis=1, concat_axis=1, tiled=True)  7.64 us
    all_to_all x1, waiting for transfers between devices, all_sum(): lax.all_to_all(spread_out, 'gx', 0, 0, tiled=True).reshape(values.shape)  7.49 us
    all_to_all x1, waiting for transfers between devices, local(): lax.all_to_all(backward, 'gx', split_axis=1, concat_axis=1, tiled=True)  6.88 us
    all_to_all x1, waiting for transfers between devices, local(): lax.all_to_all(picked, 'gx', split_axis=1, concat_axis=1, tiled=True)  6.87 us
    ppermute x2, starting transfers between devices, exchange(): lax.ppermute(pack(heads), axis, [(i + 1, i) for i in range(ends)])  6.81 us
    ppermute x2, starting transfers between devices, exchange(): lax.ppermute(pack(tails), axis, [(i, i + 1) for i in range(ends)])  5.76 us
  transfers between devices with their start and end apart: 7, of which 4 were waited for; matrix products, arithmetic and copies ran while one was open for 5% of the time, Pallas kernels for 0%

profile of v9, /device:TPU:1, one launch (start us, length us, event | category | flops | bytes accessed | tf_op | source)
XLA Modules:
  0.0 135.6 jit_solution(11783268485620847713)
XLA Ops:
  0.7 0.8 pad_maximum_fusion.8
  2.2 4.5 %collective-permute-start = (f32[3456]{0:T(1024)S(1)}, f32[3456]{0:T(1024)S(1)}, u32[]{:S(2)}, u32[]{:S(2)}) collective-permute-start(f32[3456]{0:T(1024)S(1)} %pad_maximum_fusion.9), channel_id=1, source_target_pairs={{0,16},{16,32},{32,48},{48,64},{64,80},{80,96},{96,112},{112,128},... | collective-permute-start | bytes 41480 | tf_op jit(solution)/shard_map/ppermute | solution.py:85
  6.8 5.5 %collective-permute-start.1 = (f32[3456]{0:T(1024)S(1)}, f32[3456]{0:T(1024)S(1)}, u32[]{:S(2)}, u32[]{:S(2)}) collective-permute-start(f32[3456]{0:T(1024)S(1)} %pad_maximum_fusion.10), channel_id=1, source_target_pairs={{16,0},{32,16},{48,32},{64,48},{80,64},{96,80},{112,96},{128,112},... | collective-permute-start | bytes 41480 | tf_op jit(solution)/shard_map/ppermute | solution.py:86
  13.8 0.9 fusion.189
  16.0 0.8 copy.41
  18.0 1.3 collective-permute-start.2
  19.5 1.3 collective-permute-start.3
  21.0 1.3 fusion.157
  22.4 1.6 %collective-permute-done.3 = f32[1248]{0:T(1024)S(1)} collective-permute-done((f32[1248]{0:T(1024)S(1)}, f32[1248]{0:T(1024)S(1)}, u32[]{:S(2)}, u32[]{:S(2)}) %collective-permute-start.3) | collective-permute-done | bytes 5024 | tf_op jit(solution)/shard_map/ppermute | solution.py:86
  26.1 0.9 convolution_multiply_fusion
  27.0 0.9 broadcast_multiply_fusion
  27.9 0.9 multiply_multiply_fusion
  28.8 1.6 %fusion.67 = (f32[16,38,134]{2,1,0:T(8,128)S(1)}, f32[16,38,134]{2,1,0:T(8,128)S(1)}) fusion(f32[16,40,136]{2,1,0:T(8,128)S(1)} %get-tuple-element.16, f32[16,40,136]{2,1,0:T(8,128)S(1)} %get-tuple-element.17, f32[38,134]{1,0:T(8,128)S(1)} %get-tuple-element.84, f32[38,134]{1,0:T(8,128)S(1)} %get-tuple-element.85, f32[16,42,138]{2,1,0:T(8,128)S(1)} %get-tuple-element.11, ...), kind=kLoop, calls=%fused_computation.107 | loop fusion | flops 2444160 | bytes 4358752 | tf_op jit(solution)/shard_map/mul | solution.py:53
  30.5 1.6 %fusion.48 = (f32[16,36,132]{2,1,0:T(8,128)S(1)}, f32[16,36,132]{2,1,0:T(8,128)S(1)}) fusion(f32[16,38,134]{2,1,0:T(8,128)S(1)} %get-tuple-element.14, f32[16,38,134]{2,1,0:T(8,128)S(1)} %get-tuple-element.15, f32[36,132]{1,0:T(8,128)S(1)} %get-tuple-element.81, f32[36,132]{1,0:T(8,128)S(1)} %get-tuple-element.82, f32[16,42,138]{2,1,0:T(8,128)S(1)} %get-tuple-element.11, ...), kind=kLoop, calls=%fused_computation.79 | loop fusion | flops 2280960 | bytes 4067712 | tf_op jit(solution)/shard_map/mul | solution.py:53
  32.8 1.6 %fusion.43 = (f32[16,34,130]{2,1,0:T(8,128)S(1)}, f32[16,34,130]{2,1,0:T(8,128)S(1)}, f32[16,34,130]{2,1,0:T(8,128)S(1)}, f32[16,34,130]{2,1,0:T(8,128)S(1)}) fusion(f32[16,42,138]{2,1,0:T(8,128)S(1)} %get-tuple-element.11, f32[16,36,132]{2,1,0:T(8,128)S(1)} %get-tuple-element.13, f32[34,130]{1,0:T(8,128)S(1)} %get-tuple-element.78, ...), kind=kLoop, calls=%fused_computation.73 | loop fusion | flops 1555840 | bytes 4349280 | tf_op jit(solution)/shard_map/add | solution.py:179
  34.4 0.8 fusion.110
  37.5 7.6 %all-to-all-start = ((f32[32,1,128]{2,1,0:T(1,128)}), f32[32,1,128]{2,1,0:T(1,128)S(1)}, u32[]{:S(2)}, u32[]{:S(2)}) async-start(f32[32,1,128]{2,1,0:T(1,128)} %reshape.261), calls=%async_computation | async-start | bytes 32768 | tf_op jit(solution)/shard_map/all_to_all | solution.py:201
  45.2 6.9 %all-to-all-done = f32[32,1,128]{2,1,0:T(1,128)S(1)} async-done(((f32[32,1,128]{2,1,0:T(1,128)}), f32[32,1,128]{2,1,0:T(1,128)S(1)}, u32[]{:S(2)}, u32[]{:S(2)}) %all-to-all-start) | async-done | bytes 16416 | tf_op jit(solution)/shard_map/all_to_all | solution.py:201
  54.5 4.1 %all-to-all-start.1 = ((f32[32,1,128]{2,1,0:T(1,128)}), f32[32,1,128]{2,1,0:T(1,128)S(1)}, u32[]{:S(2)}, u32[]{:S(2)}) async-start(f32[32,1,128]{2,1,0:T(1,128)} %reshape.263), calls=%async_computation.1 | async-start | bytes 32768 | tf_op jit(solution)/shard_map/all_to_all | solution.py:207
  58.8 6.9 %all-to-all-done.1 = f32[32,1,128]{2,1,0:T(1,128)S(1)} async-done(((f32[32,1,128]{2,1,0:T(1,128)}), f32[32,1,128]{2,1,0:T(1,128)S(1)}, u32[]{:S(2)}, u32[]{:S(2)}) %all-to-all-start.1) | async-done | bytes 16416 | tf_op jit(solution)/shard_map/all_to_all | solution.py:207
  66.4 2.2 %scatter_custom_fusion = f32[16,4096]{0,1:T(8,128)S(1)} fusion(s32[256]{0:T(256)S(1)} %bitcast.156, f32[]{:T(128)} %constant.14.clone.1, f32[32,8]{1,0:T(8,128)S(1)} %copy.40, f32[32,8,16]{2,1,0:T(8,128)S(1)} %reshape.264), kind=kCustom, calls=%fused_computation.16 | custom fusion | flops 8192 | bytes 409604 | tf_op jit(solution)/shard_map/scatter-add | solution.py:210
  70.2 1.0 fusion.16
  71.7 1.1 add_multiply_fusion.2
  73.6 1.6 %add_multiply_fusion.1 = (f32[16,44,140]{2,1,0:T(8,128)S(1)}, f32[16,44,140]{2,1,0:T(8,128)S(1)}) fusion(f32[16,44,140]{2,1,0:T(8,128)S(1)} %add_multiply_fusion.2, f32[16,44,139]{2,1,0:T(8,128)S(1)} %get-tuple-element.45, f32[16,44,139]{2,1,0:T(8,128)S(1)} %get-tuple-element.44, f32[16,43,140]{2,1,0:T(8,128)S(1)} %get-tuple-element.43, ...), kind=kLoop, calls=%fused_computation.64 | loop fusion | flops 3449600 | bytes 5870464 | tf_op jit(solution)/shard_map/mul | solution.py:135
  76.1 1.3 add_multiply_fusion
  78.3 1.5 %fusion.14 = f32[16,44,140]{2,1,0:T(8,128)S(1)} fusion(f32[16,44,140]{2,1,0:T(8,128)S(1)} %get-tuple-element.6, f32[16,44,140]{2,1,0:T(8,128)S(1)} %get-tuple-element.8, f32[16,44,140]{2,1,0:T(8,128)S(1)} %add_multiply_fusion.2, f32[16,44,140]{2,1,0:T(8,128)S(1)} %get-tuple-element.55, f32[16,32,128]{2,1,0:T(8,128)S(1)} %copy.49, ...), kind=kLoop, calls=%fused_computation.30 | loop fusion | flops 3351040 | bytes 5882240 | tf_op jit(solution)/shard_map/mul | solution.py:138
  80.2 1.8 %fusion.25 = f32[16,44,32]{1,2,0:T(8,128)S(1)} fusion(f32[16,44,140]{2,1,0:T(8,128)S(1)} %fusion.14, f32[16,44,139]{2,1,0:T(8,128)S(1)} %get-tuple-element.21, f32[16,44,139]{2,1,0:T(8,128)S(1)} %get-tuple-element.20, f32[16,43,140]{2,1,0:T(8,128)S(1)} %get-tuple-element.19, f32[16,43,140]{2,1,0:T(8,128)S(1)} %get-tuple-element.18, ...), kind=kOutput, calls=%fused_computation.45 | convolution fusion | flops 39038720 | bytes 2178880 | tf_op jit(solution)/shard_map/rxy,yb->rxb/dot_general | solution.py:142
  82.8 11.3 %all_to_all.25 = f32[32,8,128]{2,1,0:T(8,128)S(1)} all-to-all(f32[32,8,128]{2,1,0:T(8,128)S(1)} %reshape_reshape.6), channel_id=1, replica_groups=mesh['gx'=32,'gy'=16] {'gx'}, dimensions={0} | all-to-all | bytes 262144 | tf_op jit(solution)/shard_map/all_to_all | solution.py:96
  94.2 26.2 %all_to_all.26 = f32[16,8,128]{2,1,0:T(8,128)S(1)} all-to-all(f32[16,8,128]{2,1,0:T(8,128)S(1)} %broadcast_in_dim.22), channel_id=1, replica_groups=mesh['gx'=32,'gy'=16] {'gy'}, dimensions={0} | all-to-all | bytes 131072 | tf_op jit(solution)/shard_map/all_to_all | solution.py:98
  121.0 5.7 %all-to-all-start.4 = ((f32[32,8,128]{2,1,0:T(8,128)}), f32[32,8,128]{2,1,0:T(8,128)S(1)}, u32[]{:S(2)}, u32[]{:S(2)}) async-start(f32[32,8,128]{2,1,0:T(8,128)} %broadcast_in_dim.23), calls=%async_computation.4 | async-start | bytes 262144 | tf_op jit(solution)/shard_map/all_to_all | solution.py:100
  127.0 7.5 %all-to-all-done.4 = f32[32,8,128]{2,1,0:T(8,128)S(1)} async-done(((f32[32,8,128]{2,1,0:T(8,128)}), f32[32,8,128]{2,1,0:T(8,128)S(1)}, u32[]{:S(2)}, u32[]{:S(2)}) %all-to-all-start.4) | async-done | bytes 131104 | tf_op jit(solution)/shard_map/all_to_all | solution.py:100
  134.7 0.9 copy.46
  (126 shorter events, 20.3 us)
Async XLA Ops:
  0.6 23.5 %copy-start.4 = (f32[32,128]{1,0:T(8,128)S(1)}, f32[32,128]{1,0:T(8,128)}, u32[]{:S(2)}) copy-start(f32[32,128]{1,0:T(8,128)} %param.11) | copy-start | bytes 49156
  0.6 23.5 %copy-start.3 = (f32[32,128]{1,0:T(8,128)S(1)}, f32[32,128]{1,0:T(8,128)}, u32[]{:S(2)}) copy-start(f32[32,128]{1,0:T(8,128)} %param.12) | copy-start | bytes 49156
  0.7 23.5 %copy-start.2 = (f32[32,128]{1,0:T(8,128)S(1)}, f32[32,128]{1,0:T(8,128)}, u32[]{:S(2)}) copy-start(f32[32,128]{1,0:T(8,128)} %param.13) | copy-start | bytes 49156
  2.2 14.6 %collective-permute-start = (f32[3456]{0:T(1024)S(1)}, f32[3456]{0:T(1024)S(1)}, u32[]{:S(2)}, u32[]{:S(2)}) collective-permute-start(f32[3456]{0:T(1024)S(1)} %pad_maximum_fusion.9), channel_id=1, source_target_pairs={{0,16},{16,32},{32,48},{48,64},{64,80},{80,96},{96,112},{112,128},... | collective-permute-start | bytes 41480 | tf_op jit(solution)/shard_map/ppermute | solution.py:85
  6.8 10.0 %collective-permute-start.1 = (f32[3456]{0:T(1024)S(1)}, f32[3456]{0:T(1024)S(1)}, u32[]{:S(2)}, u32[]{:S(2)}) collective-permute-start(f32[3456]{0:T(1024)S(1)} %pad_maximum_fusion.10), channel_id=1, source_target_pairs={{16,0},{32,16},{48,32},{64,48},{80,64},{96,80},{112,96},{128,112},... | collective-permute-start | bytes 41480 | tf_op jit(solution)/shard_map/ppermute | solution.py:86
  18.0 4.3 %collective-permute-start.2 = (f32[1248]{0:T(1024)S(1)}, f32[1248]{0:T(1024)S(1)}, u32[]{:S(2)}, u32[]{:S(2)}) collective-permute-start(f32[1248]{0:T(1024)S(1)} %pad_maximum_fusion.11), channel_id=1, source_target_pairs={{0,1},{1,2},{2,3},{3,4},{4,5},{5,6},{6,7},{7,8},{8,9},{9,10},{10,1... | collective-permute-start | bytes 14984 | tf_op jit(solution)/shard_map/ppermute | solution.py:85
  19.5 4.5 %collective-permute-start.3 = (f32[1248]{0:T(1024)S(1)}, f32[1248]{0:T(1024)S(1)}, u32[]{:S(2)}, u32[]{:S(2)}) collective-permute-start(f32[1248]{0:T(1024)S(1)} %pad_maximum_fusion.12), channel_id=1, source_target_pairs={{1,0},{2,1},{3,2},{4,3},{5,4},{6,5},{7,6},{8,7},{9,8},{10,9},{11,1... | collective-permute-start | bytes 14984 | tf_op jit(solution)/shard_map/ppermute | solution.py:86
  24.2 1.9 %copy-start.1 = (f32[128,32]{0,1:T(8,128)S(1)}, f32[128,32]{0,1:T(8,128)}, u32[]{:S(2)}) copy-start(f32[128,32]{0,1:T(8,128)} %param.15) | copy-start | bytes 49156
  35.3 18.2 %copy-start.7 = (f32[1,1,40]{2,1,0:T(1,128)S(1)}, f32[1,1,40]{2,1,0:T(1,128)}, u32[]{:S(2)}) copy-start(f32[1,1,40]{2,1,0:T(1,128)} %param.21) | copy-start | bytes 484
  37.5 14.5 %all-to-all-start = ((f32[32,1,128]{2,1,0:T(1,128)}), f32[32,1,128]{2,1,0:T(1,128)S(1)}, u32[]{:S(2)}, u32[]{:S(2)}) async-start(f32[32,1,128]{2,1,0:T(1,128)} %reshape.261), calls=%async_computation | async-start | bytes 32768 | tf_op jit(solution)/shard_map/all_to_all | solution.py:201
  53.5 15.7 %copy-start.6 = (f32[16,40]{1,0:T(8,128)}, f32[16,40]{1,0:T(8,128)S(1)}, u32[]{:S(2)}) copy-start(f32[16,40]{1,0:T(8,128)S(1)} %fusion.129) | copy-start | bytes 7684
  54.5 11.1 %all-to-all-start.1 = ((f32[32,1,128]{2,1,0:T(1,128)}), f32[32,1,128]{2,1,0:T(1,128)S(1)}, u32[]{:S(2)}, u32[]{:S(2)}) async-start(f32[32,1,128]{2,1,0:T(1,128)} %reshape.263), calls=%async_computation.1 | async-start | bytes 32768 | tf_op jit(solution)/shard_map/all_to_all | solution.py:207
  80.2 1.9 %copy-start.5 = (f32[32,64]{1,0:T(8,128)S(1)}, f32[32,64]{1,0:T(8,128)}, u32[]{:S(2)}) copy-start(f32[32,64]{1,0:T(8,128)} %param.14) | copy-start | bytes 24580
  82.0 44.7 %copy-start = (f32[16,64,32]{1,2,0:T(8,128)S(1)}, f32[16,64,32]{1,2,0:T(8,128)}, u32[]{:S(2)}) copy-start(f32[16,64,32]{1,2,0:T(8,128)} %param.16) | copy-start | bytes 393220
  121.0 13.4 %all-to-all-start.4 = ((f32[32,8,128]{2,1,0:T(8,128)}), f32[32,8,128]{2,1,0:T(8,128)S(1)}, u32[]{:S(2)}, u32[]{:S(2)}) async-start(f32[32,8,128]{2,1,0:T(8,128)} %broadcast_in_dim.23), calls=%async_computation.4 | async-start | bytes 262144 | tf_op jit(solution)/shard_map/all_to_all | solution.py:100
